TPU v7x, 256 devices: a whole 4x4x8 slice. The times are simulated.
256 devices in a mesh: dp: 16 (over y_lo, x, core), tensor: 16 (over z, y_hi).
Axes of the slice: x: 4, y: 4 (y_hi: 2, y_lo: 2; y = y_hi * 2 + y_lo), z: 8, core: 2. Of those that a mesh axis runs over, the one named last changes fastest.
Arguments:
- gate_pre: bfloat16 [8192, 14336], P('dp', 'tensor'), may hold values from -6 to 6
- up_pre: bfloat16 [8192, 14336], P('dp', 'tensor'), may hold values from -6 to 6
- grad_out: bfloat16 [8192, 4096], P(('dp', 'tensor')), may hold values from -24 to 24
- codes: bfloat16 [14336, 4096], P('tensor'), as said below
- scales: int32 [448, 4096], P('tensor'), may hold values from 117 to 120
Outputs:
- out: bfloat16 [8192, 4096], P(('dp', 'tensor'))
- grad_gate: bfloat16 [8192, 14336], P('dp', 'tensor')
- grad_up: bfloat16 [8192, 14336], P('dp', 'tensor')
- grad_weight: bfloat16 [14336, 4096], P('tensor', 'dp')
Inputs may be any that keep to these rules, and one draw needn't show every extreme that they name: `codes`: every entry is an FP8 E4M3 normal value (sign, exponent field 4 to 9, three mantissa bits), held exactly.
All inputs are finite; a program needn't handle non-finite values.
Results may differ from a plain program's by a relative error of at most 0.022.
Values may be sent and summed in bfloat16 or wider, within the bound.
No kernel may reach another device: no remote copies, remote signals or barrier semaphores. Data moves between devices by JAX's collectives and lax.ppermute only.
A program may use at most 128 MiB of HBM per device.

v0:
```python
import jax
import jax.numpy as jnp
from jax import lax
from jax.sharding import PartitionSpec as P


def decode(codes, scales):
    factor = jnp.exp2(scales.astype(jnp.float32) - 127.0).astype(jnp.bfloat16)
    blocks = codes.reshape(scales.shape[0], 32, codes.shape[1]) * factor[:, None, :]
    return blocks.reshape(codes.shape)


def weight_gradient(hidden, cotangent):
    partial_grad = lax.dot_general(
        hidden, cotangent, (((0,), (0,)), ((), ())), preferred_element_type=jnp.float32
    )
    return lax.psum_scatter(
        partial_grad.astype(jnp.bfloat16), "dp", scatter_dimension=1, tiled=True
    )


def per_device(gate_pre, up_pre, grad_out, codes, scales):
    weight = decode(codes, scales)
    gate_value = gate_pre.astype(jnp.float32)
    up_value = up_pre.astype(jnp.float32)
    sigmoid_gate = jax.nn.sigmoid(gate_value)
    hidden = (gate_value * sigmoid_gate * up_value).astype(jnp.bfloat16)
    out = lax.psum_scatter(
        jnp.dot(hidden, weight, preferred_element_type=jnp.float32).astype(jnp.bfloat16),
        "tensor",
        scatter_dimension=0,
        tiled=True,
    )
    cotangent = lax.all_gather(grad_out, "tensor", axis=0, tiled=True)
    grad_hidden = lax.dot_general(
        cotangent, weight, (((1,), (1,)), ((), ())), preferred_element_type=jnp.float32
    )
    grad_weight = weight_gradient(hidden, cotangent)
    grad_gate = (
        grad_hidden * up_value * sigmoid_gate * (1.0 + gate_value * (1.0 - sigmoid_gate))
    ).astype(jnp.bfloat16)
    grad_up = (grad_hidden * gate_value * sigmoid_gate).astype(jnp.bfloat16)
    return (out, grad_gate, grad_up, grad_weight)


def solution(mesh):
    in_specs = (
        P("dp", "tensor"),
        P("dp", "tensor"),
        P(("dp", "tensor"), None),
        P("tensor", None),
        P("tensor", None),
    )
    out_specs = (P(("dp", "tensor"), None), P("dp", "tensor"), P("dp", "tensor"), P("tensor", "dp"))
    return jax.shard_map(
        per_device, mesh=mesh, in_specs=in_specs, out_specs=out_specs, check_vma=False
    )
```

profile of v0, /device:TPU:1, one launch (start us, length us, event | category | flops | bytes accessed | tf_op | source)
XLA Modules:
  0.0 409.7 jit_solution(5260447283789857836)
XLA Ops:
  7.2 0.0 copy-start.1
  7.2 0.0 all-gather.2.cloned.1.call-start
  7.2 0.7 all-gather.2.cloned.1.call-update
  7.9 0.0 copy-start.4
  7.9 0.0 reduce-scatter.3.cloned.1.call-start
  8.0 2.3 copy.10
  10.2 0.0 copy-done.1
  10.2 1.3 copy.9
  11.5 0.0 copy-done.4
  11.5 0.1 exponential_convert_fusion
  11.6 3.7 bitcast_multiply_fusion
  15.3 0.0 copy-start
  15.3 2.9 copy-done
  18.2 8.0 %convolution_convert_fusion.1 = bf16[512,4096]{1,0:T(8,128)(2,1)} fusion(bf16[896,4096]{1,0:T(8,128)(2,1)S(1)} %bitcast_multiply_fusion, bf16[512,896]{0,1:T(8,128)(2,1)} %copy.10, bf16[512,896]{0,1:T(8,128)(2,1)} %copy.9), kind=kOutput, calls=%fused_computation.2 | convolution fusion | flops 3763863552 | bytes 13369344 | tf_op jit(solution)/shard_map/dot_general | solution.py:29
  26.3 0.0 copy-start.2
  26.3 0.0 copy-start.3
  26.3 0.0 reduce-scatter.3.cloned.1.call-update
  26.3 0.0 reduce-scatter.5.cloned.1.call-start
  26.3 84.4 %all-gather.2.cloned.1.call-done = bf16[512,4096]{1,0:T(8,128)(2,1)} async-done(((bf16[32,4096]{1,0:T(8,128)(2,1)}), bf16[512,4096]{1,0:T(8,128)(2,1)}) %all-gather.2.cloned.1.call-update) | async-done | bytes 4194320 | tf_op jit(solution)/shard_map/all_gather | solution.py:34
  110.8 0.0 copy-done.2
  110.8 0.0 copy-done.3
  110.8 8.4 %convolution_convert_fusion = bf16[896,4096]{1,0:T(8,128)(2,1)} fusion(bf16[512,4096]{1,0:T(8,128)(2,1)} %all-gather.2.cloned.1.call-done, bf16[512,896]{0,1:T(8,128)(2,1)S(1)} %copy-done.2, bf16[512,896]{0,1:T(8,128)(2,1)S(1)} %copy-done.3), kind=kOutput, calls=%fused_computation.1 | convolution fusion | flops 3765436416 | bytes 13369344 | tf_op jit(solution)/shard_map/dot_general | solution.py:14
  119.2 0.0 reduce-scatter.5.cloned.1.call-update
  119.2 9.8 %fusion.9 = (bf16[512,896]{0,1:T(8,128)(2,1)S(1)}, bf16[512,896]{0,1:T(8,128)(2,1)}) fusion(bf16[512,896]{0,1:T(8,128)(2,1)S(1)} %copy-done.3, bf16[512,896]{0,1:T(8,128)(2,1)S(1)} %copy-done.2, bf16[896,4096]{1,0:T(8,128)(2,1)} %copy-done, bf16[512,4096]{1,0:T(8,128)(2,1)} %all-gather.2.cloned.1.call-done), kind=kOutput, calls=%fused_computation.18 | convolution fusion | flops 3764977664 | bytes 15204352 | tf_op jit(solution)/shard_map/dot_general | solution.py:35
  129.0 2.2 copy.11
  131.2 1.3 copy.12
  132.5 193.3 %reduce-scatter.3.cloned.1.call-done = bf16[32,4096]{1,0:T(8,128)(2,1)} async-done(((bf16[512,4096]{1,0:T(8,128)(2,1)}), bf16[32,4096]{1,0:T(8,128)(2,1)}) %reduce-scatter.3.cloned.1.call-update) | async-done | bytes 262160 | tf_op jit(solution)/shard_map/reduce_scatter | solution.py:28
  325.8 77.3 %reduce-scatter.5.cloned.1.call-done = bf16[896,256]{1,0:T(8,128)(2,1)} async-done(((bf16[896,4096]{1,0:T(8,128)(2,1)}), bf16[896,256]{1,0:T(8,128)(2,1)}) %reduce-scatter.5.cloned.1.call-update) | async-done | bytes 458768 | tf_op jit(solution)/shard_map/reduce_scatter | solution.py:17
Async XLA Ops:
  7.2 3.1 copy-start.1
  7.2 103.6 %all-gather.2.cloned.1.call-start = ((), (), s32[]{:S(2)}) async-start(), calls=%async_computation.3 | async-start | bytes 4456448 | tf_op jit(solution)/shard_map/all_gather | solution.py:34
  7.9 3.6 copy-start.4
  7.9 317.9 %reduce-scatter.3.cloned.1.call-start = ((), (), s32[]{:S(2)}) async-start(), calls=%async_computation.2 | async-start | bytes 4456448 | tf_op jit(solution)/shard_map/reduce_scatter | solution.py:28
  15.3 2.9 copy-start
  26.3 84.5 %copy-start.2 = (bf16[512,896]{0,1:T(8,128)(2,1)S(1)}, bf16[512,896]{0,1:T(8,128)(2,1)}, u32[]{:S(2)}) copy-start(bf16[512,896]{0,1:T(8,128)(2,1)} %copy.10) | copy-start | bytes 2752516
  26.3 84.5 %copy-start.3 = (bf16[512,896]{0,1:T(8,128)(2,1)S(1)}, bf16[512,896]{0,1:T(8,128)(2,1)}, u32[]{:S(2)}) copy-start(bf16[512,896]{0,1:T(8,128)(2,1)} %copy.9) | copy-start | bytes 2752516
  26.3 376.9 %reduce-scatter.5.cloned.1.call-start = ((), (), s32[]{:S(2)}) async-start(), calls=%async_computation.4 | async-start | bytes 7798784 | tf_op jit(solution)/shard_map/reduce_scatter | solution.py:17
Sparse Core Ops, SparseCore 0:
  10.6 100.1 all-gather.1
  115.4 210.4 reduce-scatter.2
  329.0 74.1 reduce-scatter.4
where the time goes:
time: 412 us; the launch traced here: 410 us
  waiting for transfers between devices  356 us (86%)
  matrix products  26.2 us (6%)
  between operations  13.8 us (3%)
  local copies, waits for them, and re-layouts  9.97 us (2%)
    reduce_scatter x1, waiting for transfers between devices, per_device(): lax.psum_scatter(jnp.dot(hidden, weight, preferred_element_type=jnp.float...  193 us
    all_gather x1, waiting for transfers between devices, per_device(): cotangent = lax.all_gather(grad_out, 'tensor', axis=0, tiled=True)  84.4 us
    reduce_scatter x1, waiting for transfers between devices, weight_gradient(): lax.psum_scatter(partial_grad.astype(jnp.bfloat16), 'dp', scatter_dimensi...  77.3 us
    unnamed x14, local copies, waits for them, and re-layouts  9.97 us
    dot_general x1, matrix products, per_device(): lax.dot_general(cotangent, weight, (((1,), (1,)), ((), ())), preferred_el...  9.8 us
    dot_general x1, matrix products, weight_gradient(): lax.dot_general(hidden, cotangent, (((0,), (0,)), ((), ())), preferred_el...  8.41 us
  transfers between devices with their start and end apart: 3, of which 3 were waited for; matrix products, arithmetic and copies ran while one was open for 9% of the time, Pallas kernels for 0%

commit v1 on v0

v1 whole, which is shorter than its diff:
```python
import jax
import jax.numpy as jnp
from jax import lax
from jax.sharding import Mesh, PartitionSpec as P

DP = ("dy", "dx", "dc")
TP = ("tz", "ty")


def decode(codes, scales):
    factor = jnp.exp2(scales.astype(jnp.float32) - 127.0).astype(jnp.bfloat16)
    blocks = codes.reshape(scales.shape[0], 32, codes.shape[1]) * factor[:, None, :]
    return blocks.reshape(codes.shape)


def weight_gradient(hidden, cotangent):
    partial_grad = lax.dot_general(
        hidden, cotangent, (((0,), (0,)), ((), ())), preferred_element_type=jnp.float32
    )
    return lax.psum_scatter(
        partial_grad.astype(jnp.bfloat16), DP, scatter_dimension=1, tiled=True
    )


def per_device(gate_pre, up_pre, grad_out, codes, scales):
    weight = decode(codes, scales)
    gate_value = gate_pre.astype(jnp.float32)
    up_value = up_pre.astype(jnp.float32)
    sigmoid_gate = jax.nn.sigmoid(gate_value)
    hidden = (gate_value * sigmoid_gate * up_value).astype(jnp.bfloat16)
    partial_out = jnp.dot(hidden, weight, preferred_element_type=jnp.float32).astype(jnp.bfloat16)
    out = lax.psum_scatter(partial_out, "tz", scatter_dimension=0, tiled=True)
    out = lax.psum_scatter(out, "ty", scatter_dimension=0, tiled=True)
    cotangent = lax.all_gather(grad_out, "ty", axis=0, tiled=True)
    cotangent = lax.all_gather(cotangent, "tz", axis=0, tiled=True)
    grad_hidden = lax.dot_general(
        cotangent, weight, (((1,), (1,)), ((), ())), preferred_element_type=jnp.float32
    )
    grad_weight = weight_gradient(hidden, cotangent)
    grad_gate = (
        grad_hidden * up_value * sigmoid_gate * (1.0 + gate_value * (1.0 - sigmoid_gate))
    ).astype(jnp.bfloat16)
    grad_up = (grad_hidden * gate_value * sigmoid_gate).astype(jnp.bfloat16)
    return (out, grad_gate, grad_up, grad_weight)


def split_mesh(mesh):
    n_dp, n_tensor = mesh.shape["dp"], mesh.shape["tensor"]
    devices = mesh.devices.reshape(2, n_dp // 4, 2, n_tensor // 2, 2)
    return Mesh(devices, DP + TP)


def solution(mesh):
    fine = split_mesh(mesh)
    in_specs = (
        P(DP, TP),
        P(DP, TP),
        P(DP + TP, None),
        P(TP, None),
        P(TP, None),
    )
    out_specs = (P(DP + TP, None), P(DP, TP), P(DP, TP), P(TP, DP))
    return jax.shard_map(
        per_device, mesh=fine, in_specs=in_specs, out_specs=out_specs, check_vma=False
    )
```

time: 412 us -> 248 us (0.60)
  waiting for transfers between devices: 356 us -> 180 us
  blocking collectives: 0 us -> 9.37 us
    reduce_scatter x2 -> x3, waiting for transfers between devices: 271 us -> 125 us  [the longest x1 74.8 us: weight_gradient(): lax.psum_scatter(partial_grad.astype(jnp.bfloat16), DP, scatter_dimension...]
    all_gather x1, waiting for transfers between devices: 84.4 us -> 55 us  [per_device(): cotangent = lax.all_gather(cotangent, 'tz', axis=0, tiled=True)]
    all_gather x0 -> x1, blocking collectives: none -> 9.37 us  [per_device(): cotangent = lax.all_gather(grad_out, 'ty', axis=0, tiled=True)]
  transfers between devices with their start and end apart: 3 -> 4, of which waited for: 3 -> 4; matrix products, arithmetic and copies ran while one was open for 9% -> 9% of each run, Pallas kernels for 0% -> 0%
where the time goes in v1:
time: 248 us; the launch traced here: 245 us
  waiting for transfers between devices  180 us (73%)
  matrix products  26.2 us (11%)
  between operations  13.8 us (6%)
  local copies, waits for them, and re-layouts  10.8 us (4%)
  blocking collectives  9.37 us (4%)
  other arithmetic  4.89 us (2%)
    reduce_scatter x1, waiting for transfers between devices, weight_gradient(): lax.psum_scatter(partial_grad.astype(jnp.bfloat16), DP, scatter_dimension...  74.8 us
    all_gather x1, waiting for transfers between devices, per_device(): cotangent = lax.all_gather(cotangent, 'tz', axis=0, tiled=True)  55 us
    reduce_scatter x1, waiting for transfers between devices, per_device(): out = lax.psum_scatter(partial_out, 'tz', scatter_dimension=0, tiled=True)  48.8 us
    unnamed x14, local copies, waits for them, and re-layouts  10.8 us
    dot_general x1, matrix products, per_device(): lax.dot_general(cotangent, weight, (((1,), (1,)), ((), ())), preferred_el...  9.8 us
    all_gather x1, blocking collectives, per_device(): cotangent = lax.all_gather(grad_out, 'ty', axis=0, tiled=True)  9.37 us
    dot_general x1, matrix products, weight_gradient(): lax.dot_general(hidden, cotangent, (((0,), (0,)), ((), ())), preferred_el...  8.41 us
    dot_general x1, matrix products, per_device(): jnp.dot(hidden, weight, preferred_element_type=jnp.float32)  7.98 us
  transfers between devices with their start and end apart: 4, of which 4 were waited for; matrix products, arithmetic and copies ran while one was open for 9% of the time, Pallas kernels for 0%

profile of v1, /device:TPU:1, one launch (start us, length us, event | category | flops | bytes accessed | tf_op | source)
XLA Modules:
  0.0 245.2 jit_solution(4515552533059041806)
XLA Ops:
  7.2 0.0 copy-start.1
  7.2 0.0 reduce-scatter.4.cloned.1.call-start
  7.2 1.2 exponential_convert_fusion
  8.4 2.2 copy.10
  10.7 0.0 copy-done.1
  10.7 1.3 copy.9
  11.9 3.7 %bitcast_multiply_fusion = bf16[896,4096]{1,0:T(8,128)(2,1)S(1)} fusion(bf16[896,4096]{1,0:T(8,128)(2,1)} %param.8, bf16[28,4096]{1,0:T(8,128)(2,1)S(1)} %exponential_convert_fusion), kind=kLoop, calls=%fused_computation | loop fusion | flops 3670016 | bytes 14909440 | tf_op jit(solution)/shard_map/mul | solution.py:12
  15.6 0.0 copy-start
  15.6 2.9 %copy-done = bf16[896,4096]{1,0:T(8,128)(2,1)} copy-done((bf16[896,4096]{1,0:T(8,128)(2,1)}, bf16[896,4096]{1,0:T(8,128)(2,1)S(1)}, u32[]{:S(2)}) %copy-start) | copy-done | bytes 7340056
  18.6 8.0 %convolution_convert_fusion.1 = bf16[512,4096]{1,0:T(8,128)(2,1)} fusion(bf16[896,4096]{1,0:T(8,128)(2,1)S(1)} %bitcast_multiply_fusion, bf16[512,896]{0,1:T(8,128)(2,1)} %copy.10, bf16[512,896]{0,1:T(8,128)(2,1)} %copy.9), kind=kOutput, calls=%fused_computation.2 | convolution fusion | flops 3763863552 | bytes 13369344 | tf_op jit(solution)/shard_map/dot_general | solution.py:31
  26.5 0.0 copy-start.4
  26.5 0.0 reduce-scatter.4.cloned.1.call-update
  26.6 0.0 copy-start.2
  26.6 0.0 copy-start.3
  26.6 0.0 all-gather.2.cloned.1.call-start
  26.6 0.8 copy-done.4
  27.5 9.4 %all_gather.6 = bf16[64,4096]{1,0:T(8,128)(2,1)} all-gather(bf16[32,4096]{1,0:T(8,128)(2,1)S(1)} %copy-done.4), channel_id=1, replica_groups=mesh['dy'=2,'dx'=4,'dc'=2,'tz'=8,'ty'=2] {'ty'}, dimensions={0}, use_global_device_ids=true | all-gather | bytes 786432 | tf_op jit(solution)/shard_map/all_gather | solution.py:34
  36.9 0.0 all-gather.2.cloned.1.call-update
  36.9 0.0 reduce-scatter.6.cloned.1.call-start
  36.9 48.8 %reduce-scatter.4.cloned.1.call-done = bf16[64,4096]{1,0:T(8,128)(2,1)} async-done(((bf16[512,4096]{1,0:T(8,128)(2,1)}), bf16[64,4096]{1,0:T(8,128)(2,1)}) %reduce-scatter.4.cloned.1.call-update) | async-done | bytes 524304 | tf_op jit(solution)/shard_map/reduce_scatter | solution.py:32
  85.8 0.0 reduce-scatter.6.cloned.1.call-update
  85.8 0.0 reduce-scatter.8.cloned.1.call-start
  85.9 55.0 %all-gather.2.cloned.1.call-done = bf16[512,4096]{1,0:T(8,128)(2,1)} async-done(((bf16[64,4096]{1,0:T(8,128)(2,1)}), bf16[512,4096]{1,0:T(8,128)(2,1)}) %all-gather.2.cloned.1.call-update) | async-done | bytes 4194320 | tf_op jit(solution)/shard_map/all_gather | solution.py:35
  140.9 0.0 copy-done.2
  140.9 0.0 copy-done.3
  140.9 8.4 %convolution_convert_fusion = bf16[896,4096]{1,0:T(8,128)(2,1)} fusion(bf16[512,4096]{1,0:T(8,128)(2,1)} %all-gather.2.cloned.1.call-done, bf16[512,896]{0,1:T(8,128)(2,1)S(1)} %copy-done.2, bf16[512,896]{0,1:T(8,128)(2,1)S(1)} %copy-done.3), kind=kOutput, calls=%fused_computation.1 | convolution fusion | flops 3765436416 | bytes 13369344 | tf_op jit(solution)/shard_map/dot_general | solution.py:17
  149.3 0.0 reduce-scatter.8.cloned.1.call-update
  149.3 9.8 %fusion.9 = (bf16[512,896]{0,1:T(8,128)(2,1)S(1)}, bf16[512,896]{0,1:T(8,128)(2,1)}) fusion(bf16[512,896]{0,1:T(8,128)(2,1)S(1)} %copy-done.3, bf16[512,896]{0,1:T(8,128)(2,1)S(1)} %copy-done.2, bf16[896,4096]{1,0:T(8,128)(2,1)} %copy-done, bf16[512,4096]{1,0:T(8,128)(2,1)} %all-gather.2.cloned.1.call-done), kind=kOutput, calls=%fused_computation.18 | convolution fusion | flops 3764977664 | bytes 15204352 | tf_op jit(solution)/shard_map/dot_general | solution.py:36
  159.1 2.2 copy.11
  161.3 1.3 copy.12
  162.6 1.2 reduce-scatter.6.cloned.1.call-done
  163.8 74.8 %reduce-scatter.8.cloned.1.call-done = bf16[896,256]{1,0:T(8,128)(2,1)} async-done(((bf16[896,4096]{1,0:T(8,128)(2,1)}), bf16[896,256]{1,0:T(8,128)(2,1)}) %reduce-scatter.8.cloned.1.call-update) | async-done | bytes 458768 | tf_op jit(solution)/shard_map/reduce_scatter | solution.py:20
Async XLA Ops:
  7.2 3.5 %copy-start.1 = (bf16[512,896]{1,0:T(8,128)(2,1)S(1)}, bf16[512,896]{1,0:T(8,128)(2,1)}, u32[]{:S(2)}) copy-start(bf16[512,896]{1,0:T(8,128)(2,1)} %param.5) | copy-start | bytes 2752516
  7.2 78.6 %reduce-scatter.4.cloned.1.call-start = ((), (), s32[]{:S(2)}) async-start(), calls=%async_computation.3 | async-start | bytes 4718592 | tf_op jit(solution)/shard_map/reduce_scatter | solution.py:32
  15.6 2.9 %copy-start = (bf16[896,4096]{1,0:T(8,128)(2,1)}, bf16[896,4096]{1,0:T(8,128)(2,1)S(1)}, u32[]{:S(2)}) copy-start(bf16[896,4096]{1,0:T(8,128)(2,1)S(1)} %bitcast_multiply_fusion) | copy-start | bytes 22020100
  26.5 0.9 copy-start.4
  26.6 114.3 %copy-start.2 = (bf16[512,896]{0,1:T(8,128)(2,1)S(1)}, bf16[512,896]{0,1:T(8,128)(2,1)}, u32[]{:S(2)}) copy-start(bf16[512,896]{0,1:T(8,128)(2,1)} %copy.10) | copy-start | bytes 2752516
  26.6 114.3 %copy-start.3 = (bf16[512,896]{0,1:T(8,128)(2,1)S(1)}, bf16[512,896]{0,1:T(8,128)(2,1)}, u32[]{:S(2)}) copy-start(bf16[512,896]{0,1:T(8,128)(2,1)} %copy.9) | copy-start | bytes 2752516
  26.6 114.3 %all-gather.2.cloned.1.call-start = ((), (), s32[]{:S(2)}) async-start(), calls=%async_computation.5 | async-start | bytes 4718592 | tf_op jit(solution)/shard_map/all_gather | solution.py:35
  36.9 127.0 %reduce-scatter.6.cloned.1.call-start = ((), (), s32[]{:S(2)}) async-start(), calls=%async_computation.4 | async-start | bytes 786432 | tf_op jit(solution)/shard_map/reduce_scatter | solution.py:33
  85.8 152.9 %reduce-scatter.8.cloned.1.call-start = ((), (), s32[]{:S(2)}) async-start(), calls=%async_computation.6 | async-start | bytes 7798784 | tf_op jit(solution)/shard_map/reduce_scatter | solution.py:20
Sparse Core Ops, SparseCore 0:
  26.7 59.0 reduce-scatter.3
  87.6 53.2 all-gather.1
  144.0 19.8 reduce-scatter.5
  166.8 71.7 reduce-scatter.7

commit v2 on v1

--- a/solution.py
+++ b/solution.py
@@ -13,13 +13,32 @@
     return blocks.reshape(codes.shape)
 
 
+def exchange(value, axis, size, shift):
+    perm = [(i, (i + shift) % size) for i in range(size)]
+    return lax.ppermute(value, axis, perm)
+
+
 def weight_gradient(hidden, cotangent):
     partial_grad = lax.dot_general(
         hidden, cotangent, (((0,), (0,)), ((), ())), preferred_element_type=jnp.float32
-    )
-    return lax.psum_scatter(
-        partial_grad.astype(jnp.bfloat16), DP, scatter_dimension=1, tiled=True
-    )
+    ).astype(jnp.bfloat16)
+    rows = partial_grad.shape[0]
+    n_x = partial_grad.shape[1] // 1024
+    parts = partial_grad.reshape(rows, 2, n_x, 2, 256)
+    dc = lax.axis_index("dc")
+    mine = jnp.take(parts, dc, axis=3)
+    theirs = jnp.take(parts, 1 - dc, axis=3)
+    total = mine.astype(jnp.float32) + exchange(theirs, "dc", 2, 1).astype(jnp.float32)
+    sent = total.astype(jnp.bfloat16)
+    dx = lax.axis_index("dx")
+    acc = jnp.take(total, dx, axis=2)
+    for shift in range(1, n_x):
+        block = jnp.take(sent, (dx + shift) % n_x, axis=2)
+        acc = acc + exchange(block, "dx", n_x, shift).astype(jnp.float32)
+    dy = lax.axis_index("dy")
+    sent = acc.astype(jnp.bfloat16)
+    acc = jnp.take(acc, dy, axis=1) + exchange(jnp.take(sent, 1 - dy, axis=1), "dy", 2, 1).astype(jnp.float32)
+    return acc.astype(jnp.bfloat16)
 
 
 def per_device(gate_pre, up_pre, grad_out, codes, scales):

time: 248 us -> 210 us (0.85); the launches traced: 245 us -> 210 us
  waiting for transfers between devices: 180 us -> 87.5 us
  local copies, waits for them, and re-layouts: 10.8 us -> 41.5 us
  other arithmetic: 4.89 us -> 23.8 us
  starting transfers between devices: 0.16 us -> 5.73 us
  blocking collectives: 9.37 us -> 12.1 us
    reduce_scatter x1 -> x0, waiting for transfers between devices: 74.8 us -> none  [weight_gradient(): lax.psum_scatter(partial_grad.astype(jnp.bfloat16), DP, scatter_dimension...]
    reduce_scatter x1, waiting for transfers between devices: 48.8 us -> 0.01 us  [per_device(): out = lax.psum_scatter(partial_out, 'tz', scatter_dimension=0, tiled=True)]
    ppermute x0 -> x5, waiting for transfers between devices: none -> 48.7 us  [exchange(): return lax.ppermute(value, axis, perm)]
    another operation x0 -> x1, local copies, waits for them, and re-layouts: none -> 17.7 us  [weight_gradient(): mine = jnp.take(parts, dc, axis=3)]
    all_gather x1, waiting for transfers between devices: 55 us -> 38.7 us  [per_device(): cotangent = lax.all_gather(cotangent, 'tz', axis=0, tiled=True)]
    reshape x0 -> x1, local copies, waits for them, and re-layouts: none -> 13 us  [weight_gradient(): parts = partial_grad.reshape(rows, 2, n_x, 2, 256)]
    convert_element_type x0 -> x2, other arithmetic: none -> 10.9 us  [the longest x1 10 us: weight_gradient(): sent = total.astype(jnp.bfloat16)]
    select_n x0 -> x3, other arithmetic: none -> 6.27 us  [the longest x1 4.28 us: weight_gradient(): theirs = jnp.take(parts, 1 - dc, axis=3)]
  transfers between devices with their start and end apart: 4 -> 8, of which waited for: 4 -> 5; matrix products, arithmetic and copies ran while one was open for 9% -> 42% of each run, Pallas kernels for 0% -> 0%
where the time goes in v2:
time: 210 us
  waiting for transfers between devices  87.5 us (42%)
  local copies, waits for them, and re-layouts  41.5 us (20%)
  matrix products  25.3 us (12%)
  other arithmetic  23.8 us (11%)
  between operations  13.8 us (7%)
  blocking collectives  12.1 us (6%)
  starting transfers between devices  5.73 us (3%)
    ppermute x5, waiting for transfers between devices, exchange(): return lax.ppermute(value, axis, perm)  48.7 us
    all_gather x1, waiting for transfers between devices, per_device(): cotangent = lax.all_gather(cotangent, 'tz', axis=0, tiled=True)  38.7 us
    another operation x1, local copies, waits for them, and re-layouts, weight_gradient(): mine = jnp.take(parts, dc, axis=3)  17.7 us
    reshape x1, local copies, waits for them, and re-layouts, weight_gradient(): parts = partial_grad.reshape(rows, 2, n_x, 2, 256)  13 us
    all_gather x1, blocking collectives, per_device(): cotangent = lax.all_gather(grad_out, 'ty', axis=0, tiled=True)  12.1 us
    unnamed x18, local copies, waits for them, and re-layouts  10.9 us
    convert_element_type x1, other arithmetic, weight_gradient(): sent = total.astype(jnp.bfloat16)  10 us
    dot_general x1, matrix products, per_device(): lax.dot_general(cotangent, weight, (((1,), (1,)), ((), ())), preferred_el...  8.91 us
  transfers between devices with their start and end apart: 8, of which 5 were waited for; matrix products, arithmetic and copies ran while one was open for 42% of the time, Pallas kernels for 0%

profile of v2, /device:TPU:1, one launch (start us, length us, event | category | flops | bytes accessed | tf_op | source)
XLA Modules:
  0.0 209.7 jit_solution(8275430707940729730)
XLA Ops:
  7.2 0.0 all-gather.2.cloned.1.call-start
  7.2 12.1 %all_gather.6 = bf16[64,4096]{1,0:T(8,128)(2,1)} all-gather(bf16[32,4096]{1,0:T(8,128)(2,1)} %param.11), channel_id=1, replica_groups=mesh['dy'=2,'dx'=4,'dc'=2,'tz'=8,'ty'=2] {'ty'}, dimensions={0}, use_global_device_ids=true | all-gather | bytes 786432 | tf_op jit(solution)/shard_map/all_gather | solution.py:53
  19.3 0.0 reduce-scatter.3.cloned.1.call-start
  19.4 2.2 %copy.10 = bf16[512,896]{0,1:T(8,128)(2,1)} copy(bf16[512,896]{1,0:T(8,128)(2,1)} %param.10) | data formatting | bytes 1835008 | tf_op args[1]
  21.6 1.3 copy.9
  22.9 0.1 exponential_convert_fusion
  23.0 3.7 %bitcast_multiply_fusion = bf16[896,4096]{1,0:T(8,128)(2,1)S(1)} fusion(bf16[896,4096]{1,0:T(8,128)(2,1)} %param.12, bf16[28,4096]{1,0:T(8,128)(2,1)S(1)} %exponential_convert_fusion), kind=kLoop, calls=%fused_computation | loop fusion | flops 3670016 | bytes 14909440 | tf_op jit(solution)/shard_map/mul | solution.py:12
  26.7 2.9 %copy-done = bf16[896,4096]{1,0:T(8,128)(2,1)} copy-done((bf16[896,4096]{1,0:T(8,128)(2,1)}, bf16[896,4096]{1,0:T(8,128)(2,1)S(1)}, u32[]{:S(2)}) %copy-start) | copy-done | bytes 7340056
  29.6 8.1 %convolution_convert_fusion.1 = bf16[512,4096]{1,0:T(8,128)(2,1)} fusion(bf16[896,4096]{1,0:T(8,128)(2,1)S(1)} %bitcast_multiply_fusion, bf16[512,896]{0,1:T(8,128)(2,1)} %copy.10, bf16[512,896]{0,1:T(8,128)(2,1)} %copy.9), kind=kOutput, calls=%fused_computation.3 | convolution fusion | flops 3763863552 | bytes 13369344 | tf_op jit(solution)/shard_map/dot_general | solution.py:50
  37.7 0.0 reduce-scatter.5.cloned.1.call-start
  37.8 38.7 %all-gather.2.cloned.1.call-done = bf16[512,4096]{1,0:T(8,128)(2,1)} async-done(((bf16[64,4096]{1,0:T(8,128)(2,1)}), bf16[512,4096]{1,0:T(8,128)(2,1)}) %all-gather.2.cloned.1.call-update) | async-done | bytes 4194320 | tf_op jit(solution)/shard_map/all_gather | solution.py:54
  76.5 8.3 %convolution_convert_fusion = bf16[896,4096]{1,0:T(8,128)(2,1)} fusion(bf16[512,4096]{1,0:T(8,128)(2,1)} %all-gather.2.cloned.1.call-done, bf16[512,896]{0,1:T(8,128)(2,1)S(1)} %copy-done.2, bf16[512,896]{0,1:T(8,128)(2,1)S(1)} %copy-done.3), kind=kOutput, calls=%fused_computation.2 | convolution fusion | flops 3765436416 | bytes 13369344 | tf_op jit(solution)/shard_map/dot_general | solution.py:22
  84.8 13.0 %reshape.20 = bf16[896,2,4,2,256]{4,3,2,1,0:T(2,128)(2,1)} reshape(bf16[896,4096]{1,0:T(8,128)(2,1)} %convolution_convert_fusion) | data formatting | bytes 14680064 | tf_op jit(solution)/shard_map/reshape | solution.py:27
  97.8 17.7 %constant_dynamic-slice_fusion.1 = (bf16[896,2,4,1,256]{4,3,2,1,0:T(2,128)(2,1)}, bf16[896,2,4,1,256]{4,3,2,1,0:T(2,128)(2,1)S(1)}) fusion(bf16[896,2,4,2,256]{4,3,2,1,0:T(2,128)(2,1)} %reshape.20, s32[]{:T(128)S(6)} %select_n.82, s32[]{:T(128)S(6)} %select_n.84), kind=kLoop, calls=%fused_computation.37 | loop fusion | bytes 14680072 | tf_op jit(solution)/shard_map/jit(_take) | solution.py:29
  115.4 4.3 %fusion = bf16[896,2,4,256]{3,0,1,2:T(8,128)(2,1)} fusion(bf16[896,2,4,1,256]{4,3,2,1,0:T(2,128)(2,1)S(1)} %get-tuple-element.68, pred[]{:T(512)S(6)} %and.52), kind=kLoop, calls=%fused_computation.5 | loop fusion | flops 1835008 | bytes 7340033 | tf_op jit(solution)/shard_map/jit(_take)/select_n | solution.py:30
  119.7 0.8 collective-permute-start
  120.6 6.4 %collective-permute-done = bf16[896,2,4,256]{3,0,1,2:T(8,128)(2,1)} collective-permute-done((bf16[896,2,4,256]{3,0,1,2:T(8,128)(2,1)}, bf16[896,2,4,256]{3,0,1,2:T(8,128)(2,1)}, u32[]{:S(2)}, u32[]{:S(2)}) %collective-permute-start) | collective-permute-done | bytes 3670048 | tf_op jit(solution)/shard_map/ppermute | solution.py:18
  127.0 10.0 %fusion.19 = (bf16[896,2,4,256]{3,0,1,2:T(8,128)(2,1)S(1)}, f32[896,2,4,256]{3,0,1,2:T(8,128)}) fusion(bf16[896,2,4,256]{3,0,1,2:T(8,128)(2,1)} %collective-permute-done, bf16[896,2,4,1,256]{4,3,2,1,0:T(2,128)(2,1)} %get-tuple-element.67, pred[]{:T(512)S(6)} %and.51), kind=kLoop, calls=%fused_computation.38 | loop fusion | flops 9175040 | bytes 18350080 | tf_op jit(solution)/shard_map/convert_element_type | solution.py:32
  137.0 1.2 select_bitcast_fusion.2
  138.1 2.4 %collective-permute-start.3 = (bf16[896,2,256]{2,0,1:T(8,128)(2,1)}, bf16[896,2,256]{2,0,1:T(8,128)(2,1)}, u32[]{:S(2)}, u32[]{:S(2)}) collective-permute-start(bf16[896,2,256]{2,0,1:T(8,128)(2,1)} %get-tuple-element.70), channel_id=1, source_target_pairs={{0,96},{32,0},{64,32},{96,64},{1,97},{33,1},{65,33},{97,65},{2,98}... | collective-permute-start | bytes 2752520 | tf_op jit(solution)/shard_map/ppermute | solution.py:18
  140.5 0.6 collective-permute-start.2
  141.1 0.6 collective-permute-start.1
  141.7 19.2 %collective-permute-done.3 = bf16[896,2,256]{2,0,1:T(8,128)(2,1)} collective-permute-done((bf16[896,2,256]{2,0,1:T(8,128)(2,1)}, bf16[896,2,256]{2,0,1:T(8,128)(2,1)}, u32[]{:S(2)}, u32[]{:S(2)}) %collective-permute-start.3) | collective-permute-done | bytes 917536 | tf_op jit(solution)/shard_map/ppermute | solution.py:18
  160.9 2.6 %collective-permute-done.2 = bf16[896,2,256]{2,0,1:T(8,128)(2,1)} collective-permute-done((bf16[896,2,256]{2,0,1:T(8,128)(2,1)S(1)}, bf16[896,2,256]{2,0,1:T(8,128)(2,1)}, u32[]{:S(2)}, u32[]{:S(2)}) %collective-permute-start.2) | collective-permute-done | bytes 917536 | tf_op jit(solution)/shard_map/ppermute | solution.py:18
  163.5 20.6 %collective-permute-done.1 = bf16[896,2,256]{2,0,1:T(8,128)(2,1)} collective-permute-done((bf16[896,2,256]{2,0,1:T(8,128)(2,1)S(1)}, bf16[896,2,256]{2,0,1:T(8,128)(2,1)}, u32[]{:S(2)}, u32[]{:S(2)}) %collective-permute-start.1) | collective-permute-done | bytes 917536 | tf_op jit(solution)/shard_map/ppermute | solution.py:18
  184.1 2.9 %fusion.13 = f32[896,2,256]{2,0,1:T(8,128)S(1)} fusion(f32[896,2,4,256]{3,0,1,2:T(8,128)} %get-tuple-element.66, s32[]{:T(128)S(6)} %select_n.52, bf16[896,2,256]{2,0,1:T(8,128)(2,1)} %collective-permute-done.3, bf16[896,2,256]{2,0,1:T(8,128)(2,1)} %collective-permute-done.2, bf16[896,2,256]{2,0,1:T(8,128)(2,1)} %collective-permute-done.1, pred[]{:T(512)S(6)} %and.49), kind=kLoop, calls=%fused_computation.26 | loop fusion | flops 3211264 | bytes 6422533 | tf_op jit(solution)/shard_map/add | solution.py:37
  186.9 0.8 fusion.16
  187.8 1.2 collective-permute-start.4
  189.0 8.9 %fusion.11 = (bf16[512,896]{0,1:T(8,128)(2,1)}, bf16[512,896]{0,1:T(8,128)(2,1)}) fusion(bf16[512,896]{0,1:T(8,128)(2,1)S(1)} %copy-done.4, bf16[512,896]{0,1:T(8,128)(2,1)S(1)} %copy-done.2, bf16[896,4096]{1,0:T(8,128)(2,1)} %copy-done, bf16[512,4096]{1,0:T(8,128)(2,1)S(1)} %copy-done.6), kind=kOutput, calls=%fused_computation.23 | convolution fusion | flops 3764977664 | bytes 15204352 | tf_op jit(solution)/shard_map/dot_general | solution.py:55
  197.9 2.2 %copy.13 = bf16[512,896]{1,0:T(8,128)(2,1)} copy(bf16[512,896]{0,1:T(8,128)(2,1)} %get-tuple-element.73) | data formatting | bytes 1835008
  200.1 2.2 %copy.14 = bf16[512,896]{1,0:T(8,128)(2,1)} copy(bf16[512,896]{0,1:T(8,128)(2,1)} %get-tuple-element.72) | data formatting | bytes 1835008
  202.3 0.9 fusion.14
  (19 shorter events, 0.1 us)
Async XLA Ops:
  7.2 14.4 %copy-start.1 = (bf16[512,896]{1,0:T(8,128)(2,1)S(1)}, bf16[512,896]{1,0:T(8,128)(2,1)}, u32[]{:S(2)}) copy-start(bf16[512,896]{1,0:T(8,128)(2,1)} %param.9) | copy-start | bytes 2752516
  7.2 15.7 %copy-start.5 = (s32[28,4096]{1,0:T(8,128)S(1)}, s32[28,4096]{1,0:T(8,128)}, u32[]{:S(2)}) copy-start(s32[28,4096]{1,0:T(8,128)} %param.13) | copy-start | bytes 1376260
  7.2 69.3 %all-gather.2.cloned.1.call-start = ((), (), s32[]{:S(2)}) async-start(), calls=%async_computation.4 | async-start | bytes 4718592 | tf_op jit(solution)/shard_map/all_gather | solution.py:54
  19.3 122.4 %reduce-scatter.3.cloned.1.call-start = ((), (), s32[]{:S(2)}) async-start(), calls=%async_computation.2 | async-start | bytes 4718592 | tf_op jit(solution)/shard_map/reduce_scatter | solution.py:51
  26.7 2.9 %copy-start = (bf16[896,4096]{1,0:T(8,128)(2,1)}, bf16[896,4096]{1,0:T(8,128)(2,1)S(1)}, u32[]{:S(2)}) copy-start(bf16[896,4096]{1,0:T(8,128)(2,1)S(1)} %bitcast_multiply_fusion) | copy-start | bytes 22020100
  37.7 38.8 %copy-start.2 = (bf16[512,896]{0,1:T(8,128)(2,1)S(1)}, bf16[512,896]{0,1:T(8,128)(2,1)}, u32[]{:S(2)}) copy-start(bf16[512,896]{0,1:T(8,128)(2,1)} %copy.10) | copy-start | bytes 2752516
  37.7 38.8 %copy-start.3 = (bf16[512,896]{0,1:T(8,128)(2,1)S(1)}, bf16[512,896]{0,1:T(8,128)(2,1)}, u32[]{:S(2)}) copy-start(bf16[512,896]{0,1:T(8,128)(2,1)} %copy.9) | copy-start | bytes 2752516
  37.7 165.5 %reduce-scatter.5.cloned.1.call-start = ((), (), s32[]{:S(2)}) async-start(), calls=%async_computation.3 | async-start | bytes 786432 | tf_op jit(solution)/shard_map/reduce_scatter | solution.py:52
  119.7 7.2 %collective-permute-start = (bf16[896,2,4,256]{3,0,1,2:T(8,128)(2,1)}, bf16[896,2,4,256]{3,0,1,2:T(8,128)(2,1)}, u32[]{:S(2)}, u32[]{:S(2)}) collective-permute-start(bf16[896,2,4,256]{3,0,1,2:T(8,128)(2,1)} %fusion), channel_id=1, source_target_pairs={{0,16},{16,0},{1,17},{17,1},{2,18},{18,2},{3,19},{19,3},{4,20},{20... | collective-permute-start | bytes 11010056 | tf_op jit(solution)/shard_map/ppermute | solution.py:18
  138.1 22.8 %collective-permute-start.3 = (bf16[896,2,256]{2,0,1:T(8,128)(2,1)}, bf16[896,2,256]{2,0,1:T(8,128)(2,1)}, u32[]{:S(2)}, u32[]{:S(2)}) collective-permute-start(bf16[896,2,256]{2,0,1:T(8,128)(2,1)} %get-tuple-element.70), channel_id=1, source_target_pairs={{0,96},{32,0},{64,32},{96,64},{1,97},{33,1},{65,33},{97,65},{2,98}... | collective-permute-start | bytes 2752520 | tf_op jit(solution)/shard_map/ppermute | solution.py:18
  140.5 22.9 %collective-permute-start.2 = (bf16[896,2,256]{2,0,1:T(8,128)(2,1)S(1)}, bf16[896,2,256]{2,0,1:T(8,128)(2,1)}, u32[]{:S(2)}, u32[]{:S(2)}) collective-permute-start(bf16[896,2,256]{2,0,1:T(8,128)(2,1)S(1)} %get-tuple-element.71), channel_id=1, source_target_pairs={{0,64},{32,96},{64,0},{96,32},{1,65},{33,97},{65,1},{97,33},{2,66}... | collective-permute-start | bytes 2752520 | tf_op jit(solution)/shard_map/ppermute | solution.py:18
  141.1 43.0 %collective-permute-start.1 = (bf16[896,2,256]{2,0,1:T(8,128)(2,1)S(1)}, bf16[896,2,256]{2,0,1:T(8,128)(2,1)}, u32[]{:S(2)}, u32[]{:S(2)}) collective-permute-start(bf16[896,2,256]{2,0,1:T(8,128)(2,1)S(1)} %get-tuple-element.69), channel_id=1, source_target_pairs={{0,32},{32,64},{64,96},{96,0},{1,33},{33,65},{65,97},{97,1},{2,34}... | collective-permute-start | bytes 2752520 | tf_op jit(solution)/shard_map/ppermute | solution.py:18
  184.1 4.9 %copy-start.4 = (bf16[512,896]{0,1:T(8,128)(2,1)S(1)}, bf16[512,896]{0,1:T(8,128)(2,1)}, u32[]{:S(2)}) copy-start(bf16[512,896]{0,1:T(8,128)(2,1)} %copy.9) | copy-start | bytes 2752516
  184.1 4.9 %copy-start.6 = (bf16[512,4096]{1,0:T(8,128)(2,1)S(1)}, bf16[512,4096]{1,0:T(8,128)(2,1)}, u32[]{:S(2)}) copy-start(bf16[512,4096]{1,0:T(8,128)(2,1)} %all-gather.2.cloned.1.call-done) | copy-start | bytes 12582916
  187.8 14.5 %collective-permute-start.4 = (bf16[896,256]{1,0:T(8,128)(2,1)}, bf16[896,256]{1,0:T(8,128)(2,1)S(1)}, u32[]{:S(2)}, u32[]{:S(2)}) collective-permute-start(bf16[896,256]{1,0:T(8,128)(2,1)} %fusion.16), channel_id=1, source_target_pairs={{0,128},{128,0},{1,129},{129,1},{2,130},{130,2},{3,131},{131,3},{4... | collective-permute-start | bytes 1376264 | tf_op jit(solution)/shard_map/ppermute | solution.py:18
Sparse Core Ops, SparseCore 0:
  19.5 56.9 all-gather.1
  79.0 54.0 reduce-scatter.2
  141.8 19.4 reduce-scatter.4

commit v3 on v2

--- a/solution.py
+++ b/solution.py
@@ -1,6 +1,7 @@
 import jax
 import jax.numpy as jnp
 from jax import lax
+from jax.experimental.layout import Layout, with_layout_constraint
 from jax.sharding import Mesh, PartitionSpec as P
 
 DP = ("dy", "dx", "dc")
@@ -19,26 +20,29 @@
 
 
 def weight_gradient(hidden, cotangent):
-    partial_grad = lax.dot_general(
-        hidden, cotangent, (((0,), (0,)), ((), ())), preferred_element_type=jnp.float32
+    n_x = cotangent.shape[1] // 1024
+    width = 256
+    partial = lax.dot_general(
+        cotangent, hidden, (((0,), (0,)), ((), ())), preferred_element_type=jnp.float32
     ).astype(jnp.bfloat16)
-    rows = partial_grad.shape[0]
-    n_x = partial_grad.shape[1] // 1024
-    parts = partial_grad.reshape(rows, 2, n_x, 2, 256)
+    partial = with_layout_constraint(partial, Layout(major_to_minor=(0, 1)))
+    parts = partial.reshape(2, n_x, 2, width, partial.shape[1])
     dc = lax.axis_index("dc")
-    mine = jnp.take(parts, dc, axis=3)
-    theirs = jnp.take(parts, 1 - dc, axis=3)
-    total = mine.astype(jnp.float32) + exchange(theirs, "dc", 2, 1).astype(jnp.float32)
+    mine = jnp.take(parts, dc, axis=2)
+    arrived = exchange(jnp.take(parts, 1 - dc, axis=2), "dc", 2, 1)
+    total = mine.astype(jnp.float32) + arrived.astype(jnp.float32)
+    total = with_layout_constraint(total, Layout(major_to_minor=(0, 1, 2, 3)))
     sent = total.astype(jnp.bfloat16)
     dx = lax.axis_index("dx")
-    acc = jnp.take(total, dx, axis=2)
+    acc = jnp.take(total, dx, axis=1)
     for shift in range(1, n_x):
-        block = jnp.take(sent, (dx + shift) % n_x, axis=2)
+        block = jnp.take(sent, (dx + shift) % n_x, axis=1)
         acc = acc + exchange(block, "dx", n_x, shift).astype(jnp.float32)
     dy = lax.axis_index("dy")
     sent = acc.astype(jnp.bfloat16)
-    acc = jnp.take(acc, dy, axis=1) + exchange(jnp.take(sent, 1 - dy, axis=1), "dy", 2, 1).astype(jnp.float32)
-    return acc.astype(jnp.bfloat16)
+    acc = jnp.take(acc, dy, axis=0) + exchange(jnp.take(sent, 1 - dy, axis=0), "dy", 2, 1).astype(jnp.float32)
+    acc = with_layout_constraint(acc.astype(jnp.bfloat16), Layout(major_to_minor=(0, 1)))
+    return acc.T
 
 
 def per_device(gate_pre, up_pre, grad_out, codes, scales):
@@ -49,7 +53,12 @@
     hidden = (gate_value * sigmoid_gate * up_value).astype(jnp.bfloat16)
     partial_out = jnp.dot(hidden, weight, preferred_element_type=jnp.float32).astype(jnp.bfloat16)
     out = lax.psum_scatter(partial_out, "tz", scatter_dimension=0, tiled=True)
-    out = lax.psum_scatter(out, "ty", scatter_dimension=0, tiled=True)
+    rows = out.shape[0] // 2
+    ty = lax.axis_index("ty")
+    out = lax.dynamic_slice_in_dim(out, ty * rows, rows, 0).astype(jnp.float32) + exchange(
+        lax.dynamic_slice_in_dim(out, (1 - ty) * rows, rows, 0), "ty", 2, 1
+    ).astype(jnp.float32)
+    out = out.astype(jnp.bfloat16)
     cotangent = lax.all_gather(grad_out, "ty", axis=0, tiled=True)
     cotangent = lax.all_gather(cotangent, "tz", axis=0, tiled=True)
     grad_hidden = lax.dot_general(

time: 210 us -> 171 us (0.81)
  local copies, waits for them, and re-layouts: 41.5 us -> 14.1 us
  other arithmetic: 23.8 us -> 15.8 us
  matrix products: 25.3 us -> 21.2 us
  starting transfers between devices: 5.73 us -> 8.59 us
  waiting for transfers between devices: 87.5 us -> 84.9 us
    ppermute x5 -> x6, waiting for transfers between devices: 48.7 us -> 27.5 us  [exchange(): return lax.ppermute(value, axis, perm)]
    reduce_scatter x1, waiting for transfers between devices: 0.01 us -> 17.8 us  [per_device(): out = lax.psum_scatter(partial_out, 'tz', scatter_dimension=0, tiled=True)]
    another operation x1 -> x0, local copies, waits for them, and re-layouts: 17.7 us -> none  [weight_gradient(): mine = jnp.take(parts, dc, axis=3)]
    reshape x1 -> x0, local copies, waits for them, and re-layouts: 13 us -> none  [weight_gradient(): parts = partial_grad.reshape(rows, 2, n_x, 2, 256)]
    convert_element_type x2 -> x1, other arithmetic: 10.9 us -> 0.77 us  [per_device(): out = out.astype(jnp.bfloat16)]
    add x0 -> x1, other arithmetic: none -> 4.36 us  [weight_gradient(): total = mine.astype(jnp.float32) + arrived.astype(jnp.float32)]
    dot_general x1, matrix products: 8.91 us -> 5.85 us  [per_device(): lax.dot_general(cotangent, weight, (((1,), (1,)), ((), ())), preferred_el...]
    ppermute x5 -> x6, starting transfers between devices: 5.6 us -> 8.51 us  [exchange(): return lax.ppermute(value, axis, perm)]
  transfers between devices with their start and end apart: 8 -> 8, of which waited for: 5 -> 5; matrix products, arithmetic and copies ran while one was open for 42% -> 26% of each run, Pallas kernels for 0% -> 0%
where the time goes in v3:
time: 171 us
  waiting for transfers between devices  84.9 us (50%)
  matrix products  21.2 us (12%)
  other arithmetic  15.8 us (9%)
  between operations  14.2 us (8%)
  local copies, waits for them, and re-layouts  14.1 us (8%)
  blocking collectives  12.1 us (7%)
  starting transfers between devices  8.59 us (5%)
    all_gather x1, waiting for transfers between devices, per_device(): cotangent = lax.all_gather(cotangent, 'tz', axis=0, tiled=True)  39.5 us
    ppermute x6, waiting for transfers between devices, exchange(): return lax.ppermute(value, axis, perm)  27.5 us
    reduce_scatter x1, waiting for transfers between devices, per_device(): out = lax.psum_scatter(partial_out, 'tz', scatter_dimension=0, tiled=True)  17.8 us
    unnamed x35, local copies, waits for them, and re-layouts  13.1 us
    all_gather x1, blocking collectives, per_device(): cotangent = lax.all_gather(grad_out, 'ty', axis=0, tiled=True)  12.1 us
    ppermute x6, starting transfers between devices, exchange(): return lax.ppermute(value, axis, perm)  8.51 us
    dot_general x1, matrix products, per_device(): jnp.dot(hidden, weight, preferred_element_type=jnp.float32)  8.1 us
    dot_general x1, matrix products, weight_gradient(): lax.dot_general(cotangent, hidden, (((0,), (0,)), ((), ())), preferred_el...  7.19 us
  transfers between devices with their start and end apart: 8, of which 5 were waited for; matrix products, arithmetic and copies ran while one was open for 26% of the time, Pallas kernels for 0%

profile of v3, /device:TPU:1, one launch (start us, length us, event | category | flops | bytes accessed | tf_op | source)
XLA Modules:
  0.0 170.8 jit_solution(15946947193299180030)
XLA Ops:
  7.2 12.1 %all_gather.6 = bf16[64,4096]{1,0:T(8,128)(2,1)} all-gather(bf16[32,4096]{1,0:T(8,128)(2,1)} %param.11), channel_id=1, replica_groups=mesh['dy'=2,'dx'=4,'dc'=2,'tz'=8,'ty'=2] {'ty'}, dimensions={0}, use_global_device_ids=true | all-gather | bytes 786432 | tf_op jit(solution)/shard_map/all_gather | solution.py:62
  19.5 1.3 copy.17
  20.8 1.3 copy.16
  22.0 0.1 exponential_convert_fusion
  22.2 3.7 %bitcast_multiply_fusion = bf16[896,4096]{1,0:T(8,128)(2,1)S(1)} fusion(bf16[896,4096]{1,0:T(8,128)(2,1)} %param.12, bf16[28,4096]{1,0:T(8,128)(2,1)S(1)} %exponential_convert_fusion), kind=kLoop, calls=%fused_computation | loop fusion | flops 3670016 | bytes 14909440 | tf_op jit(solution)/shard_map/mul | solution.py:13
  25.8 2.9 %copy-done.1 = bf16[896,4096]{1,0:T(8,128)(2,1)} copy-done((bf16[896,4096]{1,0:T(8,128)(2,1)}, bf16[896,4096]{1,0:T(8,128)(2,1)S(1)}, u32[]{:S(2)}) %copy-start.1) | copy-done | bytes 7340056
  28.8 8.1 %convolution_convert_fusion.1 = bf16[512,4096]{1,0:T(8,128)(2,1)} fusion(bf16[896,4096]{1,0:T(8,128)(2,1)S(1)} %bitcast_multiply_fusion, bf16[512,896]{0,1:T(8,128)(2,1)} %copy.17, bf16[512,896]{0,1:T(8,128)(2,1)} %copy.16), kind=kOutput, calls=%fused_computation.3 | convolution fusion | flops 3763863552 | bytes 13369344 | tf_op jit(solution)/shard_map/dot_general | solution.py:54
  36.9 39.5 %all-gather.2.cloned.1.call-done = bf16[512,4096]{1,0:T(8,128)(2,1)} async-done(((bf16[64,4096]{1,0:T(8,128)(2,1)}), bf16[512,4096]{1,0:T(8,128)(2,1)}) %all-gather.2.cloned.1.call-update) | async-done | bytes 4194320 | tf_op jit(solution)/shard_map/all_gather | solution.py:63
  76.5 7.2 %convolution_convert_fusion = bf16[896,4096]{0,1:T(8,128)(2,1)S(1)} fusion(bf16[512,4096]{1,0:T(8,128)(2,1)} %all-gather.2.cloned.1.call-done, bf16[512,896]{0,1:T(8,128)(2,1)S(1)} %copy-done.5, bf16[512,896]{0,1:T(8,128)(2,1)S(1)} %copy-done.7), kind=kOutput, calls=%fused_computation.2 | convolution fusion | flops 3765436416 | bytes 13369344 | tf_op jit(solution)/shard_map/dot_general | solution.py:25
  83.7 3.0 %copy-done.2 = bf16[896,4096]{0,1:T(8,128)(2,1)} copy-done((bf16[896,4096]{0,1:T(8,128)(2,1)}, bf16[896,4096]{0,1:T(8,128)(2,1)S(1)}, u32[]{:S(2)}) %copy-start.2) | copy-done | bytes 7340056
  86.7 2.3 %fusion = bf16[2,4,256,896]{3,2,1,0:T(8,128)(2,1)} fusion(bf16[2,4,2,256,896]{4,3,2,1,0:T(8,128)(2,1)S(1)} %bitcast.52, s32[]{:T(128)S(6)} %select_n.90, pred[]{:T(512)S(6)} %and.53), kind=kLoop, calls=%fused_computation.5 | loop fusion | flops 1835008 | bytes 7340037 | tf_op jit(solution)/shard_map/jit(_take)/select_n | solution.py:32
  89.0 0.8 collective-permute-start.1
  89.8 6.4 %collective-permute-done.1 = bf16[2,4,256,896]{3,2,1,0:T(8,128)(2,1)} collective-permute-done((bf16[2,4,256,896]{3,2,1,0:T(8,128)(2,1)}, bf16[2,4,256,896]{3,2,1,0:T(8,128)(2,1)}, u32[]{:S(2)}, u32[]{:S(2)}) %collective-permute-start.1) | collective-permute-done | bytes 3670048 | tf_op jit(solution)/shard_map/ppermute | solution.py:19
  96.2 4.4 %convert_add_fusion = f32[2,4,256,896]{3,2,1,0:T(8,128)S(1)} fusion(bf16[2,4,256,896]{3,2,1,0:T(8,128)(2,1)} %collective-permute-done.1, bf16[2,4,2,256,896]{4,3,2,1,0:T(8,128)(2,1)} %bitcast.53, s32[]{:T(128)S(6)} %select_n.88, pred[]{:T(512)S(6)} %and.52), kind=kLoop, calls=%fused_computation.1 | loop fusion | flops 7340032 | bytes 14680069 | tf_op jit(solution)/shard_map/add | solution.py:33
  100.6 1.6 select_bitcast_fusion.2
  102.2 2.4 %collective-permute-start.4 = (bf16[2,256,896]{2,1,0:T(8,128)(2,1)}, bf16[2,256,896]{2,1,0:T(8,128)(2,1)}, u32[]{:S(2)}, u32[]{:S(2)}) collective-permute-start(bf16[2,256,896]{2,1,0:T(8,128)(2,1)} %get-tuple-element.70), channel_id=1, source_target_pairs={{0,96},{32,0},{64,32},{96,64},{1,97},{33,1},{65,33},{97,65},{2,98}... | collective-permute-start | bytes 2752520 | tf_op jit(solution)/shard_map/ppermute | solution.py:19
  104.6 0.6 collective-permute-start.3
  105.2 0.6 collective-permute-start.2
  105.8 5.9 %fusion.11 = (bf16[512,896]{0,1:T(8,128)(2,1)}, bf16[512,896]{0,1:T(8,128)(2,1)}) fusion(bf16[512,896]{0,1:T(8,128)(2,1)S(1)} %copy-done.8, bf16[512,896]{0,1:T(8,128)(2,1)S(1)} %copy-done.6, bf16[896,4096]{1,0:T(8,128)(2,1)S(1)} %bitcast.51, bf16[512,4096]{1,0:T(8,128)(2,1)S(1)} %copy-done.12), kind=kOutput, calls=%fused_computation.23 | convolution fusion | flops 3764977664 | bytes 15204352 | tf_op jit(solution)/shard_map/dot_general | solution.py:64
  111.6 2.3 %copy.22 = bf16[512,896]{1,0:T(8,128)(2,1)} copy(bf16[512,896]{0,1:T(8,128)(2,1)} %get-tuple-element.73) | data formatting | bytes 1835008
  114.0 1.3 copy.23
  115.2 17.8 %reduce-scatter.2.cloned.1.call-done = bf16[64,4096]{1,0:T(8,128)(2,1)} async-done(((bf16[512,4096]{1,0:T(8,128)(2,1)}), bf16[64,4096]{1,0:T(8,128)(2,1)}) %reduce-scatter.2.cloned.1.call-update) | async-done | bytes 524304 | tf_op jit(solution)/shard_map/reduce_scatter | solution.py:55
  133.0 1.0 constant_dynamic-slice_fusion
  134.0 2.8 %collective-permute-start = (bf16[32,4096]{1,0:T(8,128)(2,1)S(1)}, bf16[32,4096]{1,0:T(8,128)(2,1)S(1)}, u32[]{:S(2)}, u32[]{:S(2)}) collective-permute-start(bf16[32,4096]{1,0:T(8,128)(2,1)S(1)} %constant_dynamic-slice_fusion), channel_id=1, source_target_pairs={{0,1},{1,0},{2,3},{3,2},{4,5},{5,4},{6,7},{7,6},{8,9},{9,8},{10,11... | collective-permute-start | bytes 786440 | tf_op jit(solution)/shard_map/ppermute | solution.py:19
  136.9 11.5 %collective-permute-done.2 = bf16[2,256,896]{2,1,0:T(8,128)(2,1)} collective-permute-done((bf16[2,256,896]{2,1,0:T(8,128)(2,1)}, bf16[2,256,896]{2,1,0:T(8,128)(2,1)}, u32[]{:S(2)}, u32[]{:S(2)}) %collective-permute-start.2) | collective-permute-done | bytes 917536 | tf_op jit(solution)/shard_map/ppermute | solution.py:19
  148.4 2.8 %fusion.13 = f32[2,256,896]{2,1,0:T(8,128)S(1)} fusion(s32[]{:T(128)S(6)} %select_n.60, bf16[2,256,896]{2,1,0:T(8,128)(2,1)} %collective-permute-done.4, bf16[2,256,896]{2,1,0:T(8,128)(2,1)} %collective-permute-done.3, bf16[2,256,896]{2,1,0:T(8,128)(2,1)} %collective-permute-done.2, pred[]{:T(512)S(6)} %and.50, f32[2,4,256,896]{3,2,1,0:T(8,128)} %copy-done), kind=kLoop, calls=%fused_computation.26 | loop fusion | flops 3211264 | bytes 6422533 | tf_op jit(solution)/shard_map/add | solution.py:40
  151.1 0.1 fusion.17
  151.2 1.3 collective-permute-start.5
  152.5 0.8 add_convert_fusion
  153.3 9.6 %collective-permute-done.5 = bf16[256,896]{1,0:T(8,128)(2,1)S(1)} collective-permute-done((bf16[256,896]{1,0:T(8,128)(2,1)S(1)}, bf16[256,896]{1,0:T(8,128)(2,1)S(1)}, u32[]{:S(2)}, u32[]{:S(2)}) %collective-permute-start.5) | collective-permute-done | bytes 458784 | tf_op jit(solution)/shard_map/ppermute | solution.py:19
  162.9 0.1 fusion.15
  163.0 1.0 copy.24
  (36 shorter events, 0.2 us)
Async XLA Ops:
  7.2 12.3 %copy-start.3 = (bf16[512,896]{1,0:T(8,128)(2,1)S(1)}, bf16[512,896]{1,0:T(8,128)(2,1)}, u32[]{:S(2)}) copy-start(bf16[512,896]{1,0:T(8,128)(2,1)} %param.10) | copy-start | bytes 2752516
  7.2 13.6 %copy-start.4 = (bf16[512,896]{1,0:T(8,128)(2,1)S(1)}, bf16[512,896]{1,0:T(8,128)(2,1)}, u32[]{:S(2)}) copy-start(bf16[512,896]{1,0:T(8,128)(2,1)} %param.9) | copy-start | bytes 2752516
  7.2 69.3 %all-gather.2.cloned.1.call-start = ((), (), s32[]{:S(2)}) async-start(), calls=%async_computation.2 | async-start | bytes 4718592 | tf_op jit(solution)/shard_map/all_gather | solution.py:63
  19.4 2.6 %copy-start.10 = (s32[28,4096]{1,0:T(8,128)S(1)}, s32[28,4096]{1,0:T(8,128)}, u32[]{:S(2)}) copy-start(s32[28,4096]{1,0:T(8,128)} %param.13) | copy-start | bytes 1376260
  19.4 113.6 %reduce-scatter.2.cloned.1.call-start = ((), (), s32[]{:S(2)}) async-start(), calls=%async_computation.1 | async-start | bytes 4718592 | tf_op jit(solution)/shard_map/reduce_scatter | solution.py:55
  25.8 2.9 %copy-start.1 = (bf16[896,4096]{1,0:T(8,128)(2,1)}, bf16[896,4096]{1,0:T(8,128)(2,1)S(1)}, u32[]{:S(2)}) copy-start(bf16[896,4096]{1,0:T(8,128)(2,1)S(1)} %bitcast_multiply_fusion) | copy-start | bytes 22020100
  36.9 39.6 %copy-start.5 = (bf16[512,896]{0,1:T(8,128)(2,1)S(1)}, bf16[512,896]{0,1:T(8,128)(2,1)}, u32[]{:S(2)}) copy-start(bf16[512,896]{0,1:T(8,128)(2,1)} %copy.17) | copy-start | bytes 2752516
  36.9 39.6 %copy-start.7 = (bf16[512,896]{0,1:T(8,128)(2,1)S(1)}, bf16[512,896]{0,1:T(8,128)(2,1)}, u32[]{:S(2)}) copy-start(bf16[512,896]{0,1:T(8,128)(2,1)} %copy.16) | copy-start | bytes 2752516
  83.7 3.0 %copy-start.2 = (bf16[896,4096]{0,1:T(8,128)(2,1)}, bf16[896,4096]{0,1:T(8,128)(2,1)S(1)}, u32[]{:S(2)}) copy-start(bf16[896,4096]{0,1:T(8,128)(2,1)S(1)} %convolution_convert_fusion) | copy-start | bytes 22020100
  86.7 19.1 %slice-start = ((s8[7340032]{0:T(1024)(128)(4,1)}), s8[3145728]{0:T(1024)(128)(4,1)S(1)}, s32[]{:S(2)}) async-start(s8[7340032]{0:T(1024)(128)(4,1)} %bitcast.50), calls=%async_computation.3 | async-start | bytes 6291456
  89.0 7.2 %collective-permute-start.1 = (bf16[2,4,256,896]{3,2,1,0:T(8,128)(2,1)}, bf16[2,4,256,896]{3,2,1,0:T(8,128)(2,1)}, u32[]{:S(2)}, u32[]{:S(2)}) collective-permute-start(bf16[2,4,256,896]{3,2,1,0:T(8,128)(2,1)} %fusion), channel_id=1, source_target_pairs={{0,16},{16,0},{1,17},{17,1},{2,18},{18,2},{3,19},{19,3},{4,20},{20... | collective-permute-start | bytes 11010056 | tf_op jit(solution)/shard_map/ppermute | solution.py:19
  89.8 15.9 %slice-start.1 = ((s8[7340032]{0:T(1024)(128)(4,1)}), s8[4194304]{0:T(1024)(128)(4,1)S(1)}, s32[]{:S(2)}) async-start(s8[7340032]{0:T(1024)(128)(4,1)} %bitcast.50), calls=%async_computation.4 | async-start | bytes 8388608
  96.2 9.6 %copy-start.12 = (bf16[512,4096]{1,0:T(8,128)(2,1)S(1)}, bf16[512,4096]{1,0:T(8,128)(2,1)}, u32[]{:S(2)}) copy-start(bf16[512,4096]{1,0:T(8,128)(2,1)} %all-gather.2.cloned.1.call-done) | copy-start | bytes 12582916
  100.6 11.1 %copy-start = (f32[2,4,256,896]{3,2,1,0:T(8,128)}, f32[2,4,256,896]{3,2,1,0:T(8,128)S(1)}, u32[]{:S(2)}) copy-start(f32[2,4,256,896]{3,2,1,0:T(8,128)S(1)} %convert_add_fusion) | copy-start | bytes 22020100
  100.6 5.2 %copy-start.6 = (bf16[512,896]{0,1:T(8,128)(2,1)S(1)}, bf16[512,896]{0,1:T(8,128)(2,1)}, u32[]{:S(2)}) copy-start(bf16[512,896]{0,1:T(8,128)(2,1)} %copy.17) | copy-start | bytes 2752516
  100.6 5.2 %copy-start.8 = (bf16[512,896]{0,1:T(8,128)(2,1)S(1)}, bf16[512,896]{0,1:T(8,128)(2,1)}, u32[]{:S(2)}) copy-start(bf16[512,896]{0,1:T(8,128)(2,1)} %copy.16) | copy-start | bytes 2752516
  102.2 34.6 %collective-permute-start.4 = (bf16[2,256,896]{2,1,0:T(8,128)(2,1)}, bf16[2,256,896]{2,1,0:T(8,128)(2,1)}, u32[]{:S(2)}, u32[]{:S(2)}) collective-permute-start(bf16[2,256,896]{2,1,0:T(8,128)(2,1)} %get-tuple-element.70), channel_id=1, source_target_pairs={{0,96},{32,0},{64,32},{96,64},{1,97},{33,1},{65,33},{97,65},{2,98}... | collective-permute-start | bytes 2752520 | tf_op jit(solution)/shard_map/ppermute | solution.py:19
  104.6 32.2 %collective-permute-start.3 = (bf16[2,256,896]{2,1,0:T(8,128)(2,1)}, bf16[2,256,896]{2,1,0:T(8,128)(2,1)}, u32[]{:S(2)}, u32[]{:S(2)}) collective-permute-start(bf16[2,256,896]{2,1,0:T(8,128)(2,1)} %get-tuple-element.71), channel_id=1, source_target_pairs={{0,64},{32,96},{64,0},{96,32},{1,65},{33,97},{65,1},{97,33},{2,66}... | collective-permute-start | bytes 2752520 | tf_op jit(solution)/shard_map/ppermute | solution.py:19
  105.2 43.2 %collective-permute-start.2 = (bf16[2,256,896]{2,1,0:T(8,128)(2,1)}, bf16[2,256,896]{2,1,0:T(8,128)(2,1)}, u32[]{:S(2)}, u32[]{:S(2)}) collective-permute-start(bf16[2,256,896]{2,1,0:T(8,128)(2,1)} %get-tuple-element.69), channel_id=1, source_target_pairs={{0,32},{32,64},{64,96},{96,0},{1,33},{33,65},{65,97},{97,1},{2,34}... | collective-permute-start | bytes 2752520 | tf_op jit(solution)/shard_map/ppermute | solution.py:19
  111.6 2.3 %copy-start.9 = (bf16[512,896]{0,1:T(8,128)(2,1)S(1)}, bf16[512,896]{0,1:T(8,128)(2,1)}, u32[]{:S(2)}) copy-start(bf16[512,896]{0,1:T(8,128)(2,1)} %get-tuple-element.72) | copy-start | bytes 2752516
  134.0 18.5 %copy-start.11 = (bf16[64,4096]{1,0:T(8,128)(2,1)S(1)}, bf16[64,4096]{1,0:T(8,128)(2,1)}, u32[]{:S(2)}) copy-start(bf16[64,4096]{1,0:T(8,128)(2,1)} %reduce-scatter.2.cloned.1.call-done) | copy-start | bytes 1572868
  134.0 18.5 %collective-permute-start = (bf16[32,4096]{1,0:T(8,128)(2,1)S(1)}, bf16[32,4096]{1,0:T(8,128)(2,1)S(1)}, u32[]{:S(2)}, u32[]{:S(2)}) collective-permute-start(bf16[32,4096]{1,0:T(8,128)(2,1)S(1)} %constant_dynamic-slice_fusion), channel_id=1, source_target_pairs={{0,1},{1,0},{2,3},{3,2},{4,5},{5,4},{6,7},{7,6},{8,9},{9,8},{10,11... | collective-permute-start | bytes 786440 | tf_op jit(solution)/shard_map/ppermute | solution.py:19
  151.2 11.7 %collective-permute-start.5 = (bf16[256,896]{1,0:T(8,128)(2,1)S(1)}, bf16[256,896]{1,0:T(8,128)(2,1)S(1)}, u32[]{:S(2)}, u32[]{:S(2)}) collective-permute-start(bf16[256,896]{1,0:T(8,128)(2,1)S(1)} %fusion.17), channel_id=1, source_target_pairs={{0,128},{128,0},{1,129},{129,1},{2,130},{130,2},{3,131},{131,3},{4... | collective-permute-start | bytes 1376264 | tf_op jit(solution)/shard_map/ppermute | solution.py:19
Sparse Core Ops, SparseCore 0:
  19.5 56.8 all-gather.1
  79.0 54.0 reduce-scatter.1

commit v4 on v3

--- a/solution.py
+++ b/solution.py
@@ -20,6 +20,14 @@
 
 
 def weight_gradient(hidden, cotangent):
+    lanes = hidden.shape[1] // 128
+    cut = 128 * (lanes // 2)
+    return jnp.concatenate(
+        [reduce_chunk(hidden[:, :cut], cotangent), reduce_chunk(hidden[:, cut:], cotangent)], axis=0
+    )
+
+
+def reduce_chunk(hidden, cotangent):
     n_x = cotangent.shape[1] // 1024
     width = 256
     partial = lax.dot_general(

time: 171 us -> 194 us (1.13)
  waiting for transfers between devices: 84.9 us -> 99.2 us
  other arithmetic: 15.8 us -> 20.9 us
  starting transfers between devices: 8.59 us -> 11.3 us
  matrix products: 21.2 us -> 23.9 us
  local copies, waits for them, and re-layouts: 14.1 us -> 12 us
    ppermute x6 -> x11, waiting for transfers between devices: 27.5 us -> 50.9 us  [exchange(): return lax.ppermute(value, axis, perm)]
    reduce_scatter x1, waiting for transfers between devices: 17.8 us -> 0.01 us  [per_device(): out = lax.psum_scatter(partial_out, 'tz', scatter_dimension=0, tiled=True)]
    all_gather x1, waiting for transfers between devices: 39.5 us -> 48.2 us  [per_device(): cotangent = lax.all_gather(cotangent, 'tz', axis=0, tiled=True)]
    dot_general x1, matrix products: 5.85 us -> 10.4 us  [per_device(): lax.dot_general(cotangent, weight, (((1,), (1,)), ((), ())), preferred_el...]
    mul x1, other arithmetic: 3.68 us -> 6.63 us  [decode(): codes.reshape(scales.shape[0], 32, codes.shape[1]) * factor[:, None, :]]
    ppermute x6 -> x11, starting transfers between devices: 8.51 us -> 11.2 us  [exchange(): return lax.ppermute(value, axis, perm)]
    unnamed x35 -> x33, local copies, waits for them, and re-layouts: 13.1 us -> 11 us
    add x2 -> x4, other arithmetic: 7.12 us -> 8.88 us  [the longest x2 5.59 us: reduce_chunk(): total = mine.astype(jnp.float32) + arrived.astype(jnp.float32)]
  transfers between devices with their start and end apart: 8 -> 13, of which waited for: 5 -> 10; matrix products, arithmetic and copies ran while one was open for 26% -> 17% of each run, Pallas kernels for 0% -> 0%
where the time goes in v4:
time: 194 us
  waiting for transfers between devices  99.2 us (51%)
  matrix products  23.9 us (12%)
  other arithmetic  20.9 us (11%)
  between operations  14.3 us (7%)
  blocking collectives  12.1 us (6%)
  local copies, waits for them, and re-layouts  12 us (6%)
  starting transfers between devices  11.3 us (6%)
    ppermute x11, waiting for transfers between devices, exchange(): return lax.ppermute(value, axis, perm)  50.9 us
    all_gather x1, waiting for transfers between devices, per_device(): cotangent = lax.all_gather(cotangent, 'tz', axis=0, tiled=True)  48.2 us
    all_gather x1, blocking collectives, per_device(): cotangent = lax.all_gather(grad_out, 'ty', axis=0, tiled=True)  12.1 us
    ppermute x11, starting transfers between devices, exchange(): return lax.ppermute(value, axis, perm)  11.2 us
    unnamed x33, local copies, waits for them, and re-layouts  11 us
    dot_general x1, matrix products, per_device(): lax.dot_general(cotangent, weight, (((1,), (1,)), ((), ())), preferred_el...  10.4 us
    dot_general x2, matrix products, reduce_chunk(): lax.dot_general(cotangent, hidden, (((0,), (0,)), ((), ())), preferred_el...  7.14 us
    mul x1, other arithmetic, decode(): codes.reshape(scales.shape[0], 32, codes.shape[1]) * factor[:, None, :]  6.63 us
  transfers between devices with their start and end apart: 13, of which 10 were waited for; matrix products, arithmetic and copies ran while one was open for 17% of the time, Pallas kernels for 0%

profile of v4, /device:TPU:1, one launch (start us, length us, event | category | flops | bytes accessed | tf_op | source)
XLA Modules:
  0.0 193.7 jit_solution(1032878641653802069)
XLA Ops:
  7.2 12.1 %all_gather.6 = bf16[64,4096]{1,0:T(8,128)(2,1)} all-gather(bf16[32,4096]{1,0:T(8,128)(2,1)} %param.15), channel_id=1, replica_groups=mesh['dy'=2,'dx'=4,'dc'=2,'tz'=8,'ty'=2] {'ty'}, dimensions={0}, use_global_device_ids=true | all-gather | bytes 786432 | tf_op jit(solution)/shard_map/all_gather | solution.py:70
  19.4 1.5 copy.18
  21.6 6.6 %bitcast_multiply_fusion = bf16[896,4096]{1,0:T(8,128)(2,1)} fusion(bf16[896,4096]{1,0:T(8,128)(2,1)} %param.16, bf16[28,4096]{1,0:T(8,128)(2,1)S(1)} %exponential_convert_fusion), kind=kLoop, calls=%fused_computation | loop fusion | flops 3670016 | bytes 14909440 | tf_op jit(solution)/shard_map/mul | solution.py:13
  28.2 48.2 %all-gather.2.cloned.1.call-done = bf16[512,4096]{1,0:T(8,128)(2,1)} async-done(((bf16[64,4096]{1,0:T(8,128)(2,1)}), bf16[512,4096]{1,0:T(8,128)(2,1)}) %all-gather.2.cloned.1.call-update) | async-done | bytes 4194320 | tf_op jit(solution)/shard_map/all_gather | solution.py:71
  76.5 10.4 %fusion.11 = (bf16[512,896]{0,1:T(8,128)(2,1)}, bf16[512,896]{0,1:T(8,128)(2,1)}, bf16[512,896]{0,1:T(8,128)(2,1)S(1)}) fusion(bf16[512,896]{0,1:T(8,128)(2,1)S(1)} %copy.18, bf16[512,896]{0,1:T(8,128)(2,1)S(1)} %copy.19, bf16[896,4096]{1,0:T(8,128)(2,1)} %bitcast_multiply_fusion, bf16[512,4096]{1,0:T(8,128)(2,1)} %all-gather.2.cloned.1.call-done), kind=kOutput, calls=%fused_computation.25 | convolution fusion | flops 3766353920 | bytes 16121856 | tf_op jit(solution)/shard_map/dot_general | solution.py:72
  86.9 6.3 %convolution_convert_fusion = bf16[512,4096]{1,0:T(8,128)(2,1)} fusion(bf16[512,896]{0,1:T(8,128)(2,1)S(1)} %get-tuple-element.131, bf16[896,4096]{1,0:T(8,128)(2,1)S(1)} %copy-done.1), kind=kOutput, calls=%fused_computation.1 | convolution fusion | flops 3760193536 | bytes 12451840 | tf_op jit(solution)/shard_map/dot_general | solution.py:62
  93.2 4.7 %convolution_convert_fusion.2 = bf16[384,4096]{0,1:T(8,128)(2,1)S(1)} fusion(bf16[512,4096]{1,0:T(8,128)(2,1)} %all-gather.2.cloned.1.call-done, bf16[512,896]{0,1:T(8,128)(2,1)S(1)} %get-tuple-element.131), kind=kOutput, calls=%fused_computation.3 | convolution fusion | flops 1612185600 | bytes 7733248 | tf_op jit(solution)/shard_map/dot_general | solution.py:33
  98.2 1.4 copy-done.3
  100.5 2.4 %convolution_convert_fusion.1 = bf16[512,4096]{0,1:T(8,128)(2,1)S(1)} fusion(bf16[512,4096]{1,0:T(8,128)(2,1)S(1)} %copy-done.11, bf16[512,896]{0,1:T(8,128)(2,1)S(1)} %copy-done.13), kind=kOutput, calls=%fused_computation.2 | convolution fusion | flops 2149580800 | bytes 8912896 | tf_op jit(solution)/shard_map/dot_general | solution.py:33
  102.9 2.0 %copy-done.2 = bf16[512,4096]{0,1:T(8,128)(2,1)} copy-done((bf16[512,4096]{0,1:T(8,128)(2,1)}, bf16[512,4096]{0,1:T(8,128)(2,1)S(1)}, u32[]{:S(2)}) %copy-start.2) | copy-done | bytes 4194328
  104.9 1.6 fusion
  106.7 2.3 %convert_add_fusion.1 = f32[2,4,256,384]{3,2,1,0:T(8,128)S(1)} fusion(bf16[2,4,256,384]{3,2,1,0:T(8,128)(2,1)} %collective-permute-done.1, bf16[2,4,2,256,384]{4,3,2,1,0:T(8,128)(2,1)} %bitcast.96, s32[]{:T(128)S(6)} %select_n.147, pred[]{:T(512)S(6)} %and.75), kind=kLoop, calls=%fused_computation.9 | loop fusion | flops 3145728 | bytes 6291461 | tf_op jit(solution)/shard_map/add | solution.py:41
  109.0 1.1 select_bitcast_fusion.5
  110.1 2.4 %collective-permute-start.4 = (bf16[2,256,384]{2,1,0:T(8,128)(2,1)}, bf16[2,256,384]{2,1,0:T(8,128)(2,1)S(1)}, u32[]{:S(2)}, u32[]{:S(2)}) collective-permute-start(bf16[2,256,384]{2,1,0:T(8,128)(2,1)} %get-tuple-element.133), channel_id=1, source_target_pairs={{0,96},{32,0},{64,32},{96,64},{1,97},{33,1},{65,33},{97,65},{2,98}... | collective-permute-start | bytes 1179656 | tf_op jit(solution)/shard_map/ppermute | solution.py:19
  113.7 8.0 %collective-permute-done.4 = bf16[2,256,384]{2,1,0:T(8,128)(2,1)S(1)} collective-permute-done((bf16[2,256,384]{2,1,0:T(8,128)(2,1)}, bf16[2,256,384]{2,1,0:T(8,128)(2,1)S(1)}, u32[]{:S(2)}, u32[]{:S(2)}) %collective-permute-start.4) | collective-permute-done | bytes 393248 | tf_op jit(solution)/shard_map/ppermute | solution.py:19
  121.6 2.8 %collective-permute-done.3 = bf16[2,256,384]{2,1,0:T(8,128)(2,1)} collective-permute-done((bf16[2,256,384]{2,1,0:T(8,128)(2,1)}, bf16[2,256,384]{2,1,0:T(8,128)(2,1)}, u32[]{:S(2)}, u32[]{:S(2)}) %collective-permute-start.3) | collective-permute-done | bytes 393248 | tf_op jit(solution)/shard_map/ppermute | solution.py:19
  124.5 9.3 %collective-permute-done.2 = bf16[2,256,384]{2,1,0:T(8,128)(2,1)} collective-permute-done((bf16[2,256,384]{2,1,0:T(8,128)(2,1)}, bf16[2,256,384]{2,1,0:T(8,128)(2,1)}, u32[]{:S(2)}, u32[]{:S(2)}) %collective-permute-start.2) | collective-permute-done | bytes 393248 | tf_op jit(solution)/shard_map/ppermute | solution.py:19
  133.8 1.3 fusion.17
  135.1 3.3 %convert_add_fusion = f32[2,4,256,512]{3,2,1,0:T(8,128)S(1)} fusion(bf16[2,4,256,512]{3,2,1,0:T(8,128)(2,1)} %collective-permute-done.6, bf16[2,4,2,256,512]{4,3,2,1,0:T(8,128)(2,1)} %bitcast.94, s32[]{:T(128)S(6)} %select_n.147, pred[]{:T(512)S(6)} %and.75), kind=kLoop, calls=%fused_computation.4 | loop fusion | flops 4194304 | bytes 8388613 | tf_op jit(solution)/shard_map/add | solution.py:41
  138.4 2.0 %copy-done = f32[2,4,256,512]{3,2,1,0:T(8,128)} copy-done((f32[2,4,256,512]{3,2,1,0:T(8,128)}, f32[2,4,256,512]{3,2,1,0:T(8,128)S(1)}, u32[]{:S(2)}) %copy-start) | copy-done | bytes 4194328
  140.4 1.4 select_bitcast_fusion.2
  143.4 1.3 collective-permute-start.5
  144.7 1.3 copy.28
  145.9 1.3 copy.29
  147.2 1.5 collective-permute-done.5
  148.8 6.4 %collective-permute-done.9 = bf16[2,256,512]{2,1,0:T(8,128)(2,1)} collective-permute-done((bf16[2,256,512]{2,1,0:T(8,128)(2,1)}, bf16[2,256,512]{2,1,0:T(8,128)(2,1)}, u32[]{:S(2)}, u32[]{:S(2)}) %collective-permute-start.9) | collective-permute-done | bytes 524320 | tf_op jit(solution)/shard_map/ppermute | solution.py:19
  156.1 12.7 %collective-permute-done.7 = bf16[2,256,512]{2,1,0:T(8,128)(2,1)} collective-permute-done((bf16[2,256,512]{2,1,0:T(8,128)(2,1)S(1)}, bf16[2,256,512]{2,1,0:T(8,128)(2,1)}, u32[]{:S(2)}, u32[]{:S(2)}) %collective-permute-start.7) | collective-permute-done | bytes 524320 | tf_op jit(solution)/shard_map/ppermute | solution.py:19
  168.7 2.0 %fusion.15 = f32[2,256,512]{2,1,0:T(8,128)S(1)} fusion(s32[]{:T(128)S(6)} %select_n.96, bf16[2,256,512]{2,1,0:T(8,128)(2,1)} %collective-permute-done.9, bf16[2,256,512]{2,1,0:T(8,128)(2,1)} %collective-permute-done.8, bf16[2,256,512]{2,1,0:T(8,128)(2,1)} %collective-permute-done.7, pred[]{:T(512)S(6)} %and.73, f32[2,4,256,512]{3,2,1,0:T(8,128)} %copy-done), kind=kLoop, calls=%fused_computation.32 | loop fusion | flops 1835008 | bytes 3670021 | tf_op jit(solution)/shard_map/add | solution.py:48
  170.8 1.3 collective-permute-start.10
  173.1 2.5 %collective-permute-start = (bf16[32,4096]{1,0:T(8,128)(2,1)S(1)}, bf16[32,4096]{1,0:T(8,128)(2,1)S(1)}, u32[]{:S(2)}, u32[]{:S(2)}) collective-permute-start(bf16[32,4096]{1,0:T(8,128)(2,1)S(1)} %constant_dynamic-slice_fusion), channel_id=1, source_target_pairs={{0,1},{1,0},{2,3},{3,2},{4,5},{5,4},{6,7},{7,6},{8,9},{9,8},{10,11... | collective-permute-start | bytes 786440 | tf_op jit(solution)/shard_map/ppermute | solution.py:19
  175.7 2.6 %collective-permute-done.10 = bf16[256,512]{1,0:T(8,128)(2,1)S(1)} collective-permute-done((bf16[256,512]{1,0:T(8,128)(2,1)S(1)}, bf16[256,512]{1,0:T(8,128)(2,1)S(1)}, u32[]{:S(2)}, u32[]{:S(2)}) %collective-permute-start.10) | collective-permute-done | bytes 262176 | tf_op jit(solution)/shard_map/ppermute | solution.py:19
  179.4 6.7 %collective-permute-done = bf16[32,4096]{1,0:T(8,128)(2,1)S(1)} collective-permute-done((bf16[32,4096]{1,0:T(8,128)(2,1)S(1)}, bf16[32,4096]{1,0:T(8,128)(2,1)S(1)}, u32[]{:S(2)}, u32[]{:S(2)}) %collective-permute-start) | collective-permute-done | bytes 262176 | tf_op jit(solution)/shard_map/ppermute | solution.py:19
  (51 shorter events, 8.6 us)
Async XLA Ops:
  7.2 13.7 %copy-start.6 = (bf16[512,896]{1,0:T(8,128)(2,1)S(1)}, bf16[512,896]{1,0:T(8,128)(2,1)}, u32[]{:S(2)}) copy-start(bf16[512,896]{1,0:T(8,128)(2,1)} %param.14) | copy-start | bytes 2752516
  7.2 14.3 %copy-start.9 = (s32[28,4096]{1,0:T(8,128)S(1)}, s32[28,4096]{1,0:T(8,128)}, u32[]{:S(2)}) copy-start(s32[28,4096]{1,0:T(8,128)} %param.17) | copy-start | bytes 1376260
  7.2 69.3 %all-gather.2.cloned.1.call-start = ((), (), s32[]{:S(2)}) async-start(), calls=%async_computation.2 | async-start | bytes 4718592 | tf_op jit(solution)/shard_map/all_gather | solution.py:71
  19.4 152.7 %reduce-scatter.2.cloned.1.call-start = ((), (), s32[]{:S(2)}) async-start(), calls=%async_computation.1 | async-start | bytes 4718592 | tf_op jit(solution)/shard_map/reduce_scatter | solution.py:63
  76.4 10.4 %copy-start.1 = (bf16[896,4096]{1,0:T(8,128)(2,1)S(1)}, bf16[896,4096]{1,0:T(8,128)(2,1)}, u32[]{:S(2)}) copy-start(bf16[896,4096]{1,0:T(8,128)(2,1)} %bitcast_multiply_fusion) | copy-start | bytes 22020100
  86.9 6.3 %copy-start.12 = (bf16[512,896]{0,1:T(8,128)(2,1)}, bf16[512,896]{0,1:T(8,128)(2,1)S(1)}, u32[]{:S(2)}) copy-start(bf16[512,896]{0,1:T(8,128)(2,1)S(1)} %get-tuple-element.131) | copy-start | bytes 2752516
  93.2 7.2 %copy-start.11 = (bf16[512,4096]{1,0:T(8,128)(2,1)S(1)}, bf16[512,4096]{1,0:T(8,128)(2,1)}, u32[]{:S(2)}) copy-start(bf16[512,4096]{1,0:T(8,128)(2,1)} %all-gather.2.cloned.1.call-done) | copy-start | bytes 12582916
  98.0 1.6 copy-start.3
  98.0 2.5 %copy-start.13 = (bf16[512,896]{0,1:T(8,128)(2,1)S(1)}, bf16[512,896]{0,1:T(8,128)(2,1)}, u32[]{:S(2)}) copy-start(bf16[512,896]{0,1:T(8,128)(2,1)} %copy-done.12) | copy-start | bytes 2752516
  99.6 7.1 %collective-permute-start.1 = (bf16[2,4,256,384]{3,2,1,0:T(8,128)(2,1)S(1)}, bf16[2,4,256,384]{3,2,1,0:T(8,128)(2,1)}, u32[]{:S(2)}, u32[]{:S(2)}) collective-permute-start(bf16[2,4,256,384]{3,2,1,0:T(8,128)(2,1)S(1)} %fusion.12), channel_id=1, source_target_pairs={{0,16},{16,0},{1,17},{17,1},{2,18},{18,2},{3,19},{19,3},{4,20},{20... | collective-permute-start | bytes 4718600 | tf_op jit(solution)/shard_map/ppermute | solution.py:19
  102.9 2.0 %copy-start.2 = (bf16[512,4096]{0,1:T(8,128)(2,1)}, bf16[512,4096]{0,1:T(8,128)(2,1)S(1)}, u32[]{:S(2)}) copy-start(bf16[512,4096]{0,1:T(8,128)(2,1)S(1)} %convolution_convert_fusion.1) | copy-start | bytes 12582916
  106.5 28.6 %collective-permute-start.6 = (bf16[2,4,256,512]{3,2,1,0:T(8,128)(2,1)}, bf16[2,4,256,512]{3,2,1,0:T(8,128)(2,1)}, u32[]{:S(2)}, u32[]{:S(2)}) collective-permute-start(bf16[2,4,256,512]{3,2,1,0:T(8,128)(2,1)} %fusion), channel_id=1, source_target_pairs={{0,16},{16,0},{1,17},{17,1},{2,18},{18,2},{3,19},{19,3},{4,20},{20... | collective-permute-start | bytes 6291464 | tf_op jit(solution)/shard_map/ppermute | solution.py:19
  110.1 11.5 %collective-permute-start.4 = (bf16[2,256,384]{2,1,0:T(8,128)(2,1)}, bf16[2,256,384]{2,1,0:T(8,128)(2,1)S(1)}, u32[]{:S(2)}, u32[]{:S(2)}) collective-permute-start(bf16[2,256,384]{2,1,0:T(8,128)(2,1)} %get-tuple-element.133), channel_id=1, source_target_pairs={{0,96},{32,0},{64,32},{96,64},{1,97},{33,1},{65,33},{97,65},{2,98}... | collective-permute-start | bytes 1179656 | tf_op jit(solution)/shard_map/ppermute | solution.py:19
  112.5 11.9 %collective-permute-start.3 = (bf16[2,256,384]{2,1,0:T(8,128)(2,1)}, bf16[2,256,384]{2,1,0:T(8,128)(2,1)}, u32[]{:S(2)}, u32[]{:S(2)}) collective-permute-start(bf16[2,256,384]{2,1,0:T(8,128)(2,1)} %get-tuple-element.134), channel_id=1, source_target_pairs={{0,64},{32,96},{64,0},{96,32},{1,65},{33,97},{65,1},{97,33},{2,66}... | collective-permute-start | bytes 1179656 | tf_op jit(solution)/shard_map/ppermute | solution.py:19
  113.1 20.7 %collective-permute-start.2 = (bf16[2,256,384]{2,1,0:T(8,128)(2,1)}, bf16[2,256,384]{2,1,0:T(8,128)(2,1)}, u32[]{:S(2)}, u32[]{:S(2)}) collective-permute-start(bf16[2,256,384]{2,1,0:T(8,128)(2,1)} %get-tuple-element.132), channel_id=1, source_target_pairs={{0,32},{32,64},{64,96},{96,0},{1,33},{33,65},{65,97},{97,1},{2,34}... | collective-permute-start | bytes 1179656 | tf_op jit(solution)/shard_map/ppermute | solution.py:19
  135.1 8.2 %copy-start.4 = (f32[2,256,384]{2,1,0:T(8,128)}, f32[2,256,384]{2,1,0:T(8,128)S(1)}, u32[]{:S(2)}) copy-start(f32[2,256,384]{2,1,0:T(8,128)S(1)} %fusion.17) | copy-start | bytes 2359300
  138.4 2.0 %copy-start = (f32[2,4,256,512]{3,2,1,0:T(8,128)}, f32[2,4,256,512]{3,2,1,0:T(8,128)S(1)}, u32[]{:S(2)}) copy-start(f32[2,4,256,512]{3,2,1,0:T(8,128)S(1)} %convert_add_fusion) | copy-start | bytes 12582916
  140.4 4.2 %copy-start.8 = (bf16[512,896]{0,1:T(8,128)(2,1)S(1)}, bf16[512,896]{0,1:T(8,128)(2,1)}, u32[]{:S(2)}) copy-start(bf16[512,896]{0,1:T(8,128)(2,1)} %get-tuple-element.127) | copy-start | bytes 2752516
  140.4 5.5 %copy-start.7 = (bf16[512,896]{0,1:T(8,128)(2,1)S(1)}, bf16[512,896]{0,1:T(8,128)(2,1)}, u32[]{:S(2)}) copy-start(bf16[512,896]{0,1:T(8,128)(2,1)} %get-tuple-element.126) | copy-start | bytes 2752516
  141.8 13.3 %collective-permute-start.9 = (bf16[2,256,512]{2,1,0:T(8,128)(2,1)}, bf16[2,256,512]{2,1,0:T(8,128)(2,1)}, u32[]{:S(2)}, u32[]{:S(2)}) collective-permute-start(bf16[2,256,512]{2,1,0:T(8,128)(2,1)} %get-tuple-element.129), channel_id=1, source_target_pairs={{0,96},{32,0},{64,32},{96,64},{1,97},{33,1},{65,33},{97,65},{2,98}... | collective-permute-start | bytes 1572872 | tf_op jit(solution)/shard_map/ppermute | solution.py:19
  141.8 14.2 %collective-permute-start.8 = (bf16[2,256,512]{2,1,0:T(8,128)(2,1)}, bf16[2,256,512]{2,1,0:T(8,128)(2,1)}, u32[]{:S(2)}, u32[]{:S(2)}) collective-permute-start(bf16[2,256,512]{2,1,0:T(8,128)(2,1)} %get-tuple-element.130), channel_id=1, source_target_pairs={{0,64},{32,96},{64,0},{96,32},{1,65},{33,97},{65,1},{97,33},{2,66}... | collective-permute-start | bytes 1572872 | tf_op jit(solution)/shard_map/ppermute | solution.py:19
  142.4 26.3 %collective-permute-start.7 = (bf16[2,256,512]{2,1,0:T(8,128)(2,1)S(1)}, bf16[2,256,512]{2,1,0:T(8,128)(2,1)}, u32[]{:S(2)}, u32[]{:S(2)}) collective-permute-start(bf16[2,256,512]{2,1,0:T(8,128)(2,1)S(1)} %get-tuple-element.128), channel_id=1, source_target_pairs={{0,32},{32,64},{64,96},{96,0},{1,33},{33,65},{65,97},{97,1},{2,34}... | collective-permute-start | bytes 1572872 | tf_op jit(solution)/shard_map/ppermute | solution.py:19
  143.4 5.4 %copy-start.5 = (f32[2,256,384]{2,1,0:T(8,128)S(1)}, f32[2,256,384]{2,1,0:T(8,128)}, u32[]{:S(2)}) copy-start(f32[2,256,384]{2,1,0:T(8,128)} %copy-done.4) | copy-start | bytes 2359300
  143.4 5.4 %collective-permute-start.5 = (bf16[256,384]{1,0:T(8,128)(2,1)S(1)}, bf16[256,384]{1,0:T(8,128)(2,1)S(1)}, u32[]{:S(2)}, u32[]{:S(2)}) collective-permute-start(bf16[256,384]{1,0:T(8,128)(2,1)S(1)} %fusion.27), channel_id=1, source_target_pairs={{0,128},{128,0},{1,129},{129,1},{2,130},{130,2},{3,131},{131,3},{4... | collective-permute-start | bytes 589832 | tf_op jit(solution)/shard_map/ppermute | solution.py:19
  170.8 7.5 %collective-permute-start.10 = (bf16[256,512]{1,0:T(8,128)(2,1)S(1)}, bf16[256,512]{1,0:T(8,128)(2,1)S(1)}, u32[]{:S(2)}, u32[]{:S(2)}) collective-permute-start(bf16[256,512]{1,0:T(8,128)(2,1)S(1)} %fusion.24), channel_id=1, source_target_pairs={{0,128},{128,0},{1,129},{129,1},{2,130},{130,2},{3,131},{131,3},{4... | collective-permute-start | bytes 786440 | tf_op jit(solution)/shard_map/ppermute | solution.py:19
  172.1 14.0 %copy-start.10 = (bf16[64,4096]{1,0:T(8,128)(2,1)S(1)}, bf16[64,4096]{1,0:T(8,128)(2,1)}, u32[]{:S(2)}) copy-start(bf16[64,4096]{1,0:T(8,128)(2,1)} %reduce-scatter.2.cloned.1.call-done) | copy-start | bytes 1572868
  173.1 12.9 %collective-permute-start = (bf16[32,4096]{1,0:T(8,128)(2,1)S(1)}, bf16[32,4096]{1,0:T(8,128)(2,1)S(1)}, u32[]{:S(2)}, u32[]{:S(2)}) collective-permute-start(bf16[32,4096]{1,0:T(8,128)(2,1)S(1)} %constant_dynamic-slice_fusion), channel_id=1, source_target_pairs={{0,1},{1,0},{2,3},{3,2},{4,5},{5,4},{6,7},{7,6},{8,9},{9,8},{10,11... | collective-permute-start | bytes 786440 | tf_op jit(solution)/shard_map/ppermute | solution.py:19
Sparse Core Ops, SparseCore 0:
  19.5 56.8 all-gather.1
  93.3 54.0 reduce-scatter.1

commit v5 on v3

--- a/solution.py
+++ b/solution.py
@@ -19,28 +19,33 @@
     return lax.ppermute(value, axis, perm)
 
 
-def weight_gradient(hidden, cotangent):
-    n_x = cotangent.shape[1] // 1024
+def half_sum(hidden, cotangent):
+    n_x = cotangent.shape[1] // 512
     width = 256
     partial = lax.dot_general(
         cotangent, hidden, (((0,), (0,)), ((), ())), preferred_element_type=jnp.float32
     ).astype(jnp.bfloat16)
     partial = with_layout_constraint(partial, Layout(major_to_minor=(0, 1)))
-    parts = partial.reshape(2, n_x, 2, width, partial.shape[1])
+    parts = partial.reshape(n_x, 2, width, partial.shape[1])
     dc = lax.axis_index("dc")
-    mine = jnp.take(parts, dc, axis=2)
-    arrived = exchange(jnp.take(parts, 1 - dc, axis=2), "dc", 2, 1)
+    mine = jnp.take(parts, dc, axis=1)
+    arrived = exchange(jnp.take(parts, 1 - dc, axis=1), "dc", 2, 1)
     total = mine.astype(jnp.float32) + arrived.astype(jnp.float32)
-    total = with_layout_constraint(total, Layout(major_to_minor=(0, 1, 2, 3)))
+    total = with_layout_constraint(total, Layout(major_to_minor=(0, 1, 2)))
     sent = total.astype(jnp.bfloat16)
     dx = lax.axis_index("dx")
-    acc = jnp.take(total, dx, axis=1)
+    acc = jnp.take(total, dx, axis=0)
     for shift in range(1, n_x):
-        block = jnp.take(sent, (dx + shift) % n_x, axis=1)
+        block = jnp.take(sent, (dx + shift) % n_x, axis=0)
         acc = acc + exchange(block, "dx", n_x, shift).astype(jnp.float32)
-    dy = lax.axis_index("dy")
-    sent = acc.astype(jnp.bfloat16)
-    acc = jnp.take(acc, dy, axis=0) + exchange(jnp.take(sent, 1 - dy, axis=0), "dy", 2, 1).astype(jnp.float32)
+    return acc
+
+
+def weight_gradient(hidden, halves):
+    sums = [half_sum(hidden, cot) for cot in halves]
+    to_lo = lax.ppermute(sums[0].astype(jnp.bfloat16), "dy", [(1, 0)]).astype(jnp.float32)
+    to_hi = lax.ppermute(sums[1].astype(jnp.bfloat16), "dy", [(0, 1)]).astype(jnp.float32)
+    acc = jnp.where(lax.axis_index("dy") == 0, sums[0] + to_lo, sums[1] + to_hi)
     acc = with_layout_constraint(acc.astype(jnp.bfloat16), Layout(major_to_minor=(0, 1)))
     return acc.T
 
@@ -59,12 +64,16 @@
         lax.dynamic_slice_in_dim(out, (1 - ty) * rows, rows, 0), "ty", 2, 1
     ).astype(jnp.float32)
     out = out.astype(jnp.bfloat16)
-    cotangent = lax.all_gather(grad_out, "ty", axis=0, tiled=True)
-    cotangent = lax.all_gather(cotangent, "tz", axis=0, tiled=True)
+    local = lax.all_gather(grad_out, "ty", axis=0, tiled=True)
+    half = local.shape[1] // 2
+    halves = [
+        lax.all_gather(local[:, h * half:(h + 1) * half], "tz", axis=0, tiled=True) for h in range(2)
+    ]
+    cotangent = jnp.concatenate(halves, axis=1)
     grad_hidden = lax.dot_general(
         cotangent, weight, (((1,), (1,)), ((), ())), preferred_element_type=jnp.float32
     )
-    grad_weight = weight_gradient(hidden, cotangent)
+    grad_weight = weight_gradient(hidden, halves)
     grad_gate = (
         grad_hidden * up_value * sigmoid_gate * (1.0 + gate_value * (1.0 - sigmoid_gate))
     ).astype(jnp.bfloat16)

time: 171 us -> 197 us (1.15)
  starting transfers between devices: 8.59 us -> 24.9 us
  other arithmetic: 15.8 us -> 24.1 us
  local copies, waits for them, and re-layouts: 14.1 us -> 7.3 us
  waiting for transfers between devices: 84.9 us -> 90 us
  matrix products: 21.2 us -> 25.3 us
  blocking collectives: 12.1 us -> 9.83 us
    reduce_scatter x1, waiting for transfers between devices: 17.8 us -> 0.01 us  [per_device(): out = lax.psum_scatter(partial_out, 'tz', scatter_dimension=0, tiled=True)]
    all_gather x1 -> x2, waiting for transfers between devices: 39.5 us -> 56.4 us  [per_device(): lax.all_gather(local[:, h * half:(h + 1) * half], 'tz', axis=0, tiled=True)]
    ppermute x6 -> x9, starting transfers between devices: 8.51 us -> 19.5 us  [exchange(): return lax.ppermute(value, axis, perm)]
    convert_element_type x0 -> x4, other arithmetic: none -> 10.8 us  [the longest x2 7.04 us: half_sum(): sent = total.astype(jnp.bfloat16)]
    unnamed x35 -> x21, local copies, waits for them, and re-layouts: 13.1 us -> 5.51 us
    add x2 -> x0, other arithmetic: 7.12 us -> none  [the longest x1 4.36 us: weight_gradient(): total = mine.astype(jnp.float32) + arrived.astype(jnp.float32)]
    ppermute x6 -> x9, waiting for transfers between devices: 27.5 us -> 32.9 us  [exchange(): return lax.ppermute(value, axis, perm)]
    ppermute x0 -> x2, starting transfers between devices: none -> 5.33 us  [the longest x1 4.05 us: weight_gradient(): lax.ppermute(sums[1].astype(jnp.bfloat16), 'dy', [(0, 1)])]
  transfers between devices with their start and end apart: 8 -> 14, of which waited for: 5 -> 7; matrix products, arithmetic and copies ran while one was open for 26% -> 25% of each run, Pallas kernels for 0% -> 0%
where the time goes in v5:
time: 197 us; the launch traced here: 195 us
  waiting for transfers between devices  90 us (46%)
  matrix products  25.3 us (13%)
  starting transfers between devices  24.9 us (13%)
  other arithmetic  24.1 us (12%)
  between operations  13.9 us (7%)
  blocking collectives  9.83 us (5%)
  local copies, waits for them, and re-layouts  7.3 us (4%)
    all_gather x2, waiting for transfers between devices, per_device(): lax.all_gather(local[:, h * half:(h + 1) * half], 'tz', axis=0, tiled=True)  56.4 us
    ppermute x9, waiting for transfers between devices, exchange(): return lax.ppermute(value, axis, perm)  32.9 us
    ppermute x9, starting transfers between devices, exchange(): return lax.ppermute(value, axis, perm)  19.5 us
    all_gather x1, blocking collectives, per_device(): local = lax.all_gather(grad_out, 'ty', axis=0, tiled=True)  9.83 us
    dot_general x1, matrix products, per_device(): lax.dot_general(cotangent, weight, (((1,), (1,)), ((), ())), preferred_el...  9.42 us
    dot_general x2, matrix products, half_sum(): lax.dot_general(cotangent, hidden, (((0,), (0,)), ((), ())), preferred_el...  8.15 us
    dot_general x1, matrix products, per_device(): jnp.dot(hidden, weight, preferred_element_type=jnp.float32)  7.73 us
    convert_element_type x2, other arithmetic, half_sum(): sent = total.astype(jnp.bfloat16)  7.04 us
  transfers between devices with their start and end apart: 14, of which 7 were waited for; matrix products, arithmetic and copies ran while one was open for 25% of the time, Pallas kernels for 0%

profile of v5, /device:TPU:1, one launch (start us, length us, event | category | flops | bytes accessed | tf_op | source)
XLA Modules:
  0.0 195.4 jit_solution(2466349899199527917)
XLA Ops:
  7.2 9.8 %all_gather.9 = bf16[64,4096]{1,0:T(8,128)(2,1)S(1)} all-gather(bf16[32,4096]{1,0:T(8,128)(2,1)} %param.13), channel_id=1, replica_groups=mesh['dy'=2,'dx'=4,'dc'=2,'tz'=8,'ty'=2] {'ty'}, dimensions={0}, use_global_device_ids=true | all-gather | bytes 786432 | tf_op jit(solution)/shard_map/all_gather | solution.py:67
  18.8 3.7 %bitcast_multiply_fusion = bf16[896,4096]{1,0:T(8,128)(2,1)S(1)} fusion(bf16[896,4096]{1,0:T(8,128)(2,1)} %param.14, bf16[28,4096]{1,0:T(8,128)(2,1)S(1)} %exponential_convert_fusion), kind=kLoop, calls=%fused_computation | loop fusion | flops 3670016 | bytes 14909440 | tf_op jit(solution)/shard_map/mul | solution.py:13
  22.5 2.9 %copy-done = bf16[896,4096]{1,0:T(8,128)(2,1)} copy-done((bf16[896,4096]{1,0:T(8,128)(2,1)}, bf16[896,4096]{1,0:T(8,128)(2,1)S(1)}, u32[]{:S(2)}) %copy-start) | copy-done | bytes 7340056
  25.4 7.7 %convolution_convert_fusion = bf16[512,4096]{1,0:T(8,128)(2,1)} fusion(bf16[896,4096]{1,0:T(8,128)(2,1)S(1)} %bitcast_multiply_fusion, bf16[512,896]{1,0:T(8,128)(2,1)} %param.12, bf16[512,896]{1,0:T(8,128)(2,1)} %param.11), kind=kOutput, calls=%fused_computation.1 | convolution fusion | flops 3763863552 | bytes 13369344 | tf_op jit(solution)/shard_map/dot_general | solution.py:59
  33.2 26.0 %all-gather.5.cloned.1.call-done = bf16[512,2048]{1,0:T(8,128)(2,1)} async-done(((bf16[64,2048]{1,0:T(8,128)(2,1)}), bf16[512,2048]{1,0:T(8,128)(2,1)}) %all-gather.5.cloned.1.call-update) | async-done | bytes 2097168 | tf_op jit(solution)/shard_map/all_gather | solution.py:70
  59.2 4.1 %convolution_convert_fusion.1 = bf16[896,2048]{0,1:T(8,128)(2,1)S(1)} fusion(bf16[512,2048]{1,0:T(8,128)(2,1)} %all-gather.5.cloned.1.call-done, bf16[512,896]{1,0:T(8,128)(2,1)S(1)} %copy-done.7, bf16[512,896]{1,0:T(8,128)(2,1)S(1)} %copy-done.9), kind=kOutput, calls=%fused_computation.8 | convolution fusion | flops 1884553216 | bytes 7602176 | tf_op jit(solution)/shard_map/dot_general | solution.py:25
  63.3 1.7 fusion.14
  65.8 5.0 %collective-permute-start.6 = (bf16[4,256,896]{2,1,0:T(8,128)(2,1)}, bf16[4,256,896]{2,1,0:T(8,128)(2,1)}, u32[]{:S(2)}, u32[]{:S(2)}) collective-permute-start(bf16[4,256,896]{2,1,0:T(8,128)(2,1)} %fusion.14), channel_id=1, source_target_pairs={{0,16},{16,0},{1,17},{17,1},{2,18},{18,2},{3,19},{19,3},{4,20},{20... | collective-permute-start | bytes 5505032 | tf_op jit(solution)/shard_map/ppermute | solution.py:19
  70.8 30.3 %all-gather.3.cloned.1.call-done = bf16[512,2048]{1,0:T(8,128)(2,1)} async-done(((bf16[64,2048]{1,0:T(8,128)(2,1)}), bf16[512,2048]{1,0:T(8,128)(2,1)}) %all-gather.3.cloned.1.call-update) | async-done | bytes 2097168 | tf_op jit(solution)/shard_map/all_gather | solution.py:70
  101.1 4.1 %convolution_convert_fusion.2 = bf16[896,2048]{0,1:T(8,128)(2,1)S(1)} fusion(bf16[512,2048]{1,0:T(8,128)(2,1)} %all-gather.3.cloned.1.call-done, bf16[512,896]{1,0:T(8,128)(2,1)S(1)} %copy-done.7, bf16[512,896]{1,0:T(8,128)(2,1)S(1)} %copy-done.9), kind=kOutput, calls=%fused_computation.9 | convolution fusion | flops 1884553216 | bytes 7602176 | tf_op jit(solution)/shard_map/dot_general | solution.py:25
  105.2 1.6 fusion.16
  107.6 4.9 %collective-permute-start.1 = (bf16[4,256,896]{2,1,0:T(8,128)(2,1)}, bf16[4,256,896]{2,1,0:T(8,128)(2,1)S(1)}, u32[]{:S(2)}, u32[]{:S(2)}) collective-permute-start(bf16[4,256,896]{2,1,0:T(8,128)(2,1)} %fusion.16), channel_id=1, source_target_pairs={{0,16},{16,0},{1,17},{17,1},{2,18},{18,2},{3,19},{19,3},{4,20},{20... | collective-permute-start | bytes 5505032 | tf_op jit(solution)/shard_map/ppermute | solution.py:19
  112.5 4.6 %fusion.30 = (bf16[4,256,896]{2,1,0:T(8,128)(2,1)S(1)}, f32[4,256,896]{2,1,0:T(8,128)}) fusion(bf16[4,256,896]{2,1,0:T(8,128)(2,1)} %collective-permute-done.6, bf16[4,2,256,896]{3,2,1,0:T(8,128)(2,1)} %bitcast.85, s32[]{:T(128)S(6)} %select_n.94, pred[]{:T(512)S(6)} %and.53), kind=kLoop, calls=%fused_computation.55 | loop fusion | flops 4587520 | bytes 9175045 | tf_op jit(solution)/shard_map/convert_element_type | solution.py:35
  117.1 1.1 select_bitcast_fusion.2
  118.2 2.4 %collective-permute-start.9 = (bf16[256,896]{1,0:T(8,128)(2,1)S(1)}, bf16[256,896]{1,0:T(8,128)(2,1)S(1)}, u32[]{:S(2)}, u32[]{:S(2)}) collective-permute-start(bf16[256,896]{1,0:T(8,128)(2,1)S(1)} %get-tuple-element.58), channel_id=1, source_target_pairs={{0,96},{32,0},{64,32},{96,64},{1,97},{33,1},{65,33},{97,65},{2,98}... | collective-permute-start | bytes 1376264 | tf_op jit(solution)/shard_map/ppermute | solution.py:19
  121.7 2.4 %fusion.29 = (bf16[4,256,896]{2,1,0:T(8,128)(2,1)S(1)}, f32[4,256,896]{2,1,0:T(8,128)}) fusion(bf16[4,256,896]{2,1,0:T(8,128)(2,1)S(1)} %collective-permute-done.1, bf16[4,2,256,896]{3,2,1,0:T(8,128)(2,1)S(1)} %bitcast.83, s32[]{:T(128)S(6)} %select_n.94, pred[]{:T(512)S(6)} %and.53), kind=kLoop, calls=%fused_computation.54 | loop fusion | flops 4587520 | bytes 9175045 | tf_op jit(solution)/shard_map/convert_element_type | solution.py:35
  124.1 1.1 select_bitcast_fusion.5
  125.2 2.1 %collective-permute-start.4 = (bf16[256,896]{1,0:T(8,128)(2,1)}, bf16[256,896]{1,0:T(8,128)(2,1)S(1)}, u32[]{:S(2)}, u32[]{:S(2)}) collective-permute-start(bf16[256,896]{1,0:T(8,128)(2,1)} %get-tuple-element.55), channel_id=1, source_target_pairs={{0,96},{32,0},{64,32},{96,64},{1,97},{33,1},{65,33},{97,65},{2,98}... | collective-permute-start | bytes 1376264 | tf_op jit(solution)/shard_map/ppermute | solution.py:19
  127.3 1.2 collective-permute-start.3
  128.5 11.5 %collective-permute-done.9 = bf16[256,896]{1,0:T(8,128)(2,1)S(1)} collective-permute-done((bf16[256,896]{1,0:T(8,128)(2,1)S(1)}, bf16[256,896]{1,0:T(8,128)(2,1)S(1)}, u32[]{:S(2)}, u32[]{:S(2)}) %collective-permute-start.9) | collective-permute-done | bytes 458784 | tf_op jit(solution)/shard_map/ppermute | solution.py:19
  140.0 5.3 %collective-permute-done.7 = bf16[256,896]{1,0:T(8,128)(2,1)S(1)} collective-permute-done((bf16[256,896]{1,0:T(8,128)(2,1)}, bf16[256,896]{1,0:T(8,128)(2,1)S(1)}, u32[]{:S(2)}, u32[]{:S(2)}) %collective-permute-start.7) | collective-permute-done | bytes 458784 | tf_op jit(solution)/shard_map/ppermute | solution.py:19
  145.3 1.6 fusion.25
  146.8 4.0 %collective-permute-start.10 = (bf16[256,896]{1,0:T(8,128)(2,1)S(1)}, bf16[256,896]{1,0:T(8,128)(2,1)}, u32[]{:S(2)}, u32[]{:S(2)}) collective-permute-start(bf16[256,896]{1,0:T(8,128)(2,1)S(1)} %fusion.25), channel_id=1, source_target_pairs={{0,128},{1,129},{2,130},{3,131},{4,132},{5,133},{6,134},{7,135},{8... | collective-permute-start | bytes 1376264 | tf_op jit(solution)/shard_map/ppermute | solution.py:47
  150.9 9.0 %collective-permute-done.4 = bf16[256,896]{1,0:T(8,128)(2,1)S(1)} collective-permute-done((bf16[256,896]{1,0:T(8,128)(2,1)}, bf16[256,896]{1,0:T(8,128)(2,1)S(1)}, u32[]{:S(2)}, u32[]{:S(2)}) %collective-permute-start.4) | collective-permute-done | bytes 458784 | tf_op jit(solution)/shard_map/ppermute | solution.py:19
  159.9 4.3 %collective-permute-done.2 = bf16[256,896]{1,0:T(8,128)(2,1)S(1)} collective-permute-done((bf16[256,896]{1,0:T(8,128)(2,1)}, bf16[256,896]{1,0:T(8,128)(2,1)S(1)}, u32[]{:S(2)}, u32[]{:S(2)}) %collective-permute-start.2) | collective-permute-done | bytes 458784 | tf_op jit(solution)/shard_map/ppermute | solution.py:19
  164.2 2.2 %fusion.24 = bf16[256,896]{1,0:T(8,128)(2,1)} fusion(bf16[256,896]{1,0:T(8,128)(2,1)S(1)} %collective-permute-done.4, bf16[256,896]{1,0:T(8,128)(2,1)S(1)} %collective-permute-done.3, bf16[256,896]{1,0:T(8,128)(2,1)S(1)} %collective-permute-done.2, f32[4,256,896]{2,1,0:T(8,128)} %get-tuple-element.49, s32[]{:T(128)S(6)} %select_n.98, pred[]{:T(512)S(6)} %and.55), kind=kLoop, calls=%fused_computation.52 | loop fusion | flops 1835008 | bytes 2752517 | tf_op jit(solution)/shard_map/convert_element_type | solution.py:46
  166.3 1.3 collective-permute-start.5
  167.7 9.4 %fusion.13 = (bf16[512,896]{1,0:T(8,128)(2,1)}, bf16[512,896]{1,0:T(8,128)(2,1)}) fusion(bf16[512,896]{1,0:T(8,128)(2,1)} %param.11, bf16[512,896]{1,0:T(8,128)(2,1)S(1)} %copy-done.8, bf16[896,4096]{1,0:T(8,128)(2,1)} %copy-done, bf16[512,2048]{1,0:T(8,128)(2,1)S(1)} %copy-done.5, bf16[512,2048]{1,0:T(8,128)(2,1)S(1)} %copy-done.6), kind=kOutput, calls=%fused_computation.25 | convolution fusion | flops 3773366272 | bytes 15204352 | tf_op jit(solution)/shard_map/dot_general | solution.py:73
  178.0 2.8 %collective-permute-start = (bf16[32,4096]{1,0:T(8,128)(2,1)S(1)}, bf16[32,4096]{1,0:T(8,128)(2,1)}, u32[]{:S(2)}, u32[]{:S(2)}) collective-permute-start(bf16[32,4096]{1,0:T(8,128)(2,1)S(1)} %constant_dynamic-slice_fusion), channel_id=1, source_target_pairs={{0,1},{1,0},{2,3},{3,2},{4,5},{5,4},{6,7},{7,6},{8,9},{9,8},{10,11... | collective-permute-start | bytes 786440 | tf_op jit(solution)/shard_map/ppermute | solution.py:19
  180.9 2.3 %fusion.22 = bf16[896,256]{0,1:T(8,128)(2,1)S(1)} fusion(bf16[256,896]{1,0:T(8,128)(2,1)} %collective-permute-done.10, bf16[256,896]{1,0:T(8,128)(2,1)} %collective-permute-done.5, pred[]{:T(512)S(6)} %eq.10, bf16[256,896]{1,0:T(8,128)(2,1)S(1)} %collective-permute-done.4, bf16[256,896]{1,0:T(8,128)(2,1)S(1)} %collective-permute-done.3, ...), kind=kLoop, calls=%fused_computation.43 | loop fusion | flops 4587520 | bytes 5963782 | tf_op jit(solution)/shard_map/transpose | solution.py:50
  184.2 2.9 %collective-permute-done = bf16[32,4096]{1,0:T(8,128)(2,1)} collective-permute-done((bf16[32,4096]{1,0:T(8,128)(2,1)S(1)}, bf16[32,4096]{1,0:T(8,128)(2,1)}, u32[]{:S(2)}, u32[]{:S(2)}) %collective-permute-start) | collective-permute-done | bytes 262176 | tf_op jit(solution)/shard_map/ppermute | solution.py:19
  187.1 1.8 add_convert_fusion
  (39 shorter events, 6.5 us)
Async XLA Ops:
  7.2 11.5 %copy-start.4 = (s32[28,4096]{1,0:T(8,128)S(1)}, s32[28,4096]{1,0:T(8,128)}, u32[]{:S(2)}) copy-start(s32[28,4096]{1,0:T(8,128)} %param.15) | copy-start | bytes 1376260
  7.2 52.1 %all-gather.5.cloned.1.call-start = ((), (), s32[]{:S(2)}) async-start(), calls=%async_computation.3 | async-start | bytes 2359296 | tf_op jit(solution)/shard_map/all_gather | solution.py:70
  17.9 83.2 %all-gather.3.cloned.1.call-start = ((), (), s32[]{:S(2)}) async-start(), calls=%async_computation.2 | async-start | bytes 2359296 | tf_op jit(solution)/shard_map/all_gather | solution.py:70
  18.7 158.4 %reduce-scatter.2.cloned.1.call-start = ((), (), s32[]{:S(2)}) async-start(), calls=%async_computation.1 | async-start | bytes 4718592 | tf_op jit(solution)/shard_map/reduce_scatter | solution.py:60
  22.5 2.9 %copy-start = (bf16[896,4096]{1,0:T(8,128)(2,1)}, bf16[896,4096]{1,0:T(8,128)(2,1)S(1)}, u32[]{:S(2)}) copy-start(bf16[896,4096]{1,0:T(8,128)(2,1)S(1)} %bitcast_multiply_fusion) | copy-start | bytes 22020100
  33.2 26.1 %copy-start.7 = (bf16[512,896]{1,0:T(8,128)(2,1)S(1)}, bf16[512,896]{1,0:T(8,128)(2,1)}, u32[]{:S(2)}) copy-start(bf16[512,896]{1,0:T(8,128)(2,1)} %param.12) | copy-start | bytes 2752516
  33.2 26.1 %copy-start.9 = (bf16[512,896]{1,0:T(8,128)(2,1)S(1)}, bf16[512,896]{1,0:T(8,128)(2,1)}, u32[]{:S(2)}) copy-start(bf16[512,896]{1,0:T(8,128)(2,1)} %param.11) | copy-start | bytes 2752516
  63.3 2.5 %copy-start.3 = (bf16[896,2048]{0,1:T(8,128)(2,1)}, bf16[896,2048]{0,1:T(8,128)(2,1)S(1)}, u32[]{:S(2)}) copy-start(bf16[896,2048]{0,1:T(8,128)(2,1)S(1)} %convolution_convert_fusion.1) | copy-start | bytes 11010052
  65.8 46.6 %collective-permute-start.6 = (bf16[4,256,896]{2,1,0:T(8,128)(2,1)}, bf16[4,256,896]{2,1,0:T(8,128)(2,1)}, u32[]{:S(2)}, u32[]{:S(2)}) collective-permute-start(bf16[4,256,896]{2,1,0:T(8,128)(2,1)} %fusion.14), channel_id=1, source_target_pairs={{0,16},{16,0},{1,17},{17,1},{2,18},{18,2},{3,19},{19,3},{4,20},{20... | collective-permute-start | bytes 5505032 | tf_op jit(solution)/shard_map/ppermute | solution.py:19
  105.2 2.4 %copy-start.1 = (bf16[896,2048]{0,1:T(8,128)(2,1)}, bf16[896,2048]{0,1:T(8,128)(2,1)S(1)}, u32[]{:S(2)}) copy-start(bf16[896,2048]{0,1:T(8,128)(2,1)S(1)} %convolution_convert_fusion.2) | copy-start | bytes 11010052
  107.6 14.1 %collective-permute-start.1 = (bf16[4,256,896]{2,1,0:T(8,128)(2,1)}, bf16[4,256,896]{2,1,0:T(8,128)(2,1)S(1)}, u32[]{:S(2)}, u32[]{:S(2)}) collective-permute-start(bf16[4,256,896]{2,1,0:T(8,128)(2,1)} %fusion.16), channel_id=1, source_target_pairs={{0,16},{16,0},{1,17},{17,1},{2,18},{18,2},{3,19},{19,3},{4,20},{20... | collective-permute-start | bytes 5505032 | tf_op jit(solution)/shard_map/ppermute | solution.py:19
  112.4 9.3 %copy-start.2 = (bf16[896,2048]{0,1:T(8,128)(2,1)S(1)}, bf16[896,2048]{0,1:T(8,128)(2,1)}, u32[]{:S(2)}) copy-start(bf16[896,2048]{0,1:T(8,128)(2,1)} %copy-done.1) | copy-start | bytes 11010052
  118.2 21.8 %collective-permute-start.9 = (bf16[256,896]{1,0:T(8,128)(2,1)S(1)}, bf16[256,896]{1,0:T(8,128)(2,1)S(1)}, u32[]{:S(2)}, u32[]{:S(2)}) collective-permute-start(bf16[256,896]{1,0:T(8,128)(2,1)S(1)} %get-tuple-element.58), channel_id=1, source_target_pairs={{0,96},{32,0},{64,32},{96,64},{1,97},{33,1},{65,33},{97,65},{2,98}... | collective-permute-start | bytes 1376264 | tf_op jit(solution)/shard_map/ppermute | solution.py:19
  120.6 19.4 %collective-permute-start.8 = (bf16[256,896]{1,0:T(8,128)(2,1)}, bf16[256,896]{1,0:T(8,128)(2,1)S(1)}, u32[]{:S(2)}, u32[]{:S(2)}) collective-permute-start(bf16[256,896]{1,0:T(8,128)(2,1)} %get-tuple-element.59), channel_id=1, source_target_pairs={{0,64},{32,96},{64,0},{96,32},{1,65},{33,97},{65,1},{97,33},{2,66}... | collective-permute-start | bytes 1376264 | tf_op jit(solution)/shard_map/ppermute | solution.py:19
  121.1 24.1 %collective-permute-start.7 = (bf16[256,896]{1,0:T(8,128)(2,1)}, bf16[256,896]{1,0:T(8,128)(2,1)S(1)}, u32[]{:S(2)}, u32[]{:S(2)}) collective-permute-start(bf16[256,896]{1,0:T(8,128)(2,1)} %get-tuple-element.57), channel_id=1, source_target_pairs={{0,32},{32,64},{64,96},{96,0},{1,33},{33,65},{65,97},{97,1},{2,34}... | collective-permute-start | bytes 1376264 | tf_op jit(solution)/shard_map/ppermute | solution.py:19
  125.2 34.7 %collective-permute-start.4 = (bf16[256,896]{1,0:T(8,128)(2,1)}, bf16[256,896]{1,0:T(8,128)(2,1)S(1)}, u32[]{:S(2)}, u32[]{:S(2)}) collective-permute-start(bf16[256,896]{1,0:T(8,128)(2,1)} %get-tuple-element.55), channel_id=1, source_target_pairs={{0,96},{32,0},{64,32},{96,64},{1,97},{33,1},{65,33},{97,65},{2,98}... | collective-permute-start | bytes 1376264 | tf_op jit(solution)/shard_map/ppermute | solution.py:19
  127.3 32.6 %collective-permute-start.3 = (bf16[256,896]{1,0:T(8,128)(2,1)}, bf16[256,896]{1,0:T(8,128)(2,1)S(1)}, u32[]{:S(2)}, u32[]{:S(2)}) collective-permute-start(bf16[256,896]{1,0:T(8,128)(2,1)} %get-tuple-element.56), channel_id=1, source_target_pairs={{0,64},{32,96},{64,0},{96,32},{1,65},{33,97},{65,1},{97,33},{2,66}... | collective-permute-start | bytes 1376264 | tf_op jit(solution)/shard_map/ppermute | solution.py:19
  140.0 24.2 %collective-permute-start.2 = (bf16[256,896]{1,0:T(8,128)(2,1)}, bf16[256,896]{1,0:T(8,128)(2,1)S(1)}, u32[]{:S(2)}, u32[]{:S(2)}) collective-permute-start(bf16[256,896]{1,0:T(8,128)(2,1)} %get-tuple-element.54), channel_id=1, source_target_pairs={{0,32},{32,64},{64,96},{96,0},{1,33},{33,65},{65,97},{97,1},{2,34}... | collective-permute-start | bytes 1376264 | tf_op jit(solution)/shard_map/ppermute | solution.py:19
  145.3 22.4 %copy-start.6 = (bf16[512,2048]{1,0:T(8,128)(2,1)S(1)}, bf16[512,2048]{1,0:T(8,128)(2,1)}, u32[]{:S(2)}) copy-start(bf16[512,2048]{1,0:T(8,128)(2,1)} %all-gather.3.cloned.1.call-done) | copy-start | bytes 6291460
  145.3 22.4 %copy-start.8 = (bf16[512,896]{1,0:T(8,128)(2,1)S(1)}, bf16[512,896]{1,0:T(8,128)(2,1)}, u32[]{:S(2)}) copy-start(bf16[512,896]{1,0:T(8,128)(2,1)} %param.12) | copy-start | bytes 2752516
  146.8 20.8 %copy-start.5 = (bf16[512,2048]{1,0:T(8,128)(2,1)S(1)}, bf16[512,2048]{1,0:T(8,128)(2,1)}, u32[]{:S(2)}) copy-start(bf16[512,2048]{1,0:T(8,128)(2,1)} %all-gather.5.cloned.1.call-done) | copy-start | bytes 6291460
  146.8 34.0 %collective-permute-start.10 = (bf16[256,896]{1,0:T(8,128)(2,1)S(1)}, bf16[256,896]{1,0:T(8,128)(2,1)}, u32[]{:S(2)}, u32[]{:S(2)}) collective-permute-start(bf16[256,896]{1,0:T(8,128)(2,1)S(1)} %fusion.25), channel_id=1, source_target_pairs={{0,128},{1,129},{2,130},{3,131},{4,132},{5,133},{6,134},{7,135},{8... | collective-permute-start | bytes 1376264 | tf_op jit(solution)/shard_map/ppermute | solution.py:47
  166.3 14.5 %collective-permute-start.5 = (bf16[256,896]{1,0:T(8,128)(2,1)}, bf16[256,896]{1,0:T(8,128)(2,1)}, u32[]{:S(2)}, u32[]{:S(2)}) collective-permute-start(bf16[256,896]{1,0:T(8,128)(2,1)} %fusion.24), channel_id=1, source_target_pairs={{128,0},{129,1},{130,2},{131,3},{132,4},{133,5},{134,6},{135,7},{1... | collective-permute-start | bytes 1376264 | tf_op jit(solution)/shard_map/ppermute | solution.py:46
  178.0 9.0 %collective-permute-start = (bf16[32,4096]{1,0:T(8,128)(2,1)S(1)}, bf16[32,4096]{1,0:T(8,128)(2,1)}, u32[]{:S(2)}, u32[]{:S(2)}) collective-permute-start(bf16[32,4096]{1,0:T(8,128)(2,1)S(1)} %constant_dynamic-slice_fusion), channel_id=1, source_target_pairs={{0,1},{1,0},{2,3},{3,2},{4,5},{5,4},{6,7},{7,6},{8,9},{9,8},{10,11... | collective-permute-start | bytes 786440 | tf_op jit(solution)/shard_map/ppermute | solution.py:19
Sparse Core Ops, SparseCore 0:
  18.0 41.1 all-gather.4
  61.6 39.4 all-gather.2
  103.7 57.9 reduce-scatter.1

commit v6 on v3

--- a/solution.py
+++ b/solution.py
@@ -32,12 +32,20 @@
     arrived = exchange(jnp.take(parts, 1 - dc, axis=2), "dc", 2, 1)
     total = mine.astype(jnp.float32) + arrived.astype(jnp.float32)
     total = with_layout_constraint(total, Layout(major_to_minor=(0, 1, 2, 3)))
-    sent = total.astype(jnp.bfloat16)
     dx = lax.axis_index("dx")
-    acc = jnp.take(total, dx, axis=1)
-    for shift in range(1, n_x):
-        block = jnp.take(sent, (dx + shift) % n_x, axis=1)
-        acc = acc + exchange(block, "dx", n_x, shift).astype(jnp.float32)
+    rows = width // 2
+    halves = (total[:, :, :rows], total[:, :, rows:])
+    running = [None, None]
+    for step in range(n_x - 1):
+        for way, sign in ((0, 1), (1, -1)):
+            own = jnp.take(halves[way], (dx - sign * (step + 1)) % n_x, axis=1)
+            running[way] = own if step == 0 else running[way] + own
+            running[way] = exchange(
+                running[way].astype(jnp.bfloat16), "dx", n_x, sign % n_x
+            ).astype(jnp.float32)
+    acc = jnp.concatenate(
+        [jnp.take(halves[way], dx, axis=1) + running[way] for way in range(2)], axis=1
+    )
     dy = lax.axis_index("dy")
     sent = acc.astype(jnp.bfloat16)
     acc = jnp.take(acc, dy, axis=0) + exchange(jnp.take(sent, 1 - dy, axis=0), "dy", 2, 1).astype(jnp.float32)

time: 171 us -> 175 us (1.023); the launches traced: 171 us -> 172 us
  waiting for transfers between devices: 84.9 us -> 66.6 us
  other arithmetic: 15.8 us -> 21.6 us
  starting transfers between devices: 8.59 us -> 14.2 us
  local copies, waits for them, and re-layouts: 14.1 us -> 18.3 us
  matrix products: 21.2 us -> 25.2 us
    reduce_scatter x1, waiting for transfers between devices: 17.8 us -> 0.02 us  [per_device(): out = lax.psum_scatter(partial_out, 'tz', scatter_dimension=0, tiled=True)]
    convert_element_type x0 -> x6, other arithmetic: none -> 7.6 us  [weight_gradient(): running[way].astype(jnp.bfloat16)]
    ppermute x6 -> x9, starting transfers between devices: 8.51 us -> 14.1 us  [exchange(): return lax.ppermute(value, axis, perm)]
    dot_general x1, matrix products: 5.85 us -> 9.91 us  [per_device(): lax.dot_general(cotangent, weight, (((1,), (1,)), ((), ())), preferred_el...]
    slice x0 -> x1, local copies, waits for them, and re-layouts: none -> 2.62 us  [weight_gradient(): halves = (total[:, :, :rows], total[:, :, rows:])]
    unnamed x35 -> x21, local copies, waits for them, and re-layouts: 13.1 us -> 14.6 us
    ppermute x6 -> x9, waiting for transfers between devices: 27.5 us -> 27.9 us  [exchange(): return lax.ppermute(value, axis, perm)]
  transfers between devices with their start and end apart: 8 -> 11, of which waited for: 5 -> 6; matrix products, arithmetic and copies ran while one was open for 26% -> 33% of each run, Pallas kernels for 0% -> 0%
where the time goes in v6:
time: 175 us; the launch traced here: 172 us
  waiting for transfers between devices  66.6 us (38%)
  matrix products  25.2 us (14%)
  other arithmetic  21.6 us (12%)
  local copies, waits for them, and re-layouts  18.3 us (10%)
  between operations  14.3 us (8%)
  starting transfers between devices  14.2 us (8%)
  blocking collectives  12.1 us (7%)
    all_gather x1, waiting for transfers between devices, per_device(): cotangent = lax.all_gather(cotangent, 'tz', axis=0, tiled=True)  38.7 us
    ppermute x9, waiting for transfers between devices, exchange(): return lax.ppermute(value, axis, perm)  27.9 us
    unnamed x21, local copies, waits for them, and re-layouts  14.6 us
    ppermute x9, starting transfers between devices, exchange(): return lax.ppermute(value, axis, perm)  14.1 us
    all_gather x1, blocking collectives, per_device(): cotangent = lax.all_gather(grad_out, 'ty', axis=0, tiled=True)  12.1 us
    dot_general x1, matrix products, per_device(): lax.dot_general(cotangent, weight, (((1,), (1,)), ((), ())), preferred_el...  9.91 us
    dot_general x1, matrix products, per_device(): jnp.dot(hidden, weight, preferred_element_type=jnp.float32)  8.1 us
    convert_element_type x6, other arithmetic, weight_gradient(): running[way].astype(jnp.bfloat16)  7.6 us
  transfers between devices with their start and end apart: 11, of which 6 were waited for; matrix products, arithmetic and copies ran while one was open for 33% of the time, Pallas kernels for 0%

profile of v6, /device:TPU:1, one launch (start us, length us, event | category | flops | bytes accessed | tf_op | source)
XLA Modules:
  0.0 172.3 jit_solution(16037550997520453487)
XLA Ops:
  7.2 12.1 %all_gather.6 = bf16[64,4096]{1,0:T(8,128)(2,1)} all-gather(bf16[32,4096]{1,0:T(8,128)(2,1)} %param.11), channel_id=1, replica_groups=mesh['dy'=2,'dx'=4,'dc'=2,'tz'=8,'ty'=2] {'ty'}, dimensions={0}, use_global_device_ids=true | all-gather | bytes 786432 | tf_op jit(solution)/shard_map/all_gather | solution.py:70
  19.4 2.2 %copy.17 = bf16[512,896]{0,1:T(8,128)(2,1)} copy(bf16[512,896]{1,0:T(8,128)(2,1)} %param.10) | data formatting | bytes 1835008 | tf_op args[1]
  21.6 1.3 copy.16
  23.0 3.7 %bitcast_multiply_fusion = bf16[896,4096]{1,0:T(8,128)(2,1)S(1)} fusion(bf16[896,4096]{1,0:T(8,128)(2,1)} %param.12, bf16[28,4096]{1,0:T(8,128)(2,1)S(1)} %exponential_convert_fusion), kind=kLoop, calls=%fused_computation | loop fusion | flops 3670016 | bytes 14909440 | tf_op jit(solution)/shard_map/mul | solution.py:13
  26.7 2.9 %copy-done.1 = bf16[896,4096]{1,0:T(8,128)(2,1)} copy-done((bf16[896,4096]{1,0:T(8,128)(2,1)}, bf16[896,4096]{1,0:T(8,128)(2,1)S(1)}, u32[]{:S(2)}) %copy-start.1) | copy-done | bytes 7340056
  29.7 8.1 %convolution_convert_fusion.1 = bf16[512,4096]{1,0:T(8,128)(2,1)} fusion(bf16[896,4096]{1,0:T(8,128)(2,1)S(1)} %bitcast_multiply_fusion, bf16[512,896]{0,1:T(8,128)(2,1)} %copy.17, bf16[512,896]{0,1:T(8,128)(2,1)} %copy.16), kind=kOutput, calls=%fused_computation.3 | convolution fusion | flops 3763863552 | bytes 13369344 | tf_op jit(solution)/shard_map/dot_general | solution.py:62
  37.8 38.7 %all-gather.2.cloned.1.call-done = bf16[512,4096]{1,0:T(8,128)(2,1)} async-done(((bf16[64,4096]{1,0:T(8,128)(2,1)}), bf16[512,4096]{1,0:T(8,128)(2,1)}) %all-gather.2.cloned.1.call-update) | async-done | bytes 4194320 | tf_op jit(solution)/shard_map/all_gather | solution.py:71
  76.5 7.2 %convolution_convert_fusion = bf16[896,4096]{0,1:T(8,128)(2,1)S(1)} fusion(bf16[512,4096]{1,0:T(8,128)(2,1)} %all-gather.2.cloned.1.call-done, bf16[512,896]{0,1:T(8,128)(2,1)S(1)} %copy-done.4, bf16[512,896]{0,1:T(8,128)(2,1)S(1)} %copy-done.5), kind=kOutput, calls=%fused_computation.2 | convolution fusion | flops 3765436416 | bytes 13369344 | tf_op jit(solution)/shard_map/dot_general | solution.py:25
  83.7 2.5 %fusion = bf16[2,4,256,896]{3,2,1,0:T(8,128)(2,1)} fusion(bf16[2,4,2,256,896]{4,3,2,1,0:T(8,128)(2,1)S(1)} %bitcast.136, s32[]{:T(128)S(6)} %select_n.113, pred[]{:T(512)S(6)} %and.72), kind=kLoop, calls=%fused_computation.5 | loop fusion | flops 1835008 | bytes 7340037 | tf_op jit(solution)/shard_map/jit(_take)/select_n | solution.py:32
  86.2 1.8 %copy-done.2 = bf16[896,4096]{0,1:T(8,128)(2,1)} copy-done((bf16[896,4096]{0,1:T(8,128)(2,1)}, bf16[896,4096]{0,1:T(8,128)(2,1)S(1)}, u32[]{:S(2)}) %copy-start.2) | copy-done | bytes 7340056
  88.8 6.4 %collective-permute-done.1 = bf16[2,4,256,896]{3,2,1,0:T(8,128)(2,1)} collective-permute-done((bf16[2,4,256,896]{3,2,1,0:T(8,128)(2,1)}, bf16[2,4,256,896]{3,2,1,0:T(8,128)(2,1)}, u32[]{:S(2)}, u32[]{:S(2)}) %collective-permute-start.1) | collective-permute-done | bytes 3670048 | tf_op jit(solution)/shard_map/ppermute | solution.py:19
  95.2 4.2 %convert_add_fusion = f32[2,4,256,896]{3,2,1,0:T(8,128)S(1)} fusion(bf16[2,4,256,896]{3,2,1,0:T(8,128)(2,1)} %collective-permute-done.1, bf16[2,4,2,256,896]{4,3,2,1,0:T(8,128)(2,1)} %bitcast.137, s32[]{:T(128)S(6)} %select_n.111, pred[]{:T(512)S(6)} %and.71), kind=kLoop, calls=%fused_computation.1 | loop fusion | flops 7340032 | bytes 14680069 | tf_op jit(solution)/shard_map/add | solution.py:33
  99.4 2.6 %fusion.44 = (f32[2,4,128,896]{3,2,1,0:T(8,128)}, f32[2,4,128,896]{3,2,1,0:T(8,128)S(1)}) fusion(f32[2,4,256,896]{3,2,1,0:T(8,128)S(1)} %convert_add_fusion), kind=kLoop, calls=%fused_computation.69 | loop fusion | bytes 14680064 | tf_op jit(solution)/shard_map/slice | solution.py:37
  102.1 1.9 %copy-done = f32[2,4,128,896]{3,2,1,0:T(8,128)} copy-done((f32[2,4,128,896]{3,2,1,0:T(8,128)}, f32[2,4,128,896]{3,2,1,0:T(8,128)S(1)}, u32[]{:S(2)}) %copy-start) | copy-done | bytes 3670040
  104.0 2.5 %collective-permute-start.5 = (bf16[2,128,896]{2,1,0:T(8,128)(2,1)S(1)}, bf16[2,128,896]{2,1,0:T(8,128)(2,1)S(1)}, u32[]{:S(2)}, u32[]{:S(2)}) collective-permute-start(bf16[2,128,896]{2,1,0:T(8,128)(2,1)S(1)} %fusion.26), channel_id=1, source_target_pairs={{0,96},{32,0},{64,32},{96,64},{1,97},{33,1},{65,33},{97,65},{2,98}... | collective-permute-start | bytes 1376264 | tf_op jit(solution)/shard_map/ppermute | solution.py:19
  108.0 8.0 %collective-permute-done.5 = bf16[2,128,896]{2,1,0:T(8,128)(2,1)S(1)} collective-permute-done((bf16[2,128,896]{2,1,0:T(8,128)(2,1)S(1)}, bf16[2,128,896]{2,1,0:T(8,128)(2,1)S(1)}, u32[]{:S(2)}, u32[]{:S(2)}) %collective-permute-start.5) | collective-permute-done | bytes 458784 | tf_op jit(solution)/shard_map/ppermute | solution.py:19
  116.0 2.1 %fusion.24 = bf16[2,128,896]{2,1,0:T(8,128)(2,1)} fusion(f32[2,4,128,896]{3,2,1,0:T(8,128)} %copy-done, s32[]{:T(128)S(6)} %select_n.127, bf16[2,128,896]{2,1,0:T(8,128)(2,1)S(1)} %collective-permute-done.5, pred[]{:T(512)S(6)} %and.79), kind=kLoop, calls=%fused_computation.42 | loop fusion | flops 917504 | bytes 1835013 | tf_op jit(solution)/shard_map/convert_element_type | solution.py:44
  118.1 3.5 %collective-permute-start.6 = (bf16[2,128,896]{2,1,0:T(8,128)(2,1)}, bf16[2,128,896]{2,1,0:T(8,128)(2,1)}, u32[]{:S(2)}, u32[]{:S(2)}) collective-permute-start(bf16[2,128,896]{2,1,0:T(8,128)(2,1)} %fusion.24), channel_id=1, source_target_pairs={{0,96},{32,0},{64,32},{96,64},{1,97},{33,1},{65,33},{97,65},{2,98}... | collective-permute-start | bytes 1376264 | tf_op jit(solution)/shard_map/ppermute | solution.py:19
  121.6 1.4 fusion.34
  123.3 9.9 %fusion.11 = (bf16[512,896]{0,1:T(8,128)(2,1)S(1)}, bf16[512,896]{0,1:T(8,128)(2,1)}) fusion(bf16[512,896]{0,1:T(8,128)(2,1)S(1)} %copy-done.5, bf16[512,896]{0,1:T(8,128)(2,1)S(1)} %copy-done.4, bf16[896,4096]{1,0:T(8,128)(2,1)} %copy-done.1, bf16[512,4096]{1,0:T(8,128)(2,1)} %all-gather.2.cloned.1.call-done), kind=kOutput, calls=%fused_computation.27 | convolution fusion | flops 3764977664 | bytes 15204352 | tf_op jit(solution)/shard_map/dot_general | solution.py:72
  133.2 2.2 %copy.22 = bf16[512,896]{1,0:T(8,128)(2,1)} copy(bf16[512,896]{0,1:T(8,128)(2,1)} %get-tuple-element.61) | data formatting | bytes 1835008
  135.4 1.3 copy.23
  136.7 1.4 fusion.21
  138.1 2.7 %collective-permute-start.7 = (bf16[2,128,896]{2,1,0:T(8,128)(2,1)S(1)}, bf16[2,128,896]{2,1,0:T(8,128)(2,1)S(1)}, u32[]{:S(2)}, u32[]{:S(2)}) collective-permute-start(bf16[2,128,896]{2,1,0:T(8,128)(2,1)S(1)} %fusion.21), channel_id=1, source_target_pairs={{0,96},{32,0},{64,32},{96,64},{1,97},{33,1},{65,33},{97,65},{2,98}... | collective-permute-start | bytes 1376264 | tf_op jit(solution)/shard_map/ppermute | solution.py:19
  140.8 1.4 fusion.31
  143.4 2.8 %collective-permute-start = (bf16[32,4096]{1,0:T(8,128)(2,1)S(1)}, bf16[32,4096]{1,0:T(8,128)(2,1)S(1)}, u32[]{:S(2)}, u32[]{:S(2)}) collective-permute-start(bf16[32,4096]{1,0:T(8,128)(2,1)S(1)} %constant_dynamic-slice_fusion), channel_id=1, source_target_pairs={{0,1},{1,0},{2,3},{3,2},{4,5},{5,4},{6,7},{7,6},{8,9},{9,8},{10,11... | collective-permute-start | bytes 786440 | tf_op jit(solution)/shard_map/ppermute | solution.py:19
  146.2 2.8 %collective-permute-done.7 = bf16[2,128,896]{2,1,0:T(8,128)(2,1)S(1)} collective-permute-done((bf16[2,128,896]{2,1,0:T(8,128)(2,1)S(1)}, bf16[2,128,896]{2,1,0:T(8,128)(2,1)S(1)}, u32[]{:S(2)}, u32[]{:S(2)}) %collective-permute-start.7) | collective-permute-done | bytes 458784 | tf_op jit(solution)/shard_map/ppermute | solution.py:19
  149.1 1.3 fusion.28
  150.3 3.3 %collective-permute-done.4 = bf16[2,128,896]{2,1,0:T(8,128)(2,1)S(1)} collective-permute-done((bf16[2,128,896]{2,1,0:T(8,128)(2,1)S(1)}, bf16[2,128,896]{2,1,0:T(8,128)(2,1)S(1)}, u32[]{:S(2)}, u32[]{:S(2)}) %collective-permute-start.4) | collective-permute-done | bytes 458784 | tf_op jit(solution)/shard_map/ppermute | solution.py:19
  153.7 1.3 fusion.38
  155.0 1.3 collective-permute-start.8
  157.1 7.3 %collective-permute-done.8 = bf16[256,896]{1,0:T(8,128)(2,1)S(1)} collective-permute-done((bf16[256,896]{1,0:T(8,128)(2,1)S(1)}, bf16[256,896]{1,0:T(8,128)(2,1)S(1)}, u32[]{:S(2)}, u32[]{:S(2)}) %collective-permute-start.8) | collective-permute-done | bytes 458784 | tf_op jit(solution)/shard_map/ppermute | solution.py:19
  (34 shorter events, 5.8 us)
Async XLA Ops:
  7.2 14.5 %copy-start.3 = (bf16[512,896]{1,0:T(8,128)(2,1)S(1)}, bf16[512,896]{1,0:T(8,128)(2,1)}, u32[]{:S(2)}) copy-start(bf16[512,896]{1,0:T(8,128)(2,1)} %param.9) | copy-start | bytes 2752516
  7.2 15.7 %copy-start.6 = (s32[28,4096]{1,0:T(8,128)S(1)}, s32[28,4096]{1,0:T(8,128)}, u32[]{:S(2)}) copy-start(s32[28,4096]{1,0:T(8,128)} %param.13) | copy-start | bytes 1376260
  7.2 69.3 %all-gather.2.cloned.1.call-start = ((), (), s32[]{:S(2)}) async-start(), calls=%async_computation.2 | async-start | bytes 4718592 | tf_op jit(solution)/shard_map/all_gather | solution.py:71
  19.4 123.0 %reduce-scatter.2.cloned.1.call-start = ((), (), s32[]{:S(2)}) async-start(), calls=%async_computation.1 | async-start | bytes 4718592 | tf_op jit(solution)/shard_map/reduce_scatter | solution.py:63
  26.7 2.9 %copy-start.1 = (bf16[896,4096]{1,0:T(8,128)(2,1)}, bf16[896,4096]{1,0:T(8,128)(2,1)S(1)}, u32[]{:S(2)}) copy-start(bf16[896,4096]{1,0:T(8,128)(2,1)S(1)} %bitcast_multiply_fusion) | copy-start | bytes 22020100
  37.8 38.7 %copy-start.4 = (bf16[512,896]{0,1:T(8,128)(2,1)S(1)}, bf16[512,896]{0,1:T(8,128)(2,1)}, u32[]{:S(2)}) copy-start(bf16[512,896]{0,1:T(8,128)(2,1)} %copy.17) | copy-start | bytes 2752516
  37.8 38.7 %copy-start.5 = (bf16[512,896]{0,1:T(8,128)(2,1)S(1)}, bf16[512,896]{0,1:T(8,128)(2,1)}, u32[]{:S(2)}) copy-start(bf16[512,896]{0,1:T(8,128)(2,1)} %copy.16) | copy-start | bytes 2752516
  83.7 4.3 %copy-start.2 = (bf16[896,4096]{0,1:T(8,128)(2,1)}, bf16[896,4096]{0,1:T(8,128)(2,1)S(1)}, u32[]{:S(2)}) copy-start(bf16[896,4096]{0,1:T(8,128)(2,1)S(1)} %convolution_convert_fusion) | copy-start | bytes 22020100
  88.0 7.2 %collective-permute-start.1 = (bf16[2,4,256,896]{3,2,1,0:T(8,128)(2,1)}, bf16[2,4,256,896]{3,2,1,0:T(8,128)(2,1)}, u32[]{:S(2)}, u32[]{:S(2)}) collective-permute-start(bf16[2,4,256,896]{3,2,1,0:T(8,128)(2,1)} %fusion), channel_id=1, source_target_pairs={{0,16},{16,0},{1,17},{17,1},{2,18},{18,2},{3,19},{19,3},{4,20},{20... | collective-permute-start | bytes 11010056 | tf_op jit(solution)/shard_map/ppermute | solution.py:19
  102.1 1.9 %copy-start = (f32[2,4,128,896]{3,2,1,0:T(8,128)}, f32[2,4,128,896]{3,2,1,0:T(8,128)S(1)}, u32[]{:S(2)}) copy-start(f32[2,4,128,896]{3,2,1,0:T(8,128)S(1)} %get-tuple-element.59) | copy-start | bytes 11010052
  104.0 12.0 %collective-permute-start.5 = (bf16[2,128,896]{2,1,0:T(8,128)(2,1)S(1)}, bf16[2,128,896]{2,1,0:T(8,128)(2,1)S(1)}, u32[]{:S(2)}, u32[]{:S(2)}) collective-permute-start(bf16[2,128,896]{2,1,0:T(8,128)(2,1)S(1)} %fusion.26), channel_id=1, source_target_pairs={{0,96},{32,0},{64,32},{96,64},{1,97},{33,1},{65,33},{97,65},{2,98}... | collective-permute-start | bytes 1376264 | tf_op jit(solution)/shard_map/ppermute | solution.py:19
  107.8 13.8 %collective-permute-start.2 = (bf16[2,128,896]{2,1,0:T(8,128)(2,1)S(1)}, bf16[2,128,896]{2,1,0:T(8,128)(2,1)}, u32[]{:S(2)}, u32[]{:S(2)}) collective-permute-start(bf16[2,128,896]{2,1,0:T(8,128)(2,1)S(1)} %fusion.36), channel_id=1, source_target_pairs={{0,32},{32,64},{64,96},{96,0},{1,33},{33,65},{65,97},{97,1},{2,34}... | collective-permute-start | bytes 1376264 | tf_op jit(solution)/shard_map/ppermute | solution.py:19
  118.1 18.6 %collective-permute-start.6 = (bf16[2,128,896]{2,1,0:T(8,128)(2,1)}, bf16[2,128,896]{2,1,0:T(8,128)(2,1)}, u32[]{:S(2)}, u32[]{:S(2)}) collective-permute-start(bf16[2,128,896]{2,1,0:T(8,128)(2,1)} %fusion.24), channel_id=1, source_target_pairs={{0,96},{32,0},{64,32},{96,64},{1,97},{33,1},{65,33},{97,65},{2,98}... | collective-permute-start | bytes 1376264 | tf_op jit(solution)/shard_map/ppermute | solution.py:19
  123.0 17.8 %collective-permute-start.3 = (bf16[2,128,896]{2,1,0:T(8,128)(2,1)S(1)}, bf16[2,128,896]{2,1,0:T(8,128)(2,1)}, u32[]{:S(2)}, u32[]{:S(2)}) collective-permute-start(bf16[2,128,896]{2,1,0:T(8,128)(2,1)S(1)} %fusion.34), channel_id=1, source_target_pairs={{0,32},{32,64},{64,96},{96,0},{1,33},{33,65},{65,97},{97,1},{2,34}... | collective-permute-start | bytes 1376264 | tf_op jit(solution)/shard_map/ppermute | solution.py:19
  138.1 10.9 %collective-permute-start.7 = (bf16[2,128,896]{2,1,0:T(8,128)(2,1)S(1)}, bf16[2,128,896]{2,1,0:T(8,128)(2,1)S(1)}, u32[]{:S(2)}, u32[]{:S(2)}) collective-permute-start(bf16[2,128,896]{2,1,0:T(8,128)(2,1)S(1)} %fusion.21), channel_id=1, source_target_pairs={{0,96},{32,0},{64,32},{96,64},{1,97},{33,1},{65,33},{97,65},{2,98}... | collective-permute-start | bytes 1376264 | tf_op jit(solution)/shard_map/ppermute | solution.py:19
  142.3 11.4 %collective-permute-start.4 = (bf16[2,128,896]{2,1,0:T(8,128)(2,1)S(1)}, bf16[2,128,896]{2,1,0:T(8,128)(2,1)S(1)}, u32[]{:S(2)}, u32[]{:S(2)}) collective-permute-start(bf16[2,128,896]{2,1,0:T(8,128)(2,1)S(1)} %fusion.31), channel_id=1, source_target_pairs={{0,32},{32,64},{64,96},{96,0},{1,33},{33,65},{65,97},{97,1},{2,34}... | collective-permute-start | bytes 1376264 | tf_op jit(solution)/shard_map/ppermute | solution.py:19
  142.4 13.9 %copy-start.7 = (bf16[64,4096]{1,0:T(8,128)(2,1)S(1)}, bf16[64,4096]{1,0:T(8,128)(2,1)}, u32[]{:S(2)}) copy-start(bf16[64,4096]{1,0:T(8,128)(2,1)} %reduce-scatter.2.cloned.1.call-done) | copy-start | bytes 1572868
  143.4 12.9 %collective-permute-start = (bf16[32,4096]{1,0:T(8,128)(2,1)S(1)}, bf16[32,4096]{1,0:T(8,128)(2,1)S(1)}, u32[]{:S(2)}, u32[]{:S(2)}) collective-permute-start(bf16[32,4096]{1,0:T(8,128)(2,1)S(1)} %constant_dynamic-slice_fusion), channel_id=1, source_target_pairs={{0,1},{1,0},{2,3},{3,2},{4,5},{5,4},{6,7},{7,6},{8,9},{9,8},{10,11... | collective-permute-start | bytes 786440 | tf_op jit(solution)/shard_map/ppermute | solution.py:19
  155.0 9.4 %collective-permute-start.8 = (bf16[256,896]{1,0:T(8,128)(2,1)S(1)}, bf16[256,896]{1,0:T(8,128)(2,1)S(1)}, u32[]{:S(2)}, u32[]{:S(2)}) collective-permute-start(bf16[256,896]{1,0:T(8,128)(2,1)S(1)} %fusion.40), channel_id=1, source_target_pairs={{0,128},{128,0},{1,129},{129,1},{2,130},{130,2},{3,131},{131,3},{4... | collective-permute-start | bytes 1376264 | tf_op jit(solution)/shard_map/ppermute | solution.py:19
Sparse Core Ops, SparseCore 0:
  19.5 56.9 all-gather.1
  79.0 54.0 reduce-scatter.1

commit v7 on v3

--- a/solution.py
+++ b/solution.py
@@ -35,9 +35,23 @@
     sent = total.astype(jnp.bfloat16)
     dx = lax.axis_index("dx")
     acc = jnp.take(total, dx, axis=1)
-    for shift in range(1, n_x):
-        block = jnp.take(sent, (dx + shift) % n_x, axis=1)
-        acc = acc + exchange(block, "dx", n_x, shift).astype(jnp.float32)
+    if n_x == 4:
+        ahead = jnp.take(sent, (dx + 1) % n_x, axis=1)
+        behind = jnp.take(sent, (dx + 3) % n_x, axis=1)
+        across = jnp.take(sent, (dx + 2) % n_x, axis=1)
+        rows = width // 2
+        relay_up = exchange(across[:, :rows], "dx", n_x, 1)
+        relay_down = exchange(across[:, rows:], "dx", n_x, n_x - 1)
+        acc = acc + exchange(ahead, "dx", n_x, 1).astype(jnp.float32)
+        acc = acc + exchange(behind, "dx", n_x, n_x - 1).astype(jnp.float32)
+        far = jnp.concatenate(
+            [exchange(relay_up, "dx", n_x, 1), exchange(relay_down, "dx", n_x, n_x - 1)], axis=1
+        )
+        acc = acc + far.astype(jnp.float32)
+    else:
+        for shift in range(1, n_x):
+            block = jnp.take(sent, (dx + shift) % n_x, axis=1)
+            acc = acc + exchange(block, "dx", n_x, shift).astype(jnp.float32)
     dy = lax.axis_index("dy")
     sent = acc.astype(jnp.bfloat16)
     acc = jnp.take(acc, dy, axis=0) + exchange(jnp.take(sent, 1 - dy, axis=0), "dy", 2, 1).astype(jnp.float32)

time: 171 us -> 171 us (level)
  waiting for transfers between devices: 84.9 us -> 73.3 us
  starting transfers between devices: 8.59 us -> 13.7 us
  matrix products: 21.2 us -> 25.3 us
  local copies, waits for them, and re-layouts: 14.1 us -> 15.9 us
    reduce_scatter x1, waiting for transfers between devices: 17.8 us -> 0.01 us  [per_device(): out = lax.psum_scatter(partial_out, 'tz', scatter_dimension=0, tiled=True)]
    ppermute x6 -> x9, waiting for transfers between devices: 27.5 us -> 33.7 us  [exchange(): return lax.ppermute(value, axis, perm)]
    ppermute x6 -> x9, starting transfers between devices: 8.51 us -> 13.6 us  [exchange(): return lax.ppermute(value, axis, perm)]
    dot_general x1, matrix products: 5.85 us -> 9.95 us  [per_device(): lax.dot_general(cotangent, weight, (((1,), (1,)), ((), ())), preferred_el...]
    unnamed x35 -> x23, local copies, waits for them, and re-layouts: 13.1 us -> 14.8 us
  transfers between devices with their start and end apart: 8 -> 11, of which waited for: 5 -> 7; matrix products, arithmetic and copies ran while one was open for 26% -> 28% of each run, Pallas kernels for 0% -> 0%
where the time goes in v7:
time: 171 us; the launch traced here: 170 us
  waiting for transfers between devices  73.3 us (43%)
  matrix products  25.3 us (15%)
  local copies, waits for them, and re-layouts  15.9 us (9%)
  other arithmetic  15.9 us (9%)
  between operations  14.2 us (8%)
  starting transfers between devices  13.7 us (8%)
  blocking collectives  12.1 us (7%)
    all_gather x1, waiting for transfers between devices, per_device(): cotangent = lax.all_gather(cotangent, 'tz', axis=0, tiled=True)  39.6 us
    ppermute x9, waiting for transfers between devices, exchange(): return lax.ppermute(value, axis, perm)  33.7 us
    unnamed x23, local copies, waits for them, and re-layouts  14.8 us
    ppermute x9, starting transfers between devices, exchange(): return lax.ppermute(value, axis, perm)  13.6 us
    all_gather x1, blocking collectives, per_device(): cotangent = lax.all_gather(grad_out, 'ty', axis=0, tiled=True)  12.1 us
    dot_general x1, matrix products, per_device(): lax.dot_general(cotangent, weight, (((1,), (1,)), ((), ())), preferred_el...  9.95 us
    dot_general x1, matrix products, per_device(): jnp.dot(hidden, weight, preferred_element_type=jnp.float32)  8.11 us
    dot_general x1, matrix products, weight_gradient(): lax.dot_general(cotangent, hidden, (((0,), (0,)), ((), ())), preferred_el...  7.2 us
  transfers between devices with their start and end apart: 11, of which 7 were waited for; matrix products, arithmetic and copies ran while one was open for 28% of the time, Pallas kernels for 0%

profile of v7, /device:TPU:1, one launch (start us, length us, event | category | flops | bytes accessed | tf_op | source)
XLA Modules:
  0.0 170.4 jit_solution(16692500377162180315)
XLA Ops:
  7.2 12.1 %all_gather.6 = bf16[64,4096]{1,0:T(8,128)(2,1)} all-gather(bf16[32,4096]{1,0:T(8,128)(2,1)} %param.11), channel_id=1, replica_groups=mesh['dy'=2,'dx'=4,'dc'=2,'tz'=8,'ty'=2] {'ty'}, dimensions={0}, use_global_device_ids=true | all-gather | bytes 786432 | tf_op jit(solution)/shard_map/all_gather | solution.py:76
  19.4 1.3 copy.17
  20.7 1.3 copy.16
  22.1 3.7 %bitcast_multiply_fusion = bf16[896,4096]{1,0:T(8,128)(2,1)S(1)} fusion(bf16[896,4096]{1,0:T(8,128)(2,1)} %param.12, bf16[28,4096]{1,0:T(8,128)(2,1)S(1)} %exponential_convert_fusion), kind=kLoop, calls=%fused_computation | loop fusion | flops 3670016 | bytes 14909440 | tf_op jit(solution)/shard_map/mul | solution.py:13
  25.8 2.9 %copy-done.1 = bf16[896,4096]{1,0:T(8,128)(2,1)} copy-done((bf16[896,4096]{1,0:T(8,128)(2,1)}, bf16[896,4096]{1,0:T(8,128)(2,1)S(1)}, u32[]{:S(2)}) %copy-start.1) | copy-done | bytes 7340056
  28.7 8.1 %convolution_convert_fusion.1 = bf16[512,4096]{1,0:T(8,128)(2,1)} fusion(bf16[896,4096]{1,0:T(8,128)(2,1)S(1)} %bitcast_multiply_fusion, bf16[512,896]{0,1:T(8,128)(2,1)} %copy.17, bf16[512,896]{0,1:T(8,128)(2,1)} %copy.16), kind=kOutput, calls=%fused_computation.3 | convolution fusion | flops 3763863552 | bytes 13369344 | tf_op jit(solution)/shard_map/dot_general | solution.py:68
  36.9 39.6 %all-gather.2.cloned.1.call-done = bf16[512,4096]{1,0:T(8,128)(2,1)} async-done(((bf16[64,4096]{1,0:T(8,128)(2,1)}), bf16[512,4096]{1,0:T(8,128)(2,1)}) %all-gather.2.cloned.1.call-update) | async-done | bytes 4194320 | tf_op jit(solution)/shard_map/all_gather | solution.py:77
  76.5 7.2 %convolution_convert_fusion = bf16[896,4096]{0,1:T(8,128)(2,1)S(1)} fusion(bf16[512,4096]{1,0:T(8,128)(2,1)} %all-gather.2.cloned.1.call-done, bf16[512,896]{0,1:T(8,128)(2,1)S(1)} %copy-done.5, bf16[512,896]{0,1:T(8,128)(2,1)S(1)} %copy-done.6), kind=kOutput, calls=%fused_computation.2 | convolution fusion | flops 3765436416 | bytes 13369344 | tf_op jit(solution)/shard_map/dot_general | solution.py:25
  83.7 2.5 %fusion = bf16[2,4,256,896]{3,2,1,0:T(8,128)(2,1)} fusion(bf16[2,4,2,256,896]{4,3,2,1,0:T(8,128)(2,1)S(1)} %bitcast.50, s32[]{:T(128)S(6)} %select_n.90, pred[]{:T(512)S(6)} %and.53), kind=kLoop, calls=%fused_computation.5 | loop fusion | flops 1835008 | bytes 7340037 | tf_op jit(solution)/shard_map/jit(_take)/select_n | solution.py:32
  86.2 1.8 %copy-done.2 = bf16[896,4096]{0,1:T(8,128)(2,1)} copy-done((bf16[896,4096]{0,1:T(8,128)(2,1)}, bf16[896,4096]{0,1:T(8,128)(2,1)S(1)}, u32[]{:S(2)}) %copy-start.2) | copy-done | bytes 7340056
  88.0 0.8 collective-permute-start.1
  88.8 6.4 %collective-permute-done.1 = bf16[2,4,256,896]{3,2,1,0:T(8,128)(2,1)} collective-permute-done((bf16[2,4,256,896]{3,2,1,0:T(8,128)(2,1)}, bf16[2,4,256,896]{3,2,1,0:T(8,128)(2,1)}, u32[]{:S(2)}, u32[]{:S(2)}) %collective-permute-start.1) | collective-permute-done | bytes 3670048 | tf_op jit(solution)/shard_map/ppermute | solution.py:19
  95.2 4.2 %convert_add_fusion = f32[2,4,256,896]{3,2,1,0:T(8,128)S(1)} fusion(bf16[2,4,256,896]{3,2,1,0:T(8,128)(2,1)} %collective-permute-done.1, bf16[2,4,2,256,896]{4,3,2,1,0:T(8,128)(2,1)} %bitcast.51, s32[]{:T(128)S(6)} %select_n.88, pred[]{:T(512)S(6)} %and.52), kind=kLoop, calls=%fused_computation.1 | loop fusion | flops 7340032 | bytes 14680069 | tf_op jit(solution)/shard_map/add | solution.py:33
  99.5 3.0 %copy-done = f32[2,4,256,896]{3,2,1,0:T(8,128)} copy-done((f32[2,4,256,896]{3,2,1,0:T(8,128)}, f32[2,4,256,896]{3,2,1,0:T(8,128)S(1)}, u32[]{:S(2)}) %copy-start) | copy-done | bytes 7340056
  102.5 1.8 %select_bitcast_fusion = (bf16[2,256,896]{2,1,0:T(8,128)(2,1)S(1)}, bf16[2,256,896]{2,1,0:T(8,128)(2,1)}, bf16[2,256,896]{2,1,0:T(8,128)(2,1)}) fusion(s32[]{:T(128)S(6)} %select_n.96, pred[]{:T(512)S(6)} %and.56, s32[]{:T(128)S(6)} %select_n.94, pred[]{:T(512)S(6)} %and.55, s32[]{:T(128)S(6)} %select_n.92, pred[]{:T(512)S(6)} %and.54, ...), kind=kLoop, calls=%fused_computation.30 | loop fusion | flops 1376256 | bytes 5505039 | tf_op jit(solution)/shard_map/jit(_take)/select_n | solution.py:41
  104.4 2.5 %collective-permute-start.6 = (bf16[2,128,896]{2,1,0:T(8,128)(2,1)S(1)}, bf16[2,128,896]{2,1,0:T(8,128)(2,1)}, u32[]{:S(2)}, u32[]{:S(2)}) collective-permute-start(bf16[2,128,896]{2,1,0:T(8,128)(2,1)S(1)} %get-tuple-element.75), channel_id=1, source_target_pairs={{0,96},{32,0},{64,32},{96,64},{1,97},{33,1},{65,33},{97,65},{2,98}... | collective-permute-start | bytes 1376264 | tf_op jit(solution)/shard_map/ppermute | solution.py:19
  106.9 2.7 %collective-permute-start.3 = (bf16[2,256,896]{2,1,0:T(8,128)(2,1)}, bf16[2,256,896]{2,1,0:T(8,128)(2,1)}, u32[]{:S(2)}, u32[]{:S(2)}) collective-permute-start(bf16[2,256,896]{2,1,0:T(8,128)(2,1)} %get-tuple-element.70), channel_id=1, source_target_pairs={{0,96},{32,0},{64,32},{96,64},{1,97},{33,1},{65,33},{97,65},{2,98}... | collective-permute-start | bytes 2752520 | tf_op jit(solution)/shard_map/ppermute | solution.py:19
  109.5 6.8 %collective-permute-done.6 = bf16[2,128,896]{2,1,0:T(8,128)(2,1)} collective-permute-done((bf16[2,128,896]{2,1,0:T(8,128)(2,1)S(1)}, bf16[2,128,896]{2,1,0:T(8,128)(2,1)}, u32[]{:S(2)}, u32[]{:S(2)}) %collective-permute-start.6) | collective-permute-done | bytes 458784 | tf_op jit(solution)/shard_map/ppermute | solution.py:19
  116.3 3.5 %collective-permute-start.7 = (bf16[2,128,896]{2,1,0:T(8,128)(2,1)}, bf16[2,128,896]{2,1,0:T(8,128)(2,1)S(1)}, u32[]{:S(2)}, u32[]{:S(2)}) collective-permute-start(bf16[2,128,896]{2,1,0:T(8,128)(2,1)} %collective-permute-done.6), channel_id=1, source_target_pairs={{0,96},{32,0},{64,32},{96,64},{1,97},{33,1},{65,33},{97,65},{2,98}... | collective-permute-start | bytes 1376264 | tf_op jit(solution)/shard_map/ppermute | solution.py:19
  119.9 10.0 %fusion.11 = (bf16[512,896]{0,1:T(8,128)(2,1)S(1)}, bf16[512,896]{0,1:T(8,128)(2,1)}) fusion(bf16[512,896]{0,1:T(8,128)(2,1)S(1)} %copy-done.6, bf16[512,896]{0,1:T(8,128)(2,1)S(1)} %copy-done.5, bf16[896,4096]{1,0:T(8,128)(2,1)} %copy-done.1, bf16[512,4096]{1,0:T(8,128)(2,1)} %all-gather.2.cloned.1.call-done), kind=kOutput, calls=%fused_computation.23 | convolution fusion | flops 3764977664 | bytes 15204352 | tf_op jit(solution)/shard_map/dot_general | solution.py:78
  129.8 2.2 %copy.22 = bf16[512,896]{1,0:T(8,128)(2,1)} copy(bf16[512,896]{0,1:T(8,128)(2,1)} %get-tuple-element.73) | data formatting | bytes 1835008
  132.0 1.3 copy.23
  133.3 1.0 constant_dynamic-slice_fusion
  134.3 2.8 %collective-permute-start = (bf16[32,4096]{1,0:T(8,128)(2,1)S(1)}, bf16[32,4096]{1,0:T(8,128)(2,1)S(1)}, u32[]{:S(2)}, u32[]{:S(2)}) collective-permute-start(bf16[32,4096]{1,0:T(8,128)(2,1)S(1)} %constant_dynamic-slice_fusion), channel_id=1, source_target_pairs={{0,1},{1,0},{2,3},{3,2},{4,5},{5,4},{6,7},{7,6},{8,9},{9,8},{10,11... | collective-permute-start | bytes 786440 | tf_op jit(solution)/shard_map/ppermute | solution.py:19
  137.1 2.1 %collective-permute-done.2 = bf16[2,256,896]{2,1,0:T(8,128)(2,1)} collective-permute-done((bf16[2,256,896]{2,1,0:T(8,128)(2,1)}, bf16[2,256,896]{2,1,0:T(8,128)(2,1)}, u32[]{:S(2)}, u32[]{:S(2)}) %collective-permute-start.2) | collective-permute-done | bytes 917536 | tf_op jit(solution)/shard_map/ppermute | solution.py:19
  139.2 6.7 %collective-permute-done.7 = bf16[2,128,896]{2,1,0:T(8,128)(2,1)S(1)} collective-permute-done((bf16[2,128,896]{2,1,0:T(8,128)(2,1)}, bf16[2,128,896]{2,1,0:T(8,128)(2,1)S(1)}, u32[]{:S(2)}, u32[]{:S(2)}) %collective-permute-start.7) | collective-permute-done | bytes 458784 | tf_op jit(solution)/shard_map/ppermute | solution.py:19
  145.9 3.1 %collective-permute-done.5 = bf16[2,128,896]{2,1,0:T(8,128)(2,1)} collective-permute-done((bf16[2,128,896]{2,1,0:T(8,128)(2,1)}, bf16[2,128,896]{2,1,0:T(8,128)(2,1)}, u32[]{:S(2)}, u32[]{:S(2)}) %collective-permute-start.5) | collective-permute-done | bytes 458784 | tf_op jit(solution)/shard_map/ppermute | solution.py:19
  149.1 2.6 %fusion.13 = f32[2,256,896]{2,1,0:T(8,128)S(1)} fusion(s32[]{:T(128)S(6)} %select_n.60, bf16[2,256,896]{2,1,0:T(8,128)(2,1)} %collective-permute-done.3, bf16[2,256,896]{2,1,0:T(8,128)(2,1)} %collective-permute-done.2, bf16[2,128,896]{2,1,0:T(8,128)(2,1)S(1)} %collective-permute-done.7, bf16[2,128,896]{2,1,0:T(8,128)(2,1)} %collective-permute-done.5, ...), kind=kLoop, calls=%fused_computation.26 | loop fusion | flops 4587520 | bytes 6422533 | tf_op jit(solution)/shard_map/add | solution.py:50
  151.8 1.3 collective-permute-start.8
  153.1 0.8 add_convert_fusion
  153.8 8.6 %collective-permute-done.8 = bf16[256,896]{1,0:T(8,128)(2,1)S(1)} collective-permute-done((bf16[256,896]{1,0:T(8,128)(2,1)S(1)}, bf16[256,896]{1,0:T(8,128)(2,1)S(1)}, u32[]{:S(2)}, u32[]{:S(2)}) %collective-permute-start.8) | collective-permute-done | bytes 458784 | tf_op jit(solution)/shard_map/ppermute | solution.py:19
  162.5 1.0 copy.24
  (30 shorter events, 0.5 us)
Async XLA Ops:
  7.2 12.3 %copy-start.3 = (bf16[512,896]{1,0:T(8,128)(2,1)S(1)}, bf16[512,896]{1,0:T(8,128)(2,1)}, u32[]{:S(2)}) copy-start(bf16[512,896]{1,0:T(8,128)(2,1)} %param.10) | copy-start | bytes 2752516
  7.2 13.5 %copy-start.4 = (bf16[512,896]{1,0:T(8,128)(2,1)S(1)}, bf16[512,896]{1,0:T(8,128)(2,1)}, u32[]{:S(2)}) copy-start(bf16[512,896]{1,0:T(8,128)(2,1)} %param.9) | copy-start | bytes 2752516
  7.2 69.3 %all-gather.2.cloned.1.call-start = ((), (), s32[]{:S(2)}) async-start(), calls=%async_computation.2 | async-start | bytes 4718592 | tf_op jit(solution)/shard_map/all_gather | solution.py:77
  19.4 2.6 %copy-start.7 = (s32[28,4096]{1,0:T(8,128)S(1)}, s32[28,4096]{1,0:T(8,128)}, u32[]{:S(2)}) copy-start(s32[28,4096]{1,0:T(8,128)} %param.13) | copy-start | bytes 1376260
  19.4 113.9 %reduce-scatter.2.cloned.1.call-start = ((), (), s32[]{:S(2)}) async-start(), calls=%async_computation.1 | async-start | bytes 4718592 | tf_op jit(solution)/shard_map/reduce_scatter | solution.py:69
  25.8 2.9 %copy-start.1 = (bf16[896,4096]{1,0:T(8,128)(2,1)}, bf16[896,4096]{1,0:T(8,128)(2,1)S(1)}, u32[]{:S(2)}) copy-start(bf16[896,4096]{1,0:T(8,128)(2,1)S(1)} %bitcast_multiply_fusion) | copy-start | bytes 22020100
  36.8 39.6 %copy-start.5 = (bf16[512,896]{0,1:T(8,128)(2,1)S(1)}, bf16[512,896]{0,1:T(8,128)(2,1)}, u32[]{:S(2)}) copy-start(bf16[512,896]{0,1:T(8,128)(2,1)} %copy.17) | copy-start | bytes 2752516
  36.8 39.6 %copy-start.6 = (bf16[512,896]{0,1:T(8,128)(2,1)S(1)}, bf16[512,896]{0,1:T(8,128)(2,1)}, u32[]{:S(2)}) copy-start(bf16[512,896]{0,1:T(8,128)(2,1)} %copy.16) | copy-start | bytes 2752516
  83.7 4.3 %copy-start.2 = (bf16[896,4096]{0,1:T(8,128)(2,1)}, bf16[896,4096]{0,1:T(8,128)(2,1)S(1)}, u32[]{:S(2)}) copy-start(bf16[896,4096]{0,1:T(8,128)(2,1)S(1)} %convolution_convert_fusion) | copy-start | bytes 22020100
  88.0 7.2 %collective-permute-start.1 = (bf16[2,4,256,896]{3,2,1,0:T(8,128)(2,1)}, bf16[2,4,256,896]{3,2,1,0:T(8,128)(2,1)}, u32[]{:S(2)}, u32[]{:S(2)}) collective-permute-start(bf16[2,4,256,896]{3,2,1,0:T(8,128)(2,1)} %fusion), channel_id=1, source_target_pairs={{0,16},{16,0},{1,17},{17,1},{2,18},{18,2},{3,19},{19,3},{4,20},{20... | collective-permute-start | bytes 11010056 | tf_op jit(solution)/shard_map/ppermute | solution.py:19
  99.5 3.0 %copy-start = (f32[2,4,256,896]{3,2,1,0:T(8,128)}, f32[2,4,256,896]{3,2,1,0:T(8,128)S(1)}, u32[]{:S(2)}) copy-start(f32[2,4,256,896]{3,2,1,0:T(8,128)S(1)} %convert_add_fusion) | copy-start | bytes 22020100
  104.4 12.0 %collective-permute-start.6 = (bf16[2,128,896]{2,1,0:T(8,128)(2,1)S(1)}, bf16[2,128,896]{2,1,0:T(8,128)(2,1)}, u32[]{:S(2)}, u32[]{:S(2)}) collective-permute-start(bf16[2,128,896]{2,1,0:T(8,128)(2,1)S(1)} %get-tuple-element.75), channel_id=1, source_target_pairs={{0,96},{32,0},{64,32},{96,64},{1,97},{33,1},{65,33},{97,65},{2,98}... | collective-permute-start | bytes 1376264 | tf_op jit(solution)/shard_map/ppermute | solution.py:19
  106.9 13.0 %collective-permute-start.4 = (bf16[2,128,896]{2,1,0:T(8,128)(2,1)S(1)}, bf16[2,128,896]{2,1,0:T(8,128)(2,1)}, u32[]{:S(2)}, u32[]{:S(2)}) collective-permute-start(bf16[2,128,896]{2,1,0:T(8,128)(2,1)S(1)} %get-tuple-element.74), channel_id=1, source_target_pairs={{0,32},{32,64},{64,96},{96,0},{1,33},{33,65},{65,97},{97,1},{2,34}... | collective-permute-start | bytes 1376264 | tf_op jit(solution)/shard_map/ppermute | solution.py:19
  106.9 30.3 %collective-permute-start.3 = (bf16[2,256,896]{2,1,0:T(8,128)(2,1)}, bf16[2,256,896]{2,1,0:T(8,128)(2,1)}, u32[]{:S(2)}, u32[]{:S(2)}) collective-permute-start(bf16[2,256,896]{2,1,0:T(8,128)(2,1)} %get-tuple-element.70), channel_id=1, source_target_pairs={{0,96},{32,0},{64,32},{96,64},{1,97},{33,1},{65,33},{97,65},{2,98}... | collective-permute-start | bytes 2752520 | tf_op jit(solution)/shard_map/ppermute | solution.py:19
  109.5 29.7 %collective-permute-start.2 = (bf16[2,256,896]{2,1,0:T(8,128)(2,1)}, bf16[2,256,896]{2,1,0:T(8,128)(2,1)}, u32[]{:S(2)}, u32[]{:S(2)}) collective-permute-start(bf16[2,256,896]{2,1,0:T(8,128)(2,1)} %get-tuple-element.71), channel_id=1, source_target_pairs={{0,32},{32,64},{64,96},{96,0},{1,33},{33,65},{65,97},{97,1},{2,34}... | collective-permute-start | bytes 2752520 | tf_op jit(solution)/shard_map/ppermute | solution.py:19
  116.3 29.6 %collective-permute-start.7 = (bf16[2,128,896]{2,1,0:T(8,128)(2,1)}, bf16[2,128,896]{2,1,0:T(8,128)(2,1)S(1)}, u32[]{:S(2)}, u32[]{:S(2)}) collective-permute-start(bf16[2,128,896]{2,1,0:T(8,128)(2,1)} %collective-permute-done.6), channel_id=1, source_target_pairs={{0,96},{32,0},{64,32},{96,64},{1,97},{33,1},{65,33},{97,65},{2,98}... | collective-permute-start | bytes 1376264 | tf_op jit(solution)/shard_map/ppermute | solution.py:19
  119.9 29.2 %collective-permute-start.5 = (bf16[2,128,896]{2,1,0:T(8,128)(2,1)}, bf16[2,128,896]{2,1,0:T(8,128)(2,1)}, u32[]{:S(2)}, u32[]{:S(2)}) collective-permute-start(bf16[2,128,896]{2,1,0:T(8,128)(2,1)} %collective-permute-done.4), channel_id=1, source_target_pairs={{0,32},{32,64},{64,96},{96,0},{1,33},{33,65},{65,97},{97,1},{2,34}... | collective-permute-start | bytes 1376264 | tf_op jit(solution)/shard_map/ppermute | solution.py:19
  134.3 18.8 %copy-start.8 = (bf16[64,4096]{1,0:T(8,128)(2,1)S(1)}, bf16[64,4096]{1,0:T(8,128)(2,1)}, u32[]{:S(2)}) copy-start(bf16[64,4096]{1,0:T(8,128)(2,1)} %reduce-scatter.2.cloned.1.call-done) | copy-start | bytes 1572868
  134.3 18.8 %collective-permute-start = (bf16[32,4096]{1,0:T(8,128)(2,1)S(1)}, bf16[32,4096]{1,0:T(8,128)(2,1)S(1)}, u32[]{:S(2)}, u32[]{:S(2)}) collective-permute-start(bf16[32,4096]{1,0:T(8,128)(2,1)S(1)} %constant_dynamic-slice_fusion), channel_id=1, source_target_pairs={{0,1},{1,0},{2,3},{3,2},{4,5},{5,4},{6,7},{7,6},{8,9},{9,8},{10,11... | collective-permute-start | bytes 786440 | tf_op jit(solution)/shard_map/ppermute | solution.py:19
  151.8 10.6 %collective-permute-start.8 = (bf16[256,896]{1,0:T(8,128)(2,1)S(1)}, bf16[256,896]{1,0:T(8,128)(2,1)S(1)}, u32[]{:S(2)}, u32[]{:S(2)}) collective-permute-start(bf16[256,896]{1,0:T(8,128)(2,1)S(1)} %fusion.17), channel_id=1, source_target_pairs={{0,128},{128,0},{1,129},{129,1},{2,130},{130,2},{3,131},{131,3},{4... | collective-permute-start | bytes 1376264 | tf_op jit(solution)/shard_map/ppermute | solution.py:19
Sparse Core Ops, SparseCore 0:
  19.5 56.9 all-gather.1
  79.0 54.0 reduce-scatter.1

commit v8 on v3

--- a/solution.py
+++ b/solution.py
@@ -30,11 +30,10 @@
     dc = lax.axis_index("dc")
     mine = jnp.take(parts, dc, axis=2)
     arrived = exchange(jnp.take(parts, 1 - dc, axis=2), "dc", 2, 1)
-    total = mine.astype(jnp.float32) + arrived.astype(jnp.float32)
-    total = with_layout_constraint(total, Layout(major_to_minor=(0, 1, 2, 3)))
-    sent = total.astype(jnp.bfloat16)
+    sent = (mine.astype(jnp.float32) + arrived.astype(jnp.float32)).astype(jnp.bfloat16)
+    sent = with_layout_constraint(sent, Layout(major_to_minor=(0, 1, 2, 3)))
     dx = lax.axis_index("dx")
-    acc = jnp.take(total, dx, axis=1)
+    acc = jnp.take(sent, dx, axis=1).astype(jnp.float32)
     for shift in range(1, n_x):
         block = jnp.take(sent, (dx + shift) % n_x, axis=1)
         acc = acc + exchange(block, "dx", n_x, shift).astype(jnp.float32)

time: 171 us -> 172 us (level)
    convert_element_type x0 -> x1, other arithmetic: none -> 4.49 us  [weight_gradient(): (mine.astype(jnp.float32) + arrived.astype(jnp.float32)).astype(jnp.bfloa...]
    add x1 -> x0, other arithmetic: 4.36 us -> none  [weight_gradient(): total = mine.astype(jnp.float32) + arrived.astype(jnp.float32)]
  transfers between devices with their start and end apart: 8 -> 8, of which waited for: 5 -> 5; matrix products, arithmetic and copies ran while one was open for 26% -> 25% of each run, Pallas kernels for 0% -> 0%
where the time goes in v8:
time: 172 us
  waiting for transfers between devices  84.9 us (49%)
  matrix products  21.2 us (12%)
  other arithmetic  15.7 us (9%)
  local copies, waits for them, and re-layouts  15.2 us (9%)
  between operations  14.2 us (8%)
  blocking collectives  12.1 us (7%)
  starting transfers between devices  8.58 us (5%)
    all_gather x1, waiting for transfers between devices, per_device(): cotangent = lax.all_gather(cotangent, 'tz', axis=0, tiled=True)  39.5 us
    ppermute x6, waiting for transfers between devices, exchange(): return lax.ppermute(value, axis, perm)  28.8 us
    reduce_scatter x1, waiting for transfers between devices, per_device(): out = lax.psum_scatter(partial_out, 'tz', scatter_dimension=0, tiled=True)  16.5 us
    unnamed x35, local copies, waits for them, and re-layouts  14.2 us
    all_gather x1, blocking collectives, per_device(): cotangent = lax.all_gather(grad_out, 'ty', axis=0, tiled=True)  12.1 us
    ppermute x6, starting transfers between devices, exchange(): return lax.ppermute(value, axis, perm)  8.5 us
    dot_general x1, matrix products, per_device(): jnp.dot(hidden, weight, preferred_element_type=jnp.float32)  8.1 us
    dot_general x1, matrix products, weight_gradient(): lax.dot_general(cotangent, hidden, (((0,), (0,)), ((), ())), preferred_el...  7.19 us
  transfers between devices with their start and end apart: 8, of which 5 were waited for; matrix products, arithmetic and copies ran while one was open for 25% of the time, Pallas kernels for 0%

profile of v8, /device:TPU:1, one launch (start us, length us, event | category | flops | bytes accessed | tf_op | source)
XLA Modules:
  0.0 171.9 jit_solution(8435106643145560429)
XLA Ops:
  7.2 12.1 %all_gather.6 = bf16[64,4096]{1,0:T(8,128)(2,1)} all-gather(bf16[32,4096]{1,0:T(8,128)(2,1)} %param.11), channel_id=1, replica_groups=mesh['dy'=2,'dx'=4,'dc'=2,'tz'=8,'ty'=2] {'ty'}, dimensions={0}, use_global_device_ids=true | all-gather | bytes 786432 | tf_op jit(solution)/shard_map/all_gather | solution.py:61
  19.5 1.3 copy.19
  20.8 1.3 copy.18
  22.0 0.1 exponential_convert_fusion
  22.2 3.7 %bitcast_multiply_fusion = bf16[896,4096]{1,0:T(8,128)(2,1)S(1)} fusion(bf16[896,4096]{1,0:T(8,128)(2,1)} %param.12, bf16[28,4096]{1,0:T(8,128)(2,1)S(1)} %exponential_convert_fusion), kind=kLoop, calls=%fused_computation | loop fusion | flops 3670016 | bytes 14909440 | tf_op jit(solution)/shard_map/mul | solution.py:13
  25.8 2.9 %copy-done.1 = bf16[896,4096]{1,0:T(8,128)(2,1)} copy-done((bf16[896,4096]{1,0:T(8,128)(2,1)}, bf16[896,4096]{1,0:T(8,128)(2,1)S(1)}, u32[]{:S(2)}) %copy-start.1) | copy-done | bytes 7340056
  28.8 8.1 %convolution_convert_fusion.1 = bf16[512,4096]{1,0:T(8,128)(2,1)} fusion(bf16[896,4096]{1,0:T(8,128)(2,1)S(1)} %bitcast_multiply_fusion, bf16[512,896]{0,1:T(8,128)(2,1)} %copy.19, bf16[512,896]{0,1:T(8,128)(2,1)} %copy.18), kind=kOutput, calls=%fused_computation.3 | convolution fusion | flops 3763863552 | bytes 13369344 | tf_op jit(solution)/shard_map/dot_general | solution.py:53
  36.9 39.5 %all-gather.2.cloned.1.call-done = bf16[512,4096]{1,0:T(8,128)(2,1)} async-done(((bf16[64,4096]{1,0:T(8,128)(2,1)}), bf16[512,4096]{1,0:T(8,128)(2,1)}) %all-gather.2.cloned.1.call-update) | async-done | bytes 4194320 | tf_op jit(solution)/shard_map/all_gather | solution.py:62
  76.5 7.2 %convolution_convert_fusion = bf16[896,4096]{0,1:T(8,128)(2,1)S(1)} fusion(bf16[512,4096]{1,0:T(8,128)(2,1)} %all-gather.2.cloned.1.call-done, bf16[512,896]{0,1:T(8,128)(2,1)S(1)} %copy-done.5, bf16[512,896]{0,1:T(8,128)(2,1)S(1)} %copy-done.7), kind=kOutput, calls=%fused_computation.2 | convolution fusion | flops 3765436416 | bytes 13369344 | tf_op jit(solution)/shard_map/dot_general | solution.py:25
  83.7 3.0 %copy-done.2 = bf16[896,4096]{0,1:T(8,128)(2,1)} copy-done((bf16[896,4096]{0,1:T(8,128)(2,1)}, bf16[896,4096]{0,1:T(8,128)(2,1)S(1)}, u32[]{:S(2)}) %copy-start.2) | copy-done | bytes 7340056
  86.7 2.3 %fusion = bf16[2,4,256,896]{3,2,1,0:T(8,128)(2,1)} fusion(bf16[2,4,2,256,896]{4,3,2,1,0:T(8,128)(2,1)S(1)} %bitcast.68, s32[]{:T(128)S(6)} %select_n.82, pred[]{:T(512)S(6)} %and.49), kind=kLoop, calls=%fused_computation.5 | loop fusion | flops 1835008 | bytes 7340037 | tf_op jit(solution)/shard_map/jit(_take)/select_n | solution.py:32
  89.0 0.8 collective-permute-start.1
  89.8 6.4 %collective-permute-done.1 = bf16[2,4,256,896]{3,2,1,0:T(8,128)(2,1)} collective-permute-done((bf16[2,4,256,896]{3,2,1,0:T(8,128)(2,1)}, bf16[2,4,256,896]{3,2,1,0:T(8,128)(2,1)}, u32[]{:S(2)}, u32[]{:S(2)}) %collective-permute-start.1) | collective-permute-done | bytes 3670048 | tf_op jit(solution)/shard_map/ppermute | solution.py:19
  96.2 4.5 %add_convert_fusion = bf16[2,4,256,896]{3,2,1,0:T(8,128)(2,1)S(1)} fusion(bf16[2,4,256,896]{3,2,1,0:T(8,128)(2,1)} %collective-permute-done.1, bf16[2,4,2,256,896]{4,3,2,1,0:T(8,128)(2,1)} %bitcast.69, s32[]{:T(128)S(6)} %select_n.80, pred[]{:T(512)S(6)} %and.48), kind=kLoop, calls=%fused_computation.1 | loop fusion | flops 9175040 | bytes 11010053 | tf_op jit(solution)/shard_map/convert_element_type | solution.py:33
  100.7 1.7 fusion.14
  102.4 1.1 copy-done
  103.5 2.4 %collective-permute-start.4 = (bf16[2,256,896]{2,1,0:T(8,128)(2,1)}, bf16[2,256,896]{2,1,0:T(8,128)(2,1)}, u32[]{:S(2)}, u32[]{:S(2)}) collective-permute-start(bf16[2,256,896]{2,1,0:T(8,128)(2,1)} %get-tuple-element.60), channel_id=1, source_target_pairs={{0,96},{32,0},{64,32},{96,64},{1,97},{33,1},{65,33},{97,65},{2,98}... | collective-permute-start | bytes 2752520 | tf_op jit(solution)/shard_map/ppermute | solution.py:19
  105.9 0.6 collective-permute-start.3
  106.5 0.6 collective-permute-start.2
  107.1 5.9 %fusion.11 = (bf16[512,896]{0,1:T(8,128)(2,1)}, bf16[512,896]{0,1:T(8,128)(2,1)}) fusion(bf16[512,896]{0,1:T(8,128)(2,1)S(1)} %copy-done.8, bf16[512,896]{0,1:T(8,128)(2,1)S(1)} %copy-done.6, bf16[896,4096]{1,0:T(8,128)(2,1)S(1)} %bitcast.67, bf16[512,4096]{1,0:T(8,128)(2,1)S(1)} %copy-done.12), kind=kOutput, calls=%fused_computation.23 | convolution fusion | flops 3764977664 | bytes 15204352 | tf_op jit(solution)/shard_map/dot_general | solution.py:63
  112.9 2.3 %copy.26 = bf16[512,896]{1,0:T(8,128)(2,1)} copy(bf16[512,896]{0,1:T(8,128)(2,1)} %get-tuple-element.62) | data formatting | bytes 1835008
  115.2 1.3 copy.27
  116.5 16.5 %reduce-scatter.2.cloned.1.call-done = bf16[64,4096]{1,0:T(8,128)(2,1)} async-done(((bf16[512,4096]{1,0:T(8,128)(2,1)}), bf16[64,4096]{1,0:T(8,128)(2,1)}) %reduce-scatter.2.cloned.1.call-update) | async-done | bytes 524304 | tf_op jit(solution)/shard_map/reduce_scatter | solution.py:54
  133.0 1.0 constant_dynamic-slice_fusion
  134.0 2.8 %collective-permute-start = (bf16[32,4096]{1,0:T(8,128)(2,1)S(1)}, bf16[32,4096]{1,0:T(8,128)(2,1)S(1)}, u32[]{:S(2)}, u32[]{:S(2)}) collective-permute-start(bf16[32,4096]{1,0:T(8,128)(2,1)S(1)} %constant_dynamic-slice_fusion), channel_id=1, source_target_pairs={{0,1},{1,0},{2,3},{3,2},{4,5},{5,4},{6,7},{7,6},{8,9},{9,8},{10,11... | collective-permute-start | bytes 786440 | tf_op jit(solution)/shard_map/ppermute | solution.py:19
  136.9 12.8 %collective-permute-done.2 = bf16[2,256,896]{2,1,0:T(8,128)(2,1)} collective-permute-done((bf16[2,256,896]{2,1,0:T(8,128)(2,1)}, bf16[2,256,896]{2,1,0:T(8,128)(2,1)}, u32[]{:S(2)}, u32[]{:S(2)}) %collective-permute-start.2) | collective-permute-done | bytes 917536 | tf_op jit(solution)/shard_map/ppermute | solution.py:19
  149.7 2.5 %convert_add_fusion = f32[2,256,896]{2,1,0:T(8,128)S(1)} fusion(bf16[2,256,896]{2,1,0:T(8,128)(2,1)} %collective-permute-done.4, bf16[2,256,896]{2,1,0:T(8,128)(2,1)} %collective-permute-done.3, bf16[2,256,896]{2,1,0:T(8,128)(2,1)} %collective-permute-done.2, bf16[2,4,256,896]{3,2,1,0:T(8,128)(2,1)} %copy-done, s32[]{:T(128)S(6)} %select_n.84, pred[]{:T(512)S(6)} %and.50), kind=kLoop, calls=%fused_computation.24 | loop fusion | flops 3670016 | bytes 5505029 | tf_op jit(solution)/shard_map/add | solution.py:39
  152.2 1.3 collective-permute-start.5
  153.5 0.8 add_convert_fusion.1
  154.3 9.6 %collective-permute-done.5 = bf16[256,896]{1,0:T(8,128)(2,1)S(1)} collective-permute-done((bf16[256,896]{1,0:T(8,128)(2,1)S(1)}, bf16[256,896]{1,0:T(8,128)(2,1)S(1)}, u32[]{:S(2)}, u32[]{:S(2)}) %collective-permute-start.5) | collective-permute-done | bytes 458784 | tf_op jit(solution)/shard_map/ppermute | solution.py:19
  163.9 0.1 fusion.17
  164.0 1.0 copy.28
  (36 shorter events, 0.3 us)
Async XLA Ops:
  7.2 12.3 %copy-start.3 = (bf16[512,896]{1,0:T(8,128)(2,1)S(1)}, bf16[512,896]{1,0:T(8,128)(2,1)}, u32[]{:S(2)}) copy-start(bf16[512,896]{1,0:T(8,128)(2,1)} %param.10) | copy-start | bytes 2752516
  7.2 13.6 %copy-start.4 = (bf16[512,896]{1,0:T(8,128)(2,1)S(1)}, bf16[512,896]{1,0:T(8,128)(2,1)}, u32[]{:S(2)}) copy-start(bf16[512,896]{1,0:T(8,128)(2,1)} %param.9) | copy-start | bytes 2752516
  7.2 69.3 %all-gather.2.cloned.1.call-start = ((), (), s32[]{:S(2)}) async-start(), calls=%async_computation.2 | async-start | bytes 4718592 | tf_op jit(solution)/shard_map/all_gather | solution.py:62
  19.4 2.6 %copy-start.10 = (s32[28,4096]{1,0:T(8,128)S(1)}, s32[28,4096]{1,0:T(8,128)}, u32[]{:S(2)}) copy-start(s32[28,4096]{1,0:T(8,128)} %param.13) | copy-start | bytes 1376260
  19.4 113.6 %reduce-scatter.2.cloned.1.call-start = ((), (), s32[]{:S(2)}) async-start(), calls=%async_computation.1 | async-start | bytes 4718592 | tf_op jit(solution)/shard_map/reduce_scatter | solution.py:54
  25.8 2.9 %copy-start.1 = (bf16[896,4096]{1,0:T(8,128)(2,1)}, bf16[896,4096]{1,0:T(8,128)(2,1)S(1)}, u32[]{:S(2)}) copy-start(bf16[896,4096]{1,0:T(8,128)(2,1)S(1)} %bitcast_multiply_fusion) | copy-start | bytes 22020100
  36.9 39.6 %copy-start.5 = (bf16[512,896]{0,1:T(8,128)(2,1)S(1)}, bf16[512,896]{0,1:T(8,128)(2,1)}, u32[]{:S(2)}) copy-start(bf16[512,896]{0,1:T(8,128)(2,1)} %copy.19) | copy-start | bytes 2752516
  36.9 39.6 %copy-start.7 = (bf16[512,896]{0,1:T(8,128)(2,1)S(1)}, bf16[512,896]{0,1:T(8,128)(2,1)}, u32[]{:S(2)}) copy-start(bf16[512,896]{0,1:T(8,128)(2,1)} %copy.18) | copy-start | bytes 2752516
  83.7 3.0 %copy-start.2 = (bf16[896,4096]{0,1:T(8,128)(2,1)}, bf16[896,4096]{0,1:T(8,128)(2,1)S(1)}, u32[]{:S(2)}) copy-start(bf16[896,4096]{0,1:T(8,128)(2,1)S(1)} %convolution_convert_fusion) | copy-start | bytes 22020100
  86.7 20.4 %slice-start = ((s8[7340032]{0:T(1024)(128)(4,1)}), s8[3145728]{0:T(1024)(128)(4,1)S(1)}, s32[]{:S(2)}) async-start(s8[7340032]{0:T(1024)(128)(4,1)} %bitcast.66), calls=%async_computation.3 | async-start | bytes 6291456
  89.0 7.2 %collective-permute-start.1 = (bf16[2,4,256,896]{3,2,1,0:T(8,128)(2,1)}, bf16[2,4,256,896]{3,2,1,0:T(8,128)(2,1)}, u32[]{:S(2)}, u32[]{:S(2)}) collective-permute-start(bf16[2,4,256,896]{3,2,1,0:T(8,128)(2,1)} %fusion), channel_id=1, source_target_pairs={{0,16},{16,0},{1,17},{17,1},{2,18},{18,2},{3,19},{19,3},{4,20},{20... | collective-permute-start | bytes 11010056 | tf_op jit(solution)/shard_map/ppermute | solution.py:19
  89.8 17.2 %slice-start.1 = ((s8[7340032]{0:T(1024)(128)(4,1)}), s8[4194304]{0:T(1024)(128)(4,1)S(1)}, s32[]{:S(2)}) async-start(s8[7340032]{0:T(1024)(128)(4,1)} %bitcast.66), calls=%async_computation.4 | async-start | bytes 8388608
  96.2 10.9 %copy-start.12 = (bf16[512,4096]{1,0:T(8,128)(2,1)S(1)}, bf16[512,4096]{1,0:T(8,128)(2,1)}, u32[]{:S(2)}) copy-start(bf16[512,4096]{1,0:T(8,128)(2,1)} %all-gather.2.cloned.1.call-done) | copy-start | bytes 12582916
  100.7 2.8 %copy-start = (bf16[2,4,256,896]{3,2,1,0:T(8,128)(2,1)}, bf16[2,4,256,896]{3,2,1,0:T(8,128)(2,1)S(1)}, u32[]{:S(2)}) copy-start(bf16[2,4,256,896]{3,2,1,0:T(8,128)(2,1)S(1)} %add_convert_fusion) | copy-start | bytes 11010052
  100.7 6.4 %copy-start.6 = (bf16[512,896]{0,1:T(8,128)(2,1)S(1)}, bf16[512,896]{0,1:T(8,128)(2,1)}, u32[]{:S(2)}) copy-start(bf16[512,896]{0,1:T(8,128)(2,1)} %copy.19) | copy-start | bytes 2752516
  100.7 6.3 %copy-start.8 = (bf16[512,896]{0,1:T(8,128)(2,1)S(1)}, bf16[512,896]{0,1:T(8,128)(2,1)}, u32[]{:S(2)}) copy-start(bf16[512,896]{0,1:T(8,128)(2,1)} %copy.18) | copy-start | bytes 2752516
  103.5 33.4 %collective-permute-start.4 = (bf16[2,256,896]{2,1,0:T(8,128)(2,1)}, bf16[2,256,896]{2,1,0:T(8,128)(2,1)}, u32[]{:S(2)}, u32[]{:S(2)}) collective-permute-start(bf16[2,256,896]{2,1,0:T(8,128)(2,1)} %get-tuple-element.60), channel_id=1, source_target_pairs={{0,96},{32,0},{64,32},{96,64},{1,97},{33,1},{65,33},{97,65},{2,98}... | collective-permute-start | bytes 2752520 | tf_op jit(solution)/shard_map/ppermute | solution.py:19
  105.9 31.0 %collective-permute-start.3 = (bf16[2,256,896]{2,1,0:T(8,128)(2,1)}, bf16[2,256,896]{2,1,0:T(8,128)(2,1)}, u32[]{:S(2)}, u32[]{:S(2)}) collective-permute-start(bf16[2,256,896]{2,1,0:T(8,128)(2,1)} %get-tuple-element.59), channel_id=1, source_target_pairs={{0,64},{32,96},{64,0},{96,32},{1,65},{33,97},{65,1},{97,33},{2,66}... | collective-permute-start | bytes 2752520 | tf_op jit(solution)/shard_map/ppermute | solution.py:19
  106.5 43.2 %collective-permute-start.2 = (bf16[2,256,896]{2,1,0:T(8,128)(2,1)}, bf16[2,256,896]{2,1,0:T(8,128)(2,1)}, u32[]{:S(2)}, u32[]{:S(2)}) collective-permute-start(bf16[2,256,896]{2,1,0:T(8,128)(2,1)} %get-tuple-element.58), channel_id=1, source_target_pairs={{0,32},{32,64},{64,96},{96,0},{1,33},{33,65},{65,97},{97,1},{2,34}... | collective-permute-start | bytes 2752520 | tf_op jit(solution)/shard_map/ppermute | solution.py:19
  112.9 2.3 %copy-start.9 = (bf16[512,896]{0,1:T(8,128)(2,1)S(1)}, bf16[512,896]{0,1:T(8,128)(2,1)}, u32[]{:S(2)}) copy-start(bf16[512,896]{0,1:T(8,128)(2,1)} %get-tuple-element.61) | copy-start | bytes 2752516
  134.0 19.5 %copy-start.11 = (bf16[64,4096]{1,0:T(8,128)(2,1)S(1)}, bf16[64,4096]{1,0:T(8,128)(2,1)}, u32[]{:S(2)}) copy-start(bf16[64,4096]{1,0:T(8,128)(2,1)} %reduce-scatter.2.cloned.1.call-done) | copy-start | bytes 1572868
  134.0 19.5 %collective-permute-start = (bf16[32,4096]{1,0:T(8,128)(2,1)S(1)}, bf16[32,4096]{1,0:T(8,128)(2,1)S(1)}, u32[]{:S(2)}, u32[]{:S(2)}) collective-permute-start(bf16[32,4096]{1,0:T(8,128)(2,1)S(1)} %constant_dynamic-slice_fusion), channel_id=1, source_target_pairs={{0,1},{1,0},{2,3},{3,2},{4,5},{5,4},{6,7},{7,6},{8,9},{9,8},{10,11... | collective-permute-start | bytes 786440 | tf_op jit(solution)/shard_map/ppermute | solution.py:19
  152.2 11.7 %collective-permute-start.5 = (bf16[256,896]{1,0:T(8,128)(2,1)S(1)}, bf16[256,896]{1,0:T(8,128)(2,1)S(1)}, u32[]{:S(2)}, u32[]{:S(2)}) collective-permute-start(bf16[256,896]{1,0:T(8,128)(2,1)S(1)} %fusion.19), channel_id=1, source_target_pairs={{0,128},{128,0},{1,129},{129,1},{2,130},{130,2},{3,131},{131,3},{4... | collective-permute-start | bytes 1376264 | tf_op jit(solution)/shard_map/ppermute | solution.py:19
Sparse Core Ops, SparseCore 0:
  19.5 56.8 all-gather.1
  79.0 54.0 reduce-scatter.1

commit v9 on v3

--- a/solution.py
+++ b/solution.py
@@ -32,15 +32,15 @@
     arrived = exchange(jnp.take(parts, 1 - dc, axis=2), "dc", 2, 1)
     total = mine.astype(jnp.float32) + arrived.astype(jnp.float32)
     total = with_layout_constraint(total, Layout(major_to_minor=(0, 1, 2, 3)))
+    dy = lax.axis_index("dy")
+    sent = total.astype(jnp.bfloat16)
+    total = jnp.take(total, dy, axis=0) + exchange(jnp.take(sent, 1 - dy, axis=0), "dy", 2, 1).astype(jnp.float32)
     sent = total.astype(jnp.bfloat16)
     dx = lax.axis_index("dx")
-    acc = jnp.take(total, dx, axis=1)
+    acc = jnp.take(total, dx, axis=0)
     for shift in range(1, n_x):
-        block = jnp.take(sent, (dx + shift) % n_x, axis=1)
+        block = jnp.take(sent, (dx + shift) % n_x, axis=0)
         acc = acc + exchange(block, "dx", n_x, shift).astype(jnp.float32)
-    dy = lax.axis_index("dy")
-    sent = acc.astype(jnp.bfloat16)
-    acc = jnp.take(acc, dy, axis=0) + exchange(jnp.take(sent, 1 - dy, axis=0), "dy", 2, 1).astype(jnp.float32)
     acc = with_layout_constraint(acc.astype(jnp.bfloat16), Layout(major_to_minor=(0, 1)))
     return acc.T
 

time: 171 us -> 182 us (1.064)
  matrix products: 21.2 us -> 25.8 us
  local copies, waits for them, and re-layouts: 14.1 us -> 17.7 us
  waiting for transfers between devices: 84.9 us -> 88.2 us
    ppermute x6, waiting for transfers between devices: 27.5 us -> 35.7 us  [exchange(): return lax.ppermute(value, axis, perm)]
    dot_general x1, matrix products: 5.85 us -> 10.5 us  [per_device(): lax.dot_general(cotangent, weight, (((1,), (1,)), ((), ())), preferred_el...]
    reduce_scatter x1, waiting for transfers between devices: 17.8 us -> 13.9 us  [per_device(): out = lax.psum_scatter(partial_out, 'tz', scatter_dimension=0, tiled=True)]
    unnamed x35 -> x21, local copies, waits for them, and re-layouts: 13.1 us -> 16.7 us
    convert_element_type x0 -> x1, other arithmetic: none -> 3.16 us  [weight_gradient(): sent = total.astype(jnp.bfloat16)]
    add x1 -> x0, other arithmetic: 2.76 us -> none  [weight_gradient(): acc = acc + exchange(block, 'dx', n_x, shift).astype(jnp.float32)]
  transfers between devices with their start and end apart: 8 -> 8, of which waited for: 5 -> 8; matrix products, arithmetic and copies ran while one was open for 26% -> 27% of each run, Pallas kernels for 0% -> 0%
where the time goes in v9:
time: 182 us
  waiting for transfers between devices  88.2 us (48%)
  matrix products  25.8 us (14%)
  local copies, waits for them, and re-layouts  17.7 us (10%)
  other arithmetic  15.1 us (8%)
  between operations  14.2 us (8%)
  blocking collectives  12.1 us (7%)
  starting transfers between devices  8.86 us (5%)
    all_gather x1, waiting for transfers between devices, per_device(): cotangent = lax.all_gather(cotangent, 'tz', axis=0, tiled=True)  38.7 us
    ppermute x6, waiting for transfers between devices, exchange(): return lax.ppermute(value, axis, perm)  35.7 us
    unnamed x21, local copies, waits for them, and re-layouts  16.7 us
    reduce_scatter x1, waiting for transfers between devices, per_device(): out = lax.psum_scatter(partial_out, 'tz', scatter_dimension=0, tiled=True)  13.9 us
    all_gather x1, blocking collectives, per_device(): cotangent = lax.all_gather(grad_out, 'ty', axis=0, tiled=True)  12.1 us
    dot_general x1, matrix products, per_device(): lax.dot_general(cotangent, weight, (((1,), (1,)), ((), ())), preferred_el...  10.5 us
    ppermute x6, starting transfers between devices, exchange(): return lax.ppermute(value, axis, perm)  8.78 us
    dot_general x1, matrix products, per_device(): jnp.dot(hidden, weight, preferred_element_type=jnp.float32)  8.09 us
  transfers between devices with their start and end apart: 8, of which 8 were waited for; matrix products, arithmetic and copies ran while one was open for 27% of the time, Pallas kernels for 0%

profile of v9, /device:TPU:1, one launch (start us, length us, event | category | flops | bytes accessed | tf_op | source)
XLA Modules:
  0.0 182.0 jit_solution(12885139033214796383)
XLA Ops:
  7.2 12.1 %all_gather.6 = bf16[64,4096]{1,0:T(8,128)(2,1)} all-gather(bf16[32,4096]{1,0:T(8,128)(2,1)} %param.11), channel_id=1, replica_groups=mesh['dy'=2,'dx'=4,'dc'=2,'tz'=8,'ty'=2] {'ty'}, dimensions={0}, use_global_device_ids=true | all-gather | bytes 786432 | tf_op jit(solution)/shard_map/all_gather | solution.py:62
  19.4 2.2 %copy.15 = bf16[512,896]{0,1:T(8,128)(2,1)} copy(bf16[512,896]{1,0:T(8,128)(2,1)} %param.10) | data formatting | bytes 1835008 | tf_op args[1]
  21.6 1.3 copy.14
  23.0 3.7 %bitcast_multiply_fusion = bf16[896,4096]{1,0:T(8,128)(2,1)S(1)} fusion(bf16[896,4096]{1,0:T(8,128)(2,1)} %param.12, bf16[28,4096]{1,0:T(8,128)(2,1)S(1)} %exponential_convert_fusion), kind=kLoop, calls=%fused_computation | loop fusion | flops 3670016 | bytes 14909440 | tf_op jit(solution)/shard_map/mul | solution.py:13
  26.7 2.9 %copy-done.1 = bf16[896,4096]{1,0:T(8,128)(2,1)} copy-done((bf16[896,4096]{1,0:T(8,128)(2,1)}, bf16[896,4096]{1,0:T(8,128)(2,1)S(1)}, u32[]{:S(2)}) %copy-start.1) | copy-done | bytes 7340056
  29.7 8.1 %convolution_convert_fusion.1 = bf16[512,4096]{1,0:T(8,128)(2,1)} fusion(bf16[896,4096]{1,0:T(8,128)(2,1)S(1)} %bitcast_multiply_fusion, bf16[512,896]{0,1:T(8,128)(2,1)} %copy.15, bf16[512,896]{0,1:T(8,128)(2,1)} %copy.14), kind=kOutput, calls=%fused_computation.3 | convolution fusion | flops 3763863552 | bytes 13369344 | tf_op jit(solution)/shard_map/dot_general | solution.py:54
  37.8 38.7 %all-gather.2.cloned.1.call-done = bf16[512,4096]{1,0:T(8,128)(2,1)} async-done(((bf16[64,4096]{1,0:T(8,128)(2,1)}), bf16[512,4096]{1,0:T(8,128)(2,1)}) %all-gather.2.cloned.1.call-update) | async-done | bytes 4194320 | tf_op jit(solution)/shard_map/all_gather | solution.py:63
  76.5 7.2 %convolution_convert_fusion = bf16[896,4096]{0,1:T(8,128)(2,1)S(1)} fusion(bf16[512,4096]{1,0:T(8,128)(2,1)} %all-gather.2.cloned.1.call-done, bf16[512,896]{0,1:T(8,128)(2,1)S(1)} %copy-done.4, bf16[512,896]{0,1:T(8,128)(2,1)S(1)} %copy-done.5), kind=kOutput, calls=%fused_computation.2 | convolution fusion | flops 3765436416 | bytes 13369344 | tf_op jit(solution)/shard_map/dot_general | solution.py:25
  83.7 2.5 %fusion = bf16[2,4,256,896]{3,2,1,0:T(8,128)(2,1)} fusion(bf16[2,4,2,256,896]{4,3,2,1,0:T(8,128)(2,1)S(1)} %bitcast.51, s32[]{:T(128)S(6)} %select_n.86, pred[]{:T(512)S(6)} %and.53), kind=kLoop, calls=%fused_computation.6 | loop fusion | flops 1835008 | bytes 7340037 | tf_op jit(solution)/shard_map/jit(_take)/select_n | solution.py:32
  86.2 1.8 copy-done.2
  88.0 0.8 collective-permute-start.1
  88.9 6.4 %collective-permute-done.1 = bf16[2,4,256,896]{3,2,1,0:T(8,128)(2,1)} collective-permute-done((bf16[2,4,256,896]{3,2,1,0:T(8,128)(2,1)}, bf16[2,4,256,896]{3,2,1,0:T(8,128)(2,1)}, u32[]{:S(2)}, u32[]{:S(2)}) %collective-permute-start.1) | collective-permute-done | bytes 3670048 | tf_op jit(solution)/shard_map/ppermute | solution.py:19
  95.2 4.2 %convert_add_fusion = f32[2,4,256,896]{3,2,1,0:T(8,128)S(1)} fusion(bf16[2,4,256,896]{3,2,1,0:T(8,128)(2,1)} %collective-permute-done.1, bf16[2,4,2,256,896]{4,3,2,1,0:T(8,128)(2,1)} %bitcast.52, s32[]{:T(128)S(6)} %select_n.84, pred[]{:T(512)S(6)} %and.52), kind=kLoop, calls=%fused_computation.1 | loop fusion | flops 7340032 | bytes 14680069 | tf_op jit(solution)/shard_map/add | solution.py:33
  99.5 3.0 %copy-done = f32[2,4,256,896]{3,2,1,0:T(8,128)} copy-done((f32[2,4,256,896]{3,2,1,0:T(8,128)}, f32[2,4,256,896]{3,2,1,0:T(8,128)S(1)}, u32[]{:S(2)}) %copy-start) | copy-done | bytes 7340056
  102.7 1.5 collective-permute-start.2
  104.2 10.5 %fusion.11 = (bf16[512,896]{0,1:T(8,128)(2,1)}, bf16[512,896]{0,1:T(8,128)(2,1)}) fusion(bf16[512,896]{0,1:T(8,128)(2,1)} %copy.14, bf16[512,896]{0,1:T(8,128)(2,1)S(1)} %copy-done.4, bf16[896,4096]{1,0:T(8,128)(2,1)} %copy-done.1, bf16[512,4096]{1,0:T(8,128)(2,1)} %all-gather.2.cloned.1.call-done), kind=kOutput, calls=%fused_computation.25 | convolution fusion | flops 3764977664 | bytes 15204352 | tf_op jit(solution)/shard_map/dot_general | solution.py:64
  114.7 2.2 %copy.18 = bf16[512,896]{1,0:T(8,128)(2,1)} copy(bf16[512,896]{0,1:T(8,128)(2,1)} %get-tuple-element.72) | data formatting | bytes 1835008
  117.0 2.2 %copy.19 = bf16[512,896]{1,0:T(8,128)(2,1)} copy(bf16[512,896]{0,1:T(8,128)(2,1)} %get-tuple-element.71) | data formatting | bytes 1835008
  119.2 13.9 %reduce-scatter.2.cloned.1.call-done = bf16[64,4096]{1,0:T(8,128)(2,1)} async-done(((bf16[512,4096]{1,0:T(8,128)(2,1)}), bf16[64,4096]{1,0:T(8,128)(2,1)}) %reduce-scatter.2.cloned.1.call-update) | async-done | bytes 524304 | tf_op jit(solution)/shard_map/reduce_scatter | solution.py:55
  133.0 1.0 constant_dynamic-slice_fusion
  134.0 2.8 %collective-permute-start = (bf16[32,4096]{1,0:T(8,128)(2,1)S(1)}, bf16[32,4096]{1,0:T(8,128)(2,1)S(1)}, u32[]{:S(2)}, u32[]{:S(2)}) collective-permute-start(bf16[32,4096]{1,0:T(8,128)(2,1)S(1)} %constant_dynamic-slice_fusion), channel_id=1, source_target_pairs={{0,1},{1,0},{2,3},{3,2},{4,5},{5,4},{6,7},{7,6},{8,9},{9,8},{10,11... | collective-permute-start | bytes 786440 | tf_op jit(solution)/shard_map/ppermute | solution.py:19
  136.8 7.4 %collective-permute-done.2 = bf16[4,256,896]{2,1,0:T(8,128)(2,1)} collective-permute-done((bf16[4,256,896]{2,1,0:T(8,128)(2,1)S(1)}, bf16[4,256,896]{2,1,0:T(8,128)(2,1)}, u32[]{:S(2)}, u32[]{:S(2)}) %collective-permute-start.2) | collective-permute-done | bytes 1835040 | tf_op jit(solution)/shard_map/ppermute | solution.py:19
  144.3 3.2 %fusion.20 = (bf16[4,256,896]{2,1,0:T(8,128)(2,1)S(1)}, f32[4,256,896]{2,1,0:T(8,128)S(1)}) fusion(bf16[4,256,896]{2,1,0:T(8,128)(2,1)} %collective-permute-done.2, f32[2,4,256,896]{3,2,1,0:T(8,128)} %copy-done, s32[]{:T(128)S(6)} %select_n.60, pred[]{:T(512)S(6)} %and.50), kind=kLoop, calls=%fused_computation.39 | loop fusion | flops 3670016 | bytes 11010053 | tf_op jit(solution)/shard_map/convert_element_type | solution.py:38
  147.6 2.5 %collective-permute-start.5 = (bf16[256,896]{1,0:T(8,128)(2,1)S(1)}, bf16[256,896]{1,0:T(8,128)(2,1)S(1)}, u32[]{:S(2)}, u32[]{:S(2)}) collective-permute-start(bf16[256,896]{1,0:T(8,128)(2,1)S(1)} %get-tuple-element.74), channel_id=1, source_target_pairs={{0,96},{32,0},{64,32},{96,64},{1,97},{33,1},{65,33},{97,65},{2,98}... | collective-permute-start | bytes 1376264 | tf_op jit(solution)/shard_map/ppermute | solution.py:19
  150.1 0.6 collective-permute-start.4
  150.7 0.6 collective-permute-start.3
  151.3 0.7 collective-permute-done
  152.0 0.8 add_convert_fusion
  152.8 5.9 %collective-permute-done.5 = bf16[256,896]{1,0:T(8,128)(2,1)S(1)} collective-permute-done((bf16[256,896]{1,0:T(8,128)(2,1)S(1)}, bf16[256,896]{1,0:T(8,128)(2,1)S(1)}, u32[]{:S(2)}, u32[]{:S(2)}) %collective-permute-start.5) | collective-permute-done | bytes 458784 | tf_op jit(solution)/shard_map/ppermute | solution.py:19
  158.6 2.8 %collective-permute-done.4 = bf16[256,896]{1,0:T(8,128)(2,1)S(1)} collective-permute-done((bf16[256,896]{1,0:T(8,128)(2,1)S(1)}, bf16[256,896]{1,0:T(8,128)(2,1)S(1)}, u32[]{:S(2)}, u32[]{:S(2)}) %collective-permute-start.4) | collective-permute-done | bytes 458784 | tf_op jit(solution)/shard_map/ppermute | solution.py:19
  161.4 12.5 %collective-permute-done.3 = bf16[256,896]{1,0:T(8,128)(2,1)S(1)} collective-permute-done((bf16[256,896]{1,0:T(8,128)(2,1)S(1)}, bf16[256,896]{1,0:T(8,128)(2,1)S(1)}, u32[]{:S(2)}, u32[]{:S(2)}) %collective-permute-start.3) | collective-permute-done | bytes 458784 | tf_op jit(solution)/shard_map/ppermute | solution.py:19
  174.1 1.0 copy.20
  (21 shorter events, 0.9 us)
Async XLA Ops:
  7.2 14.5 %copy-start.3 = (bf16[512,896]{1,0:T(8,128)(2,1)S(1)}, bf16[512,896]{1,0:T(8,128)(2,1)}, u32[]{:S(2)}) copy-start(bf16[512,896]{1,0:T(8,128)(2,1)} %param.9) | copy-start | bytes 2752516
  7.2 15.7 %copy-start.6 = (s32[28,4096]{1,0:T(8,128)S(1)}, s32[28,4096]{1,0:T(8,128)}, u32[]{:S(2)}) copy-start(s32[28,4096]{1,0:T(8,128)} %param.13) | copy-start | bytes 1376260
  7.2 69.3 %all-gather.2.cloned.1.call-start = ((), (), s32[]{:S(2)}) async-start(), calls=%async_computation.2 | async-start | bytes 4718592 | tf_op jit(solution)/shard_map/all_gather | solution.py:63
  19.4 113.7 %reduce-scatter.2.cloned.1.call-start = ((), (), s32[]{:S(2)}) async-start(), calls=%async_computation.1 | async-start | bytes 4718592 | tf_op jit(solution)/shard_map/reduce_scatter | solution.py:55
  26.7 3.0 %copy-start.1 = (bf16[896,4096]{1,0:T(8,128)(2,1)}, bf16[896,4096]{1,0:T(8,128)(2,1)S(1)}, u32[]{:S(2)}) copy-start(bf16[896,4096]{1,0:T(8,128)(2,1)S(1)} %bitcast_multiply_fusion) | copy-start | bytes 22020100
  37.8 38.7 %copy-start.4 = (bf16[512,896]{0,1:T(8,128)(2,1)S(1)}, bf16[512,896]{0,1:T(8,128)(2,1)}, u32[]{:S(2)}) copy-start(bf16[512,896]{0,1:T(8,128)(2,1)} %copy.15) | copy-start | bytes 2752516
  37.8 38.7 %copy-start.5 = (bf16[512,896]{0,1:T(8,128)(2,1)S(1)}, bf16[512,896]{0,1:T(8,128)(2,1)}, u32[]{:S(2)}) copy-start(bf16[512,896]{0,1:T(8,128)(2,1)} %copy.14) | copy-start | bytes 2752516
  83.7 4.4 %copy-start.2 = (bf16[896,4096]{0,1:T(8,128)(2,1)}, bf16[896,4096]{0,1:T(8,128)(2,1)S(1)}, u32[]{:S(2)}) copy-start(bf16[896,4096]{0,1:T(8,128)(2,1)S(1)} %convolution_convert_fusion) | copy-start | bytes 22020100
  88.0 7.2 %collective-permute-start.1 = (bf16[2,4,256,896]{3,2,1,0:T(8,128)(2,1)}, bf16[2,4,256,896]{3,2,1,0:T(8,128)(2,1)}, u32[]{:S(2)}, u32[]{:S(2)}) collective-permute-start(bf16[2,4,256,896]{3,2,1,0:T(8,128)(2,1)} %fusion), channel_id=1, source_target_pairs={{0,16},{16,0},{1,17},{17,1},{2,18},{18,2},{3,19},{19,3},{4,20},{20... | collective-permute-start | bytes 11010056 | tf_op jit(solution)/shard_map/ppermute | solution.py:19
  99.5 3.0 %copy-start = (f32[2,4,256,896]{3,2,1,0:T(8,128)}, f32[2,4,256,896]{3,2,1,0:T(8,128)S(1)}, u32[]{:S(2)}) copy-start(f32[2,4,256,896]{3,2,1,0:T(8,128)S(1)} %convert_add_fusion) | copy-start | bytes 22020100
  102.7 41.5 %collective-permute-start.2 = (bf16[4,256,896]{2,1,0:T(8,128)(2,1)S(1)}, bf16[4,256,896]{2,1,0:T(8,128)(2,1)}, u32[]{:S(2)}, u32[]{:S(2)}) collective-permute-start(bf16[4,256,896]{2,1,0:T(8,128)(2,1)S(1)} %fusion.13), channel_id=1, source_target_pairs={{0,128},{128,0},{1,129},{129,1},{2,130},{130,2},{3,131},{131,3},{4... | collective-permute-start | bytes 5505032 | tf_op jit(solution)/shard_map/ppermute | solution.py:19
  134.0 18.0 %copy-start.7 = (bf16[64,4096]{1,0:T(8,128)(2,1)S(1)}, bf16[64,4096]{1,0:T(8,128)(2,1)}, u32[]{:S(2)}) copy-start(bf16[64,4096]{1,0:T(8,128)(2,1)} %reduce-scatter.2.cloned.1.call-done) | copy-start | bytes 1572868
  134.0 18.0 %collective-permute-start = (bf16[32,4096]{1,0:T(8,128)(2,1)S(1)}, bf16[32,4096]{1,0:T(8,128)(2,1)S(1)}, u32[]{:S(2)}, u32[]{:S(2)}) collective-permute-start(bf16[32,4096]{1,0:T(8,128)(2,1)S(1)} %constant_dynamic-slice_fusion), channel_id=1, source_target_pairs={{0,1},{1,0},{2,3},{3,2},{4,5},{5,4},{6,7},{7,6},{8,9},{9,8},{10,11... | collective-permute-start | bytes 786440 | tf_op jit(solution)/shard_map/ppermute | solution.py:19
  147.6 11.0 %collective-permute-start.5 = (bf16[256,896]{1,0:T(8,128)(2,1)S(1)}, bf16[256,896]{1,0:T(8,128)(2,1)S(1)}, u32[]{:S(2)}, u32[]{:S(2)}) collective-permute-start(bf16[256,896]{1,0:T(8,128)(2,1)S(1)} %get-tuple-element.74), channel_id=1, source_target_pairs={{0,96},{32,0},{64,32},{96,64},{1,97},{33,1},{65,33},{97,65},{2,98}... | collective-permute-start | bytes 1376264 | tf_op jit(solution)/shard_map/ppermute | solution.py:19
  150.1 11.3 %collective-permute-start.4 = (bf16[256,896]{1,0:T(8,128)(2,1)S(1)}, bf16[256,896]{1,0:T(8,128)(2,1)S(1)}, u32[]{:S(2)}, u32[]{:S(2)}) collective-permute-start(bf16[256,896]{1,0:T(8,128)(2,1)S(1)} %get-tuple-element.75), channel_id=1, source_target_pairs={{0,64},{32,96},{64,0},{96,32},{1,65},{33,97},{65,1},{97,33},{2,66}... | collective-permute-start | bytes 1376264 | tf_op jit(solution)/shard_map/ppermute | solution.py:19
  150.7 23.2 %collective-permute-start.3 = (bf16[256,896]{1,0:T(8,128)(2,1)S(1)}, bf16[256,896]{1,0:T(8,128)(2,1)S(1)}, u32[]{:S(2)}, u32[]{:S(2)}) collective-permute-start(bf16[256,896]{1,0:T(8,128)(2,1)S(1)} %get-tuple-element.73), channel_id=1, source_target_pairs={{0,32},{32,64},{64,96},{96,0},{1,33},{33,65},{65,97},{97,1},{2,34}... | collective-permute-start | bytes 1376264 | tf_op jit(solution)/shard_map/ppermute | solution.py:19
Sparse Core Ops, SparseCore 0:
  19.5 56.9 all-gather.1
  79.0 54.0 reduce-scatter.1
